TPU v7x, 256 devices: a whole 4x4x8 slice. The times are simulated.
256 devices in a mesh: req: 32 (over x, y, core), tp: 8 (over z).
Axes of the slice: x: 4, y: 4, z: 8, core: 2. Of those that a mesh axis runs over, the one named last changes fastest.
Arguments:
- query: bfloat16 [768, 4096], P('req', 'tp'), may hold values from -102 to 102
- new_key: bfloat16 [768, 1024], P('req', 'tp'), may hold values from -6 to 6
- new_value: bfloat16 [768, 1024], P('req', 'tp'), may hold values from -6 to 6
- prefix_key: bfloat16 [64, 6144, 1024], P('req', None, 'tp'), may hold values from -6 to 6
- prefix_value: bfloat16 [64, 6144, 1024], P('req', None, 'tp'), may hold values from -6 to 6
- suffix_key: bfloat16 [768, 128, 1024], P('req', None, 'tp'), may hold values from -6 to 6
- suffix_value: bfloat16 [768, 128, 1024], P('req', None, 'tp'), may hold values from -6 to 6
- group_ids: int32 [768], replicated, may hold values from 0 to 63, as said below
- prompt_len: int32 [64], P('req'), may hold values from 768 to 6144, as said below
- suffix_len: int32 [768], replicated, may hold values from 1 to 128, as said below
- o_weight: bfloat16 [4096, 4096], P('tp'), may hold values from -0.09375 to 0.09375
- residual: bfloat16 [768, 4096], P('req'), may hold values from -0.29882812 to 0.29882812
- norm_gain: bfloat16 [4096], replicated, may hold values from 0.5 to 1.5
Outputs:
- hidden: bfloat16 [768, 4096], P('req')
- normed: bfloat16 [768, 4096], P('req')
Inputs may be any that keep to these rules, and one draw needn't show every extreme that they name: Request r belongs to group group_ids[r]; groups 2k to 2k + 1 at a time are held together (group // 2 names the holder). Among each aligned block of 24 requests, every holder that appears is named by exactly 2 of them. `prompt_len`: some group has exactly 6144. `suffix_len`: some request has exactly 128.
All inputs are finite; a program needn't handle non-finite values.
Results may differ from a plain program's by a relative error of at most 0.008.
Values may be sent and summed in bfloat16 or wider, within the bound.
No kernel may reach another device: no remote copies, remote signals or barrier semaphores. Data moves between devices by JAX's collectives and lax.ppermute only.
A program may use at most 64 MiB of HBM per device.

v0:
```python
import math

import jax
import jax.numpy as jnp
from jax import lax
from jax.sharding import PartitionSpec as P

HD = 128
WIN = 4096
SINKS = 4


FAR_BELOW = -1e30
NORM_EPS = 1e-06


def prefix_attend(
    rows_query, row_group, row_suffix, prefix_key, prefix_value, prompt_len, first_group, blocks
):
    row_count = rows_query.shape[0]
    groups_dev = prefix_key.shape[0]
    prompt_max = prefix_key.shape[1]
    kv_dev = prefix_key.shape[2] // HD
    heads_dev = rows_query.shape[1] // HD
    repeat = heads_dev // kv_dev
    block_len = min(512, prompt_max)
    score_scale = 1.0 / math.sqrt(HD)
    local_group = row_group - first_group
    owned = (local_group >= 0) & (local_group < groups_dev)
    member = local_group[:, None] == jnp.arange(groups_dev, dtype=jnp.int32)[None, :]
    row_prompt = jnp.sum(jnp.where(member, prompt_len[None, :], 0), axis=1)
    row_low = row_prompt + row_suffix - WIN + 1
    queries = rows_query.reshape(row_count, kv_dev, repeat, HD)

    def key_step(block_index, loop_state):
        running, weight_sum, weighted = loop_state
        key_start = block_index * block_len
        key_block = lax.dynamic_slice_in_dim(prefix_key, key_start, block_len, 1).reshape(
            groups_dev, block_len, kv_dev, HD
        )
        value_block = lax.dynamic_slice_in_dim(prefix_value, key_start, block_len, 1).reshape(
            groups_dev, block_len, kv_dev, HD
        )
        scores = (
            jnp.einsum("rkhd,gpkd->rkhgp", queries, key_block, preferred_element_type=jnp.float32)
            * score_scale
        )
        positions = key_start + jnp.arange(block_len, dtype=jnp.int32)
        inside = positions[None, :] < prompt_len[:, None]
        window = (positions[None, :] < SINKS) | (positions[None, :] >= row_low[:, None])
        usable = member[:, :, None] & inside[None, :, :] & window[:, None, :]
        usable = usable[:, None, None, :, :]
        masked = jnp.where(usable, scores, FAR_BELOW)
        updated = jnp.maximum(running, jnp.max(masked, axis=(3, 4)))
        weights = jnp.where(usable, jnp.exp(masked - updated[..., None, None]), 0.0)
        rescale = jnp.exp(running - updated)
        weight_sum = weight_sum * rescale + jnp.sum(weights, axis=(3, 4))
        rounded = weights.astype(jnp.bfloat16)
        weighted = weighted * rescale[..., None] + jnp.einsum(
            "rkhgp,gpkd->rkhd", rounded, value_block, preferred_element_type=jnp.float32
        )
        return (updated, weight_sum, weighted)

    initial = (
        jnp.full((row_count, kv_dev, repeat), FAR_BELOW, jnp.float32),
        jnp.zeros((row_count, kv_dev, repeat), jnp.float32),
        jnp.zeros((row_count, kv_dev, repeat, HD), jnp.float32),
    )
    running, weight_sum, weighted = lax.fori_loop(0, blocks, key_step, initial)
    bounded = jnp.maximum(weight_sum, 1.0)
    normalized = jnp.where(owned[:, None, None, None], weighted / bounded[..., None], 0.0).reshape(
        row_count, heads_dev * HD
    )
    log_total = jnp.where(owned[:, None, None], running + jnp.log(bounded), 0.0).reshape(
        row_count, heads_dev
    )
    return (normalized, log_total)


def body(
    query,
    new_key,
    new_value,
    prefix_key,
    prefix_value,
    suffix_key,
    suffix_value,
    group_ids,
    prompt_len,
    suffix_len,
    o_weight,
    residual,
    norm_gain,
):
    req_dev = query.shape[0]
    heads_dev = query.shape[1] // HD
    kv_dev = new_key.shape[1] // HD
    repeat = heads_dev // kv_dev
    groups_dev = prefix_key.shape[0]
    prompt_max = prefix_key.shape[1]
    suffix_max = suffix_key.shape[1]
    block_len = min(512, prompt_max)
    score_scale = 1.0 / math.sqrt(HD)
    places = lax.axis_size("req")
    device = lax.axis_index("req")
    first_group = device * groups_dev
    own_suffix = lax.dynamic_slice_in_dim(suffix_len, device * req_dev, req_dev)
    blocks = prompt_max // block_len
    capacity = max(2, req_dev // places)
    slot_total = places * capacity
    all_groups = group_ids.reshape(places, 1, req_dev)
    all_suffix = suffix_len.reshape(places, 1, req_dev)
    all_rows = (
        jnp.arange(places, dtype=jnp.int32)[:, None] * req_dev
        + jnp.arange(req_dev, dtype=jnp.int32)[None, :]
    ).reshape(places, 1, req_dev)
    is_mine = (group_ids // groups_dev).reshape(places, req_dev) == device
    slot_order = jnp.cumsum(is_mine.astype(jnp.int32), axis=1) - 1
    slot_pick = is_mine[:, None, :] & (
        slot_order[:, None, :] == jnp.arange(capacity, dtype=jnp.int32)[None, :, None]
    )
    filled = jnp.any(slot_pick, axis=2)
    slot_group = jnp.where(
        filled, jnp.sum(jnp.where(slot_pick, all_groups, 0), axis=2), -1
    ).reshape(slot_total)
    slot_suffix = jnp.sum(jnp.where(slot_pick, all_suffix, 0), axis=2).reshape(slot_total)
    slot_row = jnp.where(filled, jnp.sum(jnp.where(slot_pick, all_rows, 0), axis=2), -1).reshape(
        slot_total
    )
    every_query = lax.all_gather(query, "req", axis=0, tiled=True)
    pick_rows = slot_row[:, None] == jnp.arange(places * req_dev, dtype=jnp.int32)[None, :]
    compact = jnp.dot(
        pick_rows.astype(jnp.bfloat16), every_query, preferred_element_type=jnp.float32
    ).astype(jnp.bfloat16)
    part_out, part_log = prefix_attend(
        compact, slot_group, slot_suffix, prefix_key, prefix_value, prompt_len, first_group, blocks
    )
    spread_rows = pick_rows.T.astype(jnp.float32)
    spread_out = jnp.dot(spread_rows, part_out, precision=lax.Precision.HIGHEST)
    spread_log = jnp.dot(spread_rows, part_log, precision=lax.Precision.HIGHEST)
    prefix_out, prefix_log = (
        lax.psum_scatter(spread_out, "req", scatter_dimension=0, tiled=True),
        lax.psum_scatter(spread_log, "req", scatter_dimension=0, tiled=True),
    )
    queries = query.reshape(req_dev, kv_dev, repeat, HD)
    key_rows = suffix_key.reshape(req_dev, suffix_max, kv_dev, HD)
    value_rows = suffix_value.reshape(req_dev, suffix_max, kv_dev, HD)
    scores = (
        jnp.einsum("rkhd,rjkd->rkhj", queries, key_rows, preferred_element_type=jnp.float32)
        * score_scale
    )
    own_score = (
        jnp.einsum(
            "rkhd,rkd->rkh",
            queries,
            new_key.reshape(req_dev, kv_dev, HD),
            preferred_element_type=jnp.float32,
        )
        * score_scale
    )
    usable = (jnp.arange(suffix_max, dtype=jnp.int32)[None, :] < own_suffix[:, None])[
        :, None, None, :
    ]
    masked = jnp.where(usable, scores, FAR_BELOW)
    running = jnp.maximum(jnp.max(masked, axis=-1), own_score)
    weights = jnp.where(usable, jnp.exp(masked - running[..., None]), 0.0)
    own_weight = jnp.exp(own_score - running)
    weight_sum = jnp.sum(weights, axis=-1) + own_weight
    weighted = jnp.einsum(
        "rkhj,rjkd->rkhd",
        weights.astype(jnp.bfloat16),
        value_rows,
        preferred_element_type=jnp.float32,
    )
    own_rounded = own_weight.astype(jnp.bfloat16).astype(jnp.float32)
    weighted = weighted + own_rounded[..., None] * new_value.reshape(req_dev, kv_dev, 1, HD).astype(
        jnp.float32
    )
    local_out = weighted / weight_sum[..., None]
    local_log = running + jnp.log(weight_sum)
    prefix_out = prefix_out.reshape(req_dev, kv_dev, repeat, HD)
    prefix_log = prefix_log.reshape(req_dev, kv_dev, repeat)
    combined = jnp.logaddexp(prefix_log, local_log)
    attended = (
        prefix_out * jnp.exp(prefix_log - combined)[..., None]
        + local_out * jnp.exp(local_log - combined)[..., None]
    )
    attended = attended.reshape(req_dev, heads_dev * HD).astype(jnp.bfloat16)
    partial_value = jnp.dot(attended, o_weight, preferred_element_type=jnp.float32)
    proj = lax.psum(partial_value, "tp")
    summed = residual.astype(jnp.float32) + proj
    hidden = summed.astype(jnp.bfloat16)
    inverse = lax.rsqrt(jnp.mean(summed * summed, axis=-1, keepdims=True) + NORM_EPS)
    normed = (summed * inverse * norm_gain.astype(jnp.float32)[None, :]).astype(jnp.bfloat16)
    return (hidden, normed)


def solution(mesh):
    placed = (
        P("req", "tp"),
        P("req", "tp"),
        P("req", "tp"),
        P("req", None, "tp"),
        P("req", None, "tp"),
        P("req", None, "tp"),
        P("req", None, "tp"),
        P(),
        P("req"),
        P(),
        P("tp", None),
        P("req", None),
        P(),
    )
    return jax.shard_map(
        body,
        mesh=mesh,
        in_specs=placed,
        out_specs=(P("req", None), P("req", None)),
        check_vma=False,
    )
```

profile of v0, /device:TPU:2, one launch (start us, length us, event | category | flops | bytes accessed | tf_op | source)
XLA Modules:
  0.0 305.6 jit_solution(10688126659396240701)
XLA Ops:
  7.3 0.8 fusion.51
  8.2 0.8 broadcast_in_dim.180
  9.3 0.8 broadcast_in_dim.188
  10.5 0.7 fusion.59
  11.4 24.9 %all_gather.3 = bf16[768,512]{1,0:T(8,128)(2,1)S(1)} all-gather(bf16[24,512]{1,0:T(8,128)(2,1)} %param.15), channel_id=1, replica_groups=mesh['req'=32,'tp'=8] {'req'}, dimensions={0}, use_global_device_ids=true | all-gather | bytes 811008 | tf_op jit(solution)/shard_map/all_gather | solution.py:130
  36.8 50.0 %while.18 = (s32[]{:T(128)}, f32[64,1,4]{0,2,1:T(4,128)S(1)}, f32[64,1,4]{0,2,1:T(4,128)S(1)}, f32[64,1,4,128]{3,0,2,1:T(8,128)S(1)}, s32[2]{0:T(128)}, /*index=...) while((s32[]{:T(128)}, f32[64,1,4]{0,2,1:T(4,128)S(1)}, ...), condition=%wide.region_9.10_spmd.clone, body=%wide.region_6.9_spmd.clone.sunk | while | flops 136876160 | bytes 4351967 | solution.py:69
  37.0 0.7 broadcast_compare_fusion.5
  37.8 1.4 fusion.83
  39.6 1.4 fusion.86
  41.2 0.7 broadcast_compare_fusion.5
  42.0 1.4 fusion.83
  43.8 1.4 fusion.86
  45.3 0.7 broadcast_compare_fusion.5
  46.2 1.4 fusion.83
  47.9 1.4 fusion.86
  49.5 0.7 broadcast_compare_fusion.5
  50.3 1.4 fusion.83
  52.1 1.4 fusion.86
  53.7 0.7 broadcast_compare_fusion.5
  54.5 1.4 fusion.83
  56.3 1.4 fusion.86
  57.8 0.7 broadcast_compare_fusion.5
  58.7 1.4 fusion.83
  60.5 1.4 fusion.86
  62.0 0.7 broadcast_compare_fusion.5
  62.9 1.4 fusion.83
  64.6 1.4 fusion.86
  66.2 0.7 broadcast_compare_fusion.5
  67.0 1.4 fusion.83
  68.8 1.4 fusion.86
  70.3 0.7 broadcast_compare_fusion.5
  71.2 1.4 fusion.83
  73.0 1.4 fusion.86
  75.4 1.4 fusion.83
  77.1 1.4 fusion.86
  78.7 0.7 broadcast_compare_fusion.5
  79.5 1.4 fusion.83
  81.3 1.4 fusion.86
  83.7 1.4 fusion.83
  85.5 1.4 fusion.86
  87.2 2.0 fusion.27
  89.3 0.8 dynamic_slice.17
  91.6 109.0 %all-reduce = f32[768,4]{0,1:T(4,128)S(1)} all-reduce(f32[768,4]{0,1:T(4,128)S(1)} %fusion.26), channel_id=3, replica_groups=mesh['req'=32,'tp'=8] {'req'}, use_global_device_ids=true, to_apply=%region_11.12.clone | all-reduce | flops 3072 | bytes 24576
  201.9 0.8 reshape.377
  203.2 3.6 %fusion.37 = f32[24,4096]{1,0:T(8,128)} fusion(bf16[512,4096]{1,0:T(8,128)(2,1)} %param.25, bf16[3,8,4,128]{3,2,1,0:T(4,128)(2,1)S(1)} %bitcast.93), kind=kOutput, calls=%fused_computation.57 | convolution fusion | flops 100663296 | bytes 4612096 | tf_op jit(solution)/shard_map/dot_general | solution.py:189
  206.8 88.9 %all-reduce.3.cloned.1.call-done = f32[24,4096]{1,0:T(8,128)} async-done(((f32[24,4096]{1,0:T(8,128)}), f32[24,4096]{1,0:T(8,128)}) %all-reduce.3.cloned.1.call-update) | async-done | bytes 393232 | tf_op jit(solution)/shard_map/psum | solution.py:190
  295.8 1.2 multiply_reduce_fusion
  297.0 1.8 multiply_convert_fusion
  (177 shorter events, 13.2 us)
Async XLA Ops:
  7.2 193.8 %copy-start = (bf16[24,128,128]{2,1,0:T(8,128)(2,1)S(1)}, bf16[24,128,128]{2,1,0:T(8,128)(2,1)}, u32[]{:S(2)}) copy-start(bf16[24,128,128]{2,1,0:T(8,128)(2,1)} %param.20) | copy-start | bytes 2359300
  7.2 194.8 %reduce-scatter.3.cloned.1.call-start = ((), (), s32[]{:S(2)}) async-start(), calls=%async_computation.1 | async-start | bytes 1622016 | tf_op jit(solution)/shard_map/reduce_scatter | solution.py:142
  86.9 2.4 copy-start.2
  86.9 3.2 %copy-start.7 = (u32[256]{0:T(256)S(1)}, u32[256]{0:T(256)}, u32[]{:S(2)}) copy-start(u32[256]{0:T(256)} %constant.130) | copy-start | bytes 3076
  86.9 113.9 %copy-start.4 = (bf16[24,128]{1,0:T(8,128)(2,1)S(1)}, bf16[24,128]{1,0:T(8,128)(2,1)}, u32[]{:S(2)}) copy-start(bf16[24,128]{1,0:T(8,128)(2,1)} %param.17) | copy-start | bytes 18436
  86.9 113.9 %copy-start.6 = (bf16[24,128]{1,0:T(8,128)(2,1)S(1)}, bf16[24,128]{1,0:T(8,128)(2,1)}, u32[]{:S(2)}) copy-start(bf16[24,128]{1,0:T(8,128)(2,1)} %param.16) | copy-start | bytes 18436
  86.9 115.8 %copy-start.5 = (bf16[24,128,128]{2,1,0:T(8,128)(2,1)S(1)}, bf16[24,128,128]{2,1,0:T(8,128)(2,1)}, u32[]{:S(2)}) copy-start(bf16[24,128,128]{2,1,0:T(8,128)(2,1)} %param.21) | copy-start | bytes 2359300
  89.2 206.5 %all-reduce.3.cloned.1.call-start = ((), (), s32[]{:S(2)}) async-start(), calls=%async_computation.2 | async-start | bytes 786432 | tf_op jit(solution)/shard_map/psum | solution.py:190
  202.8 4.0 %copy-start.3 = (bf16[4096]{0:T(1024)(128)(2,1)S(1)}, bf16[4096]{0:T(1024)(128)(2,1)}, u32[]{:S(2)}) copy-start(bf16[4096]{0:T(1024)(128)(2,1)} %param.27) | copy-start | bytes 24580
  202.8 93.0 %copy-start.1 = (bf16[24,4096]{1,0:T(8,128)(2,1)S(1)}, bf16[24,4096]{1,0:T(8,128)(2,1)}, u32[]{:S(2)}) copy-start(bf16[24,4096]{1,0:T(8,128)(2,1)} %param.26) | copy-start | bytes 589828
Sparse Core Ops, SparseCore 0:
  89.4 86.8 reduce-scatter.2
  206.9 88.8 all-reduce.2
where the time goes:
time: 307 us; the launch traced here: 306 us
  blocking collectives  134 us (44%)
  waiting for transfers between devices  89 us (29%)
  matrix products  40.4 us (13%)
  other arithmetic  21.3 us (7%)
  between operations  15 us (5%)
  local copies, waits for them, and re-layouts  5.04 us (2%)
    unnamed x1, blocking collectives  109 us
    psum x1, waiting for transfers between devices, body(): proj = lax.psum(partial_value, 'tp')  88.9 us
    all_gather x1, blocking collectives, body(): every_query = lax.all_gather(query, 'req', axis=0, tiled=True)  24.9 us
    dot_general x12, matrix products, key_step(): jnp.einsum('rkhgp,gpkd->rkhd', rounded, value_block, preferred_element_ty...  16.8 us
    dot_general x12, matrix products, key_step(): jnp.einsum('rkhd,gpkd->rkhgp', queries, key_block, preferred_element_type...  16.3 us
    lt x12, other arithmetic, key_step(): inside = positions[None, :] < prompt_len[:, None]  8.77 us
  transfers between devices with their start and end apart: 2, of which 1 were waited for; matrix products, arithmetic and copies ran while one was open for 1% of the time, Pallas kernels for 0%

commit v1 on v0

--- a/solution.py
+++ b/solution.py
@@ -127,21 +127,29 @@
     slot_row = jnp.where(filled, jnp.sum(jnp.where(slot_pick, all_rows, 0), axis=2), -1).reshape(
         slot_total
     )
-    every_query = lax.all_gather(query, "req", axis=0, tiled=True)
-    pick_rows = slot_row[:, None] == jnp.arange(places * req_dev, dtype=jnp.int32)[None, :]
-    compact = jnp.dot(
-        pick_rows.astype(jnp.bfloat16), every_query, preferred_element_type=jnp.float32
+    own_groups = lax.dynamic_slice_in_dim(group_ids, device * req_dev, req_dev)
+    own_holder = own_groups // groups_dev
+    same_holder = own_holder[:, None] == own_holder[None, :]
+    earlier = jnp.arange(req_dev, dtype=jnp.int32)[None, :] < jnp.arange(req_dev, dtype=jnp.int32)[:, None]
+    own_rank = jnp.sum(same_holder & earlier, axis=1).astype(jnp.int32)
+    own_slot = own_holder * capacity + own_rank
+    send_pick = own_slot[None, :] == jnp.arange(slot_total, dtype=jnp.int32)[:, None]
+    send_query = jnp.dot(
+        send_pick.astype(jnp.bfloat16), query, preferred_element_type=jnp.float32
     ).astype(jnp.bfloat16)
+    compact = lax.all_to_all(
+        send_query.reshape(places, capacity, heads_dev * HD), "req", 0, 0, tiled=True
+    ).reshape(slot_total, heads_dev * HD)
     part_out, part_log = prefix_attend(
         compact, slot_group, slot_suffix, prefix_key, prefix_value, prompt_len, first_group, blocks
     )
-    spread_rows = pick_rows.T.astype(jnp.float32)
-    spread_out = jnp.dot(spread_rows, part_out, precision=lax.Precision.HIGHEST)
-    spread_log = jnp.dot(spread_rows, part_log, precision=lax.Precision.HIGHEST)
-    prefix_out, prefix_log = (
-        lax.psum_scatter(spread_out, "req", scatter_dimension=0, tiled=True),
-        lax.psum_scatter(spread_log, "req", scatter_dimension=0, tiled=True),
-    )
+    packed = jnp.concatenate([part_out, part_log], axis=1)
+    returned = lax.all_to_all(
+        packed.reshape(places, capacity, packed.shape[1]), "req", 0, 0, tiled=True
+    ).reshape(slot_total, packed.shape[1])
+    picked = returned[own_slot]
+    prefix_out = picked[:, : heads_dev * HD]
+    prefix_log = picked[:, heads_dev * HD :]
     queries = query.reshape(req_dev, kv_dev, repeat, HD)
     key_rows = suffix_key.reshape(req_dev, suffix_max, kv_dev, HD)
     value_rows = suffix_value.reshape(req_dev, suffix_max, kv_dev, HD)

time: 307 us -> 181 us (0.59)
  blocking collectives: 134 us -> 0 us
  starting transfers between devices: 0.08 us -> 15 us
  waiting for transfers between devices: 89 us -> 80.3 us
    unnamed x1 -> x0, blocking collectives: 109 us -> none
    all_gather x1 -> x0, blocking collectives: 24.9 us -> none  [body(): every_query = lax.all_gather(query, 'req', axis=0, tiled=True)]
    psum x1, waiting for transfers between devices: 88.9 us -> 73.7 us  [body(): proj = lax.psum(partial_value, 'tp')]
    all_to_all x0 -> x2, starting transfers between devices: none -> 15 us  [the longest x1 7.62 us: body(): lax.all_to_all(send_query.reshape(places, capacity, heads_dev * HD), 'req...]
    all_to_all x0 -> x2, waiting for transfers between devices: none -> 6.6 us  [the longest x1 6.6 us: body(): lax.all_to_all(packed.reshape(places, capacity, packed.shape[1]), 'req',...]
  transfers between devices with their start and end apart: 2 -> 3, of which waited for: 1 -> 2; matrix products, arithmetic and copies ran while one was open for 1% -> 4% of each run, Pallas kernels for 0% -> 0%
where the time goes in v1:
time: 181 us; the launch traced here: 179 us
  waiting for transfers between devices  80.3 us (44%)
  matrix products  39.3 us (22%)
  other arithmetic  23.8 us (13%)
  starting transfers between devices  15 us (8%)
  between operations  14.3 us (8%)
  local copies, waits for them, and re-layouts  5.63 us (3%)
    psum x1, waiting for transfers between devices, body(): proj = lax.psum(partial_value, 'tp')  73.7 us
    dot_general x12, matrix products, key_step(): jnp.einsum('rkhgp,gpkd->rkhd', rounded, value_block, preferred_element_ty...  16.7 us
    dot_general x12, matrix products, key_step(): jnp.einsum('rkhd,gpkd->rkhgp', queries, key_block, preferred_element_type...  16.3 us
    lt x12, other arithmetic, key_step(): inside = positions[None, :] < prompt_len[:, None]  8.84 us
    all_to_all x1, starting transfers between devices, body(): lax.all_to_all(send_query.reshape(places, capacity, heads_dev * HD), 'req...  7.62 us
    all_to_all x1, starting transfers between devices, body(): lax.all_to_all(packed.reshape(places, capacity, packed.shape[1]), 'req',...  7.38 us
    all_to_all x1, waiting for transfers between devices, body(): lax.all_to_all(packed.reshape(places, capacity, packed.shape[1]), 'req',...  6.6 us
    reduce_sum x12, other arithmetic, key_step(): weight_sum = weight_sum * rescale + jnp.sum(weights, axis=(3, 4))  4.33 us
  transfers between devices with their start and end apart: 3, of which 2 were waited for; matrix products, arithmetic and copies ran while one was open for 4% of the time, Pallas kernels for 0%

profile of v1, /device:TPU:2, one launch (start us, length us, event | category | flops | bytes accessed | tf_op | source)
XLA Modules:
  0.0 179.4 jit_solution(5152903580054257857)
XLA Ops:
  7.2 0.8 and_select_fusion
  8.2 0.8 compare_select_fusion
  9.0 0.9 convolution_convert_fusion
  10.5 7.6 %all-to-all-start = ((bf16[32,2,512]{2,1,0:T(2,128)(2,1)}), bf16[32,2,512]{2,1,0:T(2,128)(2,1)S(1)}, u32[]{:S(2)}, u32[]{:S(2)}) async-start(bf16[32,2,512]{2,1,0:T(2,128)(2,1)} %reshape.348), calls=%async_computation | async-start | bytes 131072 | tf_op jit(solution)/shard_map/all_to_all | solution.py:140
  19.1 0.8 broadcast_in_dim.176
  19.8 0.8 broadcast_in_dim.186
  20.6 0.8 dynamic_slice.21
  21.4 0.7 reshape.351
  23.1 0.7 fusion.49
  23.8 0.8 fusion.43
  25.4 50.1 %while.18 = (s32[]{:T(128)}, f32[64,1,4]{0,2,1:T(4,128)S(1)}, f32[64,1,4]{0,2,1:T(4,128)S(1)}, f32[64,1,4,128]{3,0,2,1:T(8,128)S(1)}, s32[2]{0:T(128)}, /*index=...) while((s32[]{:T(128)}, f32[64,1,4]{0,2,1:T(4,128)S(1)}, ...), condition=%wide.region_9.10_spmd.clone, body=%wide.region_6.9_spmd.clone.sunk | while | flops 136876160 | bytes 4351959 | solution.py:69
  25.6 0.8 broadcast_compare_fusion.5
  26.5 1.4 fusion.68
  27.9 1.4 fusion.71
  29.8 0.7 broadcast_compare_fusion.5
  30.7 1.4 fusion.68
  32.1 1.4 fusion.71
  34.0 0.7 broadcast_compare_fusion.5
  34.8 1.4 fusion.68
  36.2 1.4 fusion.71
  38.2 0.7 broadcast_compare_fusion.5
  39.0 1.4 fusion.68
  40.4 1.4 fusion.71
  43.2 1.4 fusion.68
  44.6 1.4 fusion.71
  47.4 1.4 fusion.68
  48.7 1.4 fusion.71
  51.5 1.4 fusion.68
  52.9 1.4 fusion.71
  55.7 1.4 fusion.68
  57.1 1.4 fusion.71
  59.9 1.4 fusion.68
  61.2 1.4 fusion.71
  64.0 1.4 fusion.68
  65.4 1.4 fusion.71
  67.3 0.7 broadcast_compare_fusion.5
  68.2 1.4 fusion.68
  69.6 1.4 fusion.71
  71.5 0.7 broadcast_compare_fusion.5
  72.4 1.4 fusion.68
  73.7 1.4 fusion.71
  76.0 0.7 pad_maximum_fusion
  76.7 7.4 %all-to-all-start.1 = ((f32[32,2,516]{2,1,0:T(2,128)}), f32[32,2,516]{2,1,0:T(2,128)S(1)}, u32[]{:S(2)}, u32[]{:S(2)}) async-start(f32[32,2,516]{2,1,0:T(2,128)} %pad_maximum_fusion), calls=%async_computation.1 | async-start | bytes 327680 | tf_op jit(solution)/shard_map/all_to_all | solution.py:147
  84.4 6.6 %all-to-all-done.1 = f32[32,2,516]{2,1,0:T(2,128)S(1)} async-done(((f32[32,2,516]{2,1,0:T(2,128)}), f32[32,2,516]{2,1,0:T(2,128)S(1)}, u32[]{:S(2)}, u32[]{:S(2)}) %all-to-all-start.1) | async-done | bytes 132128 | tf_op jit(solution)/shard_map/all_to_all | solution.py:147
  92.2 3.6 %fusion.30 = f32[24,4096]{1,0:T(8,128)} fusion(bf16[512,4096]{1,0:T(8,128)(2,1)} %param.25, bf16[3,8,4,128]{3,2,1,0:T(4,128)(2,1)S(1)} %bitcast.84), kind=kOutput, calls=%fused_computation.52 | convolution fusion | flops 100663296 | bytes 4612096 | tf_op jit(solution)/shard_map/dot_general | solution.py:197
  95.9 73.7 %all-reduce.2.cloned.1.call-done = f32[24,4096]{1,0:T(8,128)} async-done(((f32[24,4096]{1,0:T(8,128)}), f32[24,4096]{1,0:T(8,128)}) %all-reduce.2.cloned.1.call-update) | async-done | bytes 393232 | tf_op jit(solution)/shard_map/psum | solution.py:198
  169.6 1.2 multiply_reduce_fusion
  170.7 1.8 %multiply_convert_fusion = (bf16[24,4096]{1,0:T(8,128)(2,1)}, bf16[24,4096]{1,0:T(8,128)(2,1)}) fusion(f32[4096]{0:T(1024)S(1)} %convert_element_type.66, f32[24]{0:T(128)S(1)} %add_rsqrt_fusion, f32[24,4096]{1,0:T(8,128)} %all-reduce.2.cloned.1.call-done, bf16[24,4096]{1,0:T(8,128)(2,1)S(1)} %copy-done.1), kind=kLoop, calls=%fused_computation.42 | loop fusion | flops 589824 | bytes 999520 | tf_op jit(solution)/shard_map/convert_element_type | solution.py:202
  (172 shorter events, 16.9 us)
Async XLA Ops:
  7.2 17.5 %copy-start = (bf16[24,128,128]{2,1,0:T(8,128)(2,1)S(1)}, bf16[24,128,128]{2,1,0:T(8,128)(2,1)}, u32[]{:S(2)}) copy-start(bf16[24,128,128]{2,1,0:T(8,128)(2,1)} %param.20) | copy-start | bytes 2359300
  10.5 14.8 %all-to-all-start = ((bf16[32,2,512]{2,1,0:T(2,128)(2,1)}), bf16[32,2,512]{2,1,0:T(2,128)(2,1)S(1)}, u32[]{:S(2)}, u32[]{:S(2)}) async-start(bf16[32,2,512]{2,1,0:T(2,128)(2,1)} %reshape.348), calls=%async_computation | async-start | bytes 131072 | tf_op jit(solution)/shard_map/all_to_all | solution.py:140
  25.4 58.8 %copy-start.3 = (bf16[24,128]{1,0:T(8,128)(2,1)S(1)}, bf16[24,128]{1,0:T(8,128)(2,1)}, u32[]{:S(2)}) copy-start(bf16[24,128]{1,0:T(8,128)(2,1)} %param.17) | copy-start | bytes 18436
  25.4 66.4 %copy-start.4 = (bf16[24,128,128]{2,1,0:T(8,128)(2,1)S(1)}, bf16[24,128,128]{2,1,0:T(8,128)(2,1)}, u32[]{:S(2)}) copy-start(bf16[24,128,128]{2,1,0:T(8,128)(2,1)} %param.21) | copy-start | bytes 2359300
  76.7 14.3 %all-to-all-start.1 = ((f32[32,2,516]{2,1,0:T(2,128)}), f32[32,2,516]{2,1,0:T(2,128)S(1)}, u32[]{:S(2)}, u32[]{:S(2)}) async-start(f32[32,2,516]{2,1,0:T(2,128)} %pad_maximum_fusion), calls=%async_computation.1 | async-start | bytes 327680 | tf_op jit(solution)/shard_map/all_to_all | solution.py:147
  84.1 85.5 %all-reduce.2.cloned.1.call-start = ((), (), s32[]{:S(2)}) async-start(), calls=%async_computation.2 | async-start | bytes 786432 | tf_op jit(solution)/shard_map/psum | solution.py:198
  91.8 4.0 %copy-start.2 = (bf16[4096]{0:T(1024)(128)(2,1)S(1)}, bf16[4096]{0:T(1024)(128)(2,1)}, u32[]{:S(2)}) copy-start(bf16[4096]{0:T(1024)(128)(2,1)} %param.27) | copy-start | bytes 24580
  91.8 77.7 %copy-start.1 = (bf16[24,4096]{1,0:T(8,128)(2,1)S(1)}, bf16[24,4096]{1,0:T(8,128)(2,1)}, u32[]{:S(2)}) copy-start(bf16[24,4096]{1,0:T(8,128)(2,1)} %param.26) | copy-start | bytes 589828
Sparse Core Ops, SparseCore 0:
  96.0 73.5 all-reduce.1

commit v2 on v1

--- a/solution.py
+++ b/solution.py
@@ -195,7 +195,15 @@
     )
     attended = attended.reshape(req_dev, heads_dev * HD).astype(jnp.bfloat16)
     partial_value = jnp.dot(attended, o_weight, preferred_element_type=jnp.float32)
-    proj = lax.psum(partial_value, "tp")
+    lanes = lax.axis_size("tp")
+    width = partial_value.shape[1] // lanes
+    pieces = lax.all_to_all(
+        partial_value.reshape(req_dev, lanes, width).transpose(1, 0, 2), "tp", 0, 0, tiled=True
+    )
+    owned_sum = jnp.sum(pieces, axis=0)
+    spread = jnp.broadcast_to(owned_sum[None], (lanes, req_dev, width))
+    gathered = lax.all_to_all(spread, "tp", 0, 0, tiled=True)
+    proj = gathered.transpose(1, 0, 2).reshape(req_dev, lanes * width)
     summed = residual.astype(jnp.float32) + proj
     hidden = summed.astype(jnp.bfloat16)
     inverse = lax.rsqrt(jnp.mean(summed * summed, axis=-1, keepdims=True) + NORM_EPS)

time: 181 us -> 133 us (0.73)
  waiting for transfers between devices: 80.3 us -> 14 us
  blocking collectives: 0 us -> 23.3 us
  between operations: 14.3 us -> 0.98 us
  local copies, waits for them, and re-layouts: 5.63 us -> 13 us
  starting transfers between devices: 15 us -> 18.5 us
  other arithmetic: 23.8 us -> 21.8 us
    psum x1 -> x0, waiting for transfers between devices: 73.7 us -> none  [body(): proj = lax.psum(partial_value, 'tp')]
    all_to_all x0 -> x1, blocking collectives: none -> 23.3 us  [body(): lax.all_to_all(partial_value.reshape(req_dev, lanes, width).transpose(1,...]
    all_to_all x0 -> x1, waiting for transfers between devices: none -> 13.9 us  [body(): gathered = lax.all_to_all(spread, 'tp', 0, 0, tiled=True)]
    dot_general x0 -> x1, local copies, waits for them, and re-layouts: none -> 6.54 us  [body(): jnp.dot(attended, o_weight, preferred_element_type=jnp.float32)]
    all_to_all x1, waiting for transfers between devices: 6.6 us -> 0.1 us  [body(): lax.all_to_all(packed.reshape(places, capacity, packed.shape[1]), 'req',...]
    all_to_all x0 -> x1, starting transfers between devices: none -> 3.45 us  [body(): gathered = lax.all_to_all(spread, 'tp', 0, 0, tiled=True)]
  transfers between devices with their start and end apart: 3 -> 3, of which waited for: 2 -> 2; matrix products, arithmetic and copies ran while one was open for 4% -> 10% of each run, Pallas kernels for 0% -> 0%
where the time goes in v2:
time: 133 us; the launch traced here: 132 us
  matrix products  39.1 us (29%)
  blocking collectives  23.3 us (18%)
  other arithmetic  21.8 us (16%)
  starting transfers between devices  18.5 us (14%)
  waiting for transfers between devices  14 us (11%)
  local copies, waits for them, and re-layouts  13 us (10%)
    all_to_all x1, blocking collectives, body(): lax.all_to_all(partial_value.reshape(req_dev, lanes, width).transpose(1,...  23.3 us
    dot_general x12, matrix products, key_step(): jnp.einsum('rkhgp,gpkd->rkhd', rounded, value_block, preferred_element_ty...  16.8 us
    dot_general x12, matrix products, key_step(): jnp.einsum('rkhd,gpkd->rkhgp', queries, key_block, preferred_element_type...  16.3 us
    all_to_all x1, waiting for transfers between devices, body(): gathered = lax.all_to_all(spread, 'tp', 0, 0, tiled=True)  13.9 us
    lt x12, other arithmetic, key_step(): inside = positions[None, :] < prompt_len[:, None]  8.77 us
    all_to_all x1, starting transfers between devices, body(): lax.all_to_all(send_query.reshape(places, capacity, heads_dev * HD), 'req...  7.62 us
    all_to_all x1, starting transfers between devices, body(): lax.all_to_all(packed.reshape(places, capacity, packed.shape[1]), 'req',...  7.38 us
    dot_general x1, local copies, waits for them, and re-layouts, body(): jnp.dot(attended, o_weight, preferred_element_type=jnp.float32)  6.54 us
  transfers between devices with their start and end apart: 3, of which 2 were waited for; matrix products, arithmetic and copies ran while one was open for 10% of the time, Pallas kernels for 0%

profile of v2, /device:TPU:2, one launch (start us, length us, event | category | flops | bytes accessed | tf_op | source)
XLA Modules:
  0.0 131.5 jit_solution(12909562380561389457)
XLA Ops:
  0.7 0.8 and_select_fusion
  1.7 0.8 compare_select_fusion
  2.4 0.9 convolution_convert_fusion
  4.0 7.6 %all-to-all-start = ((bf16[32,2,512]{2,1,0:T(2,128)(2,1)}), bf16[32,2,512]{2,1,0:T(2,128)(2,1)S(1)}, u32[]{:S(2)}, u32[]{:S(2)}) async-start(bf16[32,2,512]{2,1,0:T(2,128)(2,1)} %reshape.355), calls=%async_computation | async-start | bytes 131072 | tf_op jit(solution)/shard_map/all_to_all | solution.py:140
  12.5 0.8 broadcast_in_dim.182
  13.3 0.8 broadcast_in_dim.192
  14.1 0.8 dynamic_slice.21
  14.8 0.7 reshape.358
  16.5 0.7 fusion.46
  17.3 0.8 fusion.40
  18.9 50.0 %while.18 = (s32[]{:T(128)}, f32[64,1,4]{0,2,1:T(4,128)S(1)}, f32[64,1,4]{0,2,1:T(4,128)S(1)}, f32[64,1,4,128]{3,0,2,1:T(8,128)S(1)}, s32[2]{0:T(128)}, /*index=...) while((s32[]{:T(128)}, f32[64,1,4]{0,2,1:T(4,128)S(1)}, ...), condition=%wide.region_9.10_spmd.clone, body=%wide.region_6.9_spmd.clone.sunk | while | flops 136876160 | bytes 4351959 | solution.py:69
  19.9 1.4 %fusion.66 = (f32[64,4]{0,1:T(4,128)S(1)}, f32[64,1,4,2,512]{4,0,2,3,1:T(8,128)S(1)}) fusion(bf16[64,1,4,128]{3,0,2,1:T(8,128)(2,1)S(1)} %get-tuple-element.394, bf16[2,6144,128]{2,1,0:T(8,128)(2,1)} %get-tuple-element.393, s32[]{:T(128)S(6)} %select_n.147, pred[64,2,512]{2,0,1:T(8,128)(4,1)S(1)} %and_and_fusion.2), kind=kOutput, calls=%fused_computation.105.clone.1 | convolution fusion | flops 67895040 | bytes 1442820 | tf_op jit(solution)/shard_map/while/body/eval_jaxpr/rkhd,gpkd->rkhgp/dot_general | solution.py:45
  21.3 1.4 %fusion.69 = f32[64,1,4,128]{3,0,2,1:T(8,128)S(1)} fusion(f32[64,1,4,2,512]{4,0,2,3,1:T(8,128)S(1)} %get-tuple-element.357, f32[64,4]{0,1:T(4,128)S(1)} %bitcast.88, pred[64,2,512]{2,0,1:T(8,128)(4,1)S(1)} %and_and_fusion.2, bf16[2,6144,128]{2,1,0:T(8,128)(2,1)} %get-tuple-element.395, s32[]{:T(128)S(6)} %select_n.147, ...), kind=kOutput, calls=%fused_computation.6.clone.1 | convolution fusion | flops 67993600 | bytes 1640453 | tf_op jit(solution)/shard_map/while/body/eval_jaxpr/rkhgp,gpkd->rkhd/dot_general | solution.py:59
  24.1 1.4 %fusion.66 = (f32[64,4]{0,1:T(4,128)S(1)}, f32[64,1,4,2,512]{4,0,2,3,1:T(8,128)S(1)}) fusion(bf16[64,1,4,128]{3,0,2,1:T(8,128)(2,1)S(1)} %get-tuple-element.394, bf16[2,6144,128]{2,1,0:T(8,128)(2,1)} %get-tuple-element.393, s32[]{:T(128)S(6)} %select_n.147, pred[64,2,512]{2,0,1:T(8,128)(4,1)S(1)} %and_and_fusion.2), kind=kOutput, calls=%fused_computation.105.clone.1 | convolution fusion | flops 67895040 | bytes 1442820 | tf_op jit(solution)/shard_map/while/body/eval_jaxpr/rkhd,gpkd->rkhgp/dot_general | solution.py:45
  25.4 1.4 %fusion.69 = f32[64,1,4,128]{3,0,2,1:T(8,128)S(1)} fusion(f32[64,1,4,2,512]{4,0,2,3,1:T(8,128)S(1)} %get-tuple-element.357, f32[64,4]{0,1:T(4,128)S(1)} %bitcast.88, pred[64,2,512]{2,0,1:T(8,128)(4,1)S(1)} %and_and_fusion.2, bf16[2,6144,128]{2,1,0:T(8,128)(2,1)} %get-tuple-element.395, s32[]{:T(128)S(6)} %select_n.147, ...), kind=kOutput, calls=%fused_computation.6.clone.1 | convolution fusion | flops 67993600 | bytes 1640453 | tf_op jit(solution)/shard_map/while/body/eval_jaxpr/rkhgp,gpkd->rkhd/dot_general | solution.py:59
  28.2 1.4 %fusion.66 = (f32[64,4]{0,1:T(4,128)S(1)}, f32[64,1,4,2,512]{4,0,2,3,1:T(8,128)S(1)}) fusion(bf16[64,1,4,128]{3,0,2,1:T(8,128)(2,1)S(1)} %get-tuple-element.394, bf16[2,6144,128]{2,1,0:T(8,128)(2,1)} %get-tuple-element.393, s32[]{:T(128)S(6)} %select_n.147, pred[64,2,512]{2,0,1:T(8,128)(4,1)S(1)} %and_and_fusion.2), kind=kOutput, calls=%fused_computation.105.clone.1 | convolution fusion | flops 67895040 | bytes 1442820 | tf_op jit(solution)/shard_map/while/body/eval_jaxpr/rkhd,gpkd->rkhgp/dot_general | solution.py:45
  29.6 1.4 %fusion.69 = f32[64,1,4,128]{3,0,2,1:T(8,128)S(1)} fusion(f32[64,1,4,2,512]{4,0,2,3,1:T(8,128)S(1)} %get-tuple-element.357, f32[64,4]{0,1:T(4,128)S(1)} %bitcast.88, pred[64,2,512]{2,0,1:T(8,128)(4,1)S(1)} %and_and_fusion.2, bf16[2,6144,128]{2,1,0:T(8,128)(2,1)} %get-tuple-element.395, s32[]{:T(128)S(6)} %select_n.147, ...), kind=kOutput, calls=%fused_computation.6.clone.1 | convolution fusion | flops 67993600 | bytes 1640453 | tf_op jit(solution)/shard_map/while/body/eval_jaxpr/rkhgp,gpkd->rkhd/dot_general | solution.py:59
  32.4 1.4 %fusion.66 = (f32[64,4]{0,1:T(4,128)S(1)}, f32[64,1,4,2,512]{4,0,2,3,1:T(8,128)S(1)}) fusion(bf16[64,1,4,128]{3,0,2,1:T(8,128)(2,1)S(1)} %get-tuple-element.394, bf16[2,6144,128]{2,1,0:T(8,128)(2,1)} %get-tuple-element.393, s32[]{:T(128)S(6)} %select_n.147, pred[64,2,512]{2,0,1:T(8,128)(4,1)S(1)} %and_and_fusion.2), kind=kOutput, calls=%fused_computation.105.clone.1 | convolution fusion | flops 67895040 | bytes 1442820 | tf_op jit(solution)/shard_map/while/body/eval_jaxpr/rkhd,gpkd->rkhgp/dot_general | solution.py:45
  33.8 1.4 %fusion.69 = f32[64,1,4,128]{3,0,2,1:T(8,128)S(1)} fusion(f32[64,1,4,2,512]{4,0,2,3,1:T(8,128)S(1)} %get-tuple-element.357, f32[64,4]{0,1:T(4,128)S(1)} %bitcast.88, pred[64,2,512]{2,0,1:T(8,128)(4,1)S(1)} %and_and_fusion.2, bf16[2,6144,128]{2,1,0:T(8,128)(2,1)} %get-tuple-element.395, s32[]{:T(128)S(6)} %select_n.147, ...), kind=kOutput, calls=%fused_computation.6.clone.1 | convolution fusion | flops 67993600 | bytes 1640453 | tf_op jit(solution)/shard_map/while/body/eval_jaxpr/rkhgp,gpkd->rkhd/dot_general | solution.py:59
  35.7 0.7 broadcast_compare_fusion.5
  36.6 1.4 %fusion.66 = (f32[64,4]{0,1:T(4,128)S(1)}, f32[64,1,4,2,512]{4,0,2,3,1:T(8,128)S(1)}) fusion(bf16[64,1,4,128]{3,0,2,1:T(8,128)(2,1)S(1)} %get-tuple-element.394, bf16[2,6144,128]{2,1,0:T(8,128)(2,1)} %get-tuple-element.393, s32[]{:T(128)S(6)} %select_n.147, pred[64,2,512]{2,0,1:T(8,128)(4,1)S(1)} %and_and_fusion.2), kind=kOutput, calls=%fused_computation.105.clone.1 | convolution fusion | flops 67895040 | bytes 1442820 | tf_op jit(solution)/shard_map/while/body/eval_jaxpr/rkhd,gpkd->rkhgp/dot_general | solution.py:45
  37.9 1.4 %fusion.69 = f32[64,1,4,128]{3,0,2,1:T(8,128)S(1)} fusion(f32[64,1,4,2,512]{4,0,2,3,1:T(8,128)S(1)} %get-tuple-element.357, f32[64,4]{0,1:T(4,128)S(1)} %bitcast.88, pred[64,2,512]{2,0,1:T(8,128)(4,1)S(1)} %and_and_fusion.2, bf16[2,6144,128]{2,1,0:T(8,128)(2,1)} %get-tuple-element.395, s32[]{:T(128)S(6)} %select_n.147, ...), kind=kOutput, calls=%fused_computation.6.clone.1 | convolution fusion | flops 67993600 | bytes 1640453 | tf_op jit(solution)/shard_map/while/body/eval_jaxpr/rkhgp,gpkd->rkhd/dot_general | solution.py:59
  39.9 0.7 broadcast_compare_fusion.5
  40.7 1.4 %fusion.66 = (f32[64,4]{0,1:T(4,128)S(1)}, f32[64,1,4,2,512]{4,0,2,3,1:T(8,128)S(1)}) fusion(bf16[64,1,4,128]{3,0,2,1:T(8,128)(2,1)S(1)} %get-tuple-element.394, bf16[2,6144,128]{2,1,0:T(8,128)(2,1)} %get-tuple-element.393, s32[]{:T(128)S(6)} %select_n.147, pred[64,2,512]{2,0,1:T(8,128)(4,1)S(1)} %and_and_fusion.2), kind=kOutput, calls=%fused_computation.105.clone.1 | convolution fusion | flops 67895040 | bytes 1442820 | tf_op jit(solution)/shard_map/while/body/eval_jaxpr/rkhd,gpkd->rkhgp/dot_general | solution.py:45
  42.1 1.4 %fusion.69 = f32[64,1,4,128]{3,0,2,1:T(8,128)S(1)} fusion(f32[64,1,4,2,512]{4,0,2,3,1:T(8,128)S(1)} %get-tuple-element.357, f32[64,4]{0,1:T(4,128)S(1)} %bitcast.88, pred[64,2,512]{2,0,1:T(8,128)(4,1)S(1)} %and_and_fusion.2, bf16[2,6144,128]{2,1,0:T(8,128)(2,1)} %get-tuple-element.395, s32[]{:T(128)S(6)} %select_n.147, ...), kind=kOutput, calls=%fused_computation.6.clone.1 | convolution fusion | flops 67993600 | bytes 1640453 | tf_op jit(solution)/shard_map/while/body/eval_jaxpr/rkhgp,gpkd->rkhd/dot_general | solution.py:59
  44.0 0.7 broadcast_compare_fusion.5
  44.9 1.4 %fusion.66 = (f32[64,4]{0,1:T(4,128)S(1)}, f32[64,1,4,2,512]{4,0,2,3,1:T(8,128)S(1)}) fusion(bf16[64,1,4,128]{3,0,2,1:T(8,128)(2,1)S(1)} %get-tuple-element.394, bf16[2,6144,128]{2,1,0:T(8,128)(2,1)} %get-tuple-element.393, s32[]{:T(128)S(6)} %select_n.147, pred[64,2,512]{2,0,1:T(8,128)(4,1)S(1)} %and_and_fusion.2), kind=kOutput, calls=%fused_computation.105.clone.1 | convolution fusion | flops 67895040 | bytes 1442820 | tf_op jit(solution)/shard_map/while/body/eval_jaxpr/rkhd,gpkd->rkhgp/dot_general | solution.py:45
  46.3 1.4 %fusion.69 = f32[64,1,4,128]{3,0,2,1:T(8,128)S(1)} fusion(f32[64,1,4,2,512]{4,0,2,3,1:T(8,128)S(1)} %get-tuple-element.357, f32[64,4]{0,1:T(4,128)S(1)} %bitcast.88, pred[64,2,512]{2,0,1:T(8,128)(4,1)S(1)} %and_and_fusion.2, bf16[2,6144,128]{2,1,0:T(8,128)(2,1)} %get-tuple-element.395, s32[]{:T(128)S(6)} %select_n.147, ...), kind=kOutput, calls=%fused_computation.6.clone.1 | convolution fusion | flops 67993600 | bytes 1640453 | tf_op jit(solution)/shard_map/while/body/eval_jaxpr/rkhgp,gpkd->rkhd/dot_general | solution.py:59
  48.2 0.7 broadcast_compare_fusion.5
  49.1 1.4 %fusion.66 = (f32[64,4]{0,1:T(4,128)S(1)}, f32[64,1,4,2,512]{4,0,2,3,1:T(8,128)S(1)}) fusion(bf16[64,1,4,128]{3,0,2,1:T(8,128)(2,1)S(1)} %get-tuple-element.394, bf16[2,6144,128]{2,1,0:T(8,128)(2,1)} %get-tuple-element.393, s32[]{:T(128)S(6)} %select_n.147, pred[64,2,512]{2,0,1:T(8,128)(4,1)S(1)} %and_and_fusion.2), kind=kOutput, calls=%fused_computation.105.clone.1 | convolution fusion | flops 67895040 | bytes 1442820 | tf_op jit(solution)/shard_map/while/body/eval_jaxpr/rkhd,gpkd->rkhgp/dot_general | solution.py:45
  50.4 1.4 %fusion.69 = f32[64,1,4,128]{3,0,2,1:T(8,128)S(1)} fusion(f32[64,1,4,2,512]{4,0,2,3,1:T(8,128)S(1)} %get-tuple-element.357, f32[64,4]{0,1:T(4,128)S(1)} %bitcast.88, pred[64,2,512]{2,0,1:T(8,128)(4,1)S(1)} %and_and_fusion.2, bf16[2,6144,128]{2,1,0:T(8,128)(2,1)} %get-tuple-element.395, s32[]{:T(128)S(6)} %select_n.147, ...), kind=kOutput, calls=%fused_computation.6.clone.1 | convolution fusion | flops 67993600 | bytes 1640453 | tf_op jit(solution)/shard_map/while/body/eval_jaxpr/rkhgp,gpkd->rkhd/dot_general | solution.py:59
  53.2 1.4 %fusion.66 = (f32[64,4]{0,1:T(4,128)S(1)}, f32[64,1,4,2,512]{4,0,2,3,1:T(8,128)S(1)}) fusion(bf16[64,1,4,128]{3,0,2,1:T(8,128)(2,1)S(1)} %get-tuple-element.394, bf16[2,6144,128]{2,1,0:T(8,128)(2,1)} %get-tuple-element.393, s32[]{:T(128)S(6)} %select_n.147, pred[64,2,512]{2,0,1:T(8,128)(4,1)S(1)} %and_and_fusion.2), kind=kOutput, calls=%fused_computation.105.clone.1 | convolution fusion | flops 67895040 | bytes 1442820 | tf_op jit(solution)/shard_map/while/body/eval_jaxpr/rkhd,gpkd->rkhgp/dot_general | solution.py:45
  54.6 1.4 %fusion.69 = f32[64,1,4,128]{3,0,2,1:T(8,128)S(1)} fusion(f32[64,1,4,2,512]{4,0,2,3,1:T(8,128)S(1)} %get-tuple-element.357, f32[64,4]{0,1:T(4,128)S(1)} %bitcast.88, pred[64,2,512]{2,0,1:T(8,128)(4,1)S(1)} %and_and_fusion.2, bf16[2,6144,128]{2,1,0:T(8,128)(2,1)} %get-tuple-element.395, s32[]{:T(128)S(6)} %select_n.147, ...), kind=kOutput, calls=%fused_computation.6.clone.1 | convolution fusion | flops 67993600 | bytes 1640453 | tf_op jit(solution)/shard_map/while/body/eval_jaxpr/rkhgp,gpkd->rkhd/dot_general | solution.py:59
  57.4 1.4 %fusion.66 = (f32[64,4]{0,1:T(4,128)S(1)}, f32[64,1,4,2,512]{4,0,2,3,1:T(8,128)S(1)}) fusion(bf16[64,1,4,128]{3,0,2,1:T(8,128)(2,1)S(1)} %get-tuple-element.394, bf16[2,6144,128]{2,1,0:T(8,128)(2,1)} %get-tuple-element.393, s32[]{:T(128)S(6)} %select_n.147, pred[64,2,512]{2,0,1:T(8,128)(4,1)S(1)} %and_and_fusion.2), kind=kOutput, calls=%fused_computation.105.clone.1 | convolution fusion | flops 67895040 | bytes 1442820 | tf_op jit(solution)/shard_map/while/body/eval_jaxpr/rkhd,gpkd->rkhgp/dot_general | solution.py:45
  58.8 1.4 %fusion.69 = f32[64,1,4,128]{3,0,2,1:T(8,128)S(1)} fusion(f32[64,1,4,2,512]{4,0,2,3,1:T(8,128)S(1)} %get-tuple-element.357, f32[64,4]{0,1:T(4,128)S(1)} %bitcast.88, pred[64,2,512]{2,0,1:T(8,128)(4,1)S(1)} %and_and_fusion.2, bf16[2,6144,128]{2,1,0:T(8,128)(2,1)} %get-tuple-element.395, s32[]{:T(128)S(6)} %select_n.147, ...), kind=kOutput, calls=%fused_computation.6.clone.1 | convolution fusion | flops 67993600 | bytes 1640453 | tf_op jit(solution)/shard_map/while/body/eval_jaxpr/rkhgp,gpkd->rkhd/dot_general | solution.py:59
  61.6 1.4 %fusion.66 = (f32[64,4]{0,1:T(4,128)S(1)}, f32[64,1,4,2,512]{4,0,2,3,1:T(8,128)S(1)}) fusion(bf16[64,1,4,128]{3,0,2,1:T(8,128)(2,1)S(1)} %get-tuple-element.394, bf16[2,6144,128]{2,1,0:T(8,128)(2,1)} %get-tuple-element.393, s32[]{:T(128)S(6)} %select_n.147, pred[64,2,512]{2,0,1:T(8,128)(4,1)S(1)} %and_and_fusion.2), kind=kOutput, calls=%fused_computation.105.clone.1 | convolution fusion | flops 67895040 | bytes 1442820 | tf_op jit(solution)/shard_map/while/body/eval_jaxpr/rkhd,gpkd->rkhgp/dot_general | solution.py:45
  63.0 1.4 %fusion.69 = f32[64,1,4,128]{3,0,2,1:T(8,128)S(1)} fusion(f32[64,1,4,2,512]{4,0,2,3,1:T(8,128)S(1)} %get-tuple-element.357, f32[64,4]{0,1:T(4,128)S(1)} %bitcast.88, pred[64,2,512]{2,0,1:T(8,128)(4,1)S(1)} %and_and_fusion.2, bf16[2,6144,128]{2,1,0:T(8,128)(2,1)} %get-tuple-element.395, s32[]{:T(128)S(6)} %select_n.147, ...), kind=kOutput, calls=%fused_computation.6.clone.1 | convolution fusion | flops 67993600 | bytes 1640453 | tf_op jit(solution)/shard_map/while/body/eval_jaxpr/rkhgp,gpkd->rkhd/dot_general | solution.py:59
  65.7 1.4 %fusion.66 = (f32[64,4]{0,1:T(4,128)S(1)}, f32[64,1,4,2,512]{4,0,2,3,1:T(8,128)S(1)}) fusion(bf16[64,1,4,128]{3,0,2,1:T(8,128)(2,1)S(1)} %get-tuple-element.394, bf16[2,6144,128]{2,1,0:T(8,128)(2,1)} %get-tuple-element.393, s32[]{:T(128)S(6)} %select_n.147, pred[64,2,512]{2,0,1:T(8,128)(4,1)S(1)} %and_and_fusion.2), kind=kOutput, calls=%fused_computation.105.clone.1 | convolution fusion | flops 67895040 | bytes 1442820 | tf_op jit(solution)/shard_map/while/body/eval_jaxpr/rkhd,gpkd->rkhgp/dot_general | solution.py:45
  67.1 1.4 %fusion.69 = f32[64,1,4,128]{3,0,2,1:T(8,128)S(1)} fusion(f32[64,1,4,2,512]{4,0,2,3,1:T(8,128)S(1)} %get-tuple-element.357, f32[64,4]{0,1:T(4,128)S(1)} %bitcast.88, pred[64,2,512]{2,0,1:T(8,128)(4,1)S(1)} %and_and_fusion.2, bf16[2,6144,128]{2,1,0:T(8,128)(2,1)} %get-tuple-element.395, s32[]{:T(128)S(6)} %select_n.147, ...), kind=kOutput, calls=%fused_computation.6.clone.1 | convolution fusion | flops 67993600 | bytes 1640453 | tf_op jit(solution)/shard_map/while/body/eval_jaxpr/rkhgp,gpkd->rkhd/dot_general | solution.py:59
  69.4 0.7 pad_maximum_fusion
  70.1 7.4 %all-to-all-start.1 = ((f32[32,2,516]{2,1,0:T(2,128)}), f32[32,2,516]{2,1,0:T(2,128)S(1)}, u32[]{:S(2)}, u32[]{:S(2)}) async-start(f32[32,2,516]{2,1,0:T(2,128)} %pad_maximum_fusion), calls=%async_computation.1 | async-start | bytes 327680 | tf_op jit(solution)/shard_map/all_to_all | solution.py:147
  77.5 6.5 %copy.50 = bf16[4096,512]{1,0:T(8,128)(2,1)} copy(bf16[4096,512]{0,1:T(8,128)(2,1)} %bitcast.84) | data formatting | bytes 8388608 | tf_op jit(solution)/shard_map/dot_general | solution.py:197
  85.6 3.4 %convolution_bitcast_fusion.1 = f32[8,24,512]{2,1,0:T(8,128)S(1)} fusion(bf16[24,512,1]{1,0,2:T(8,128)(2,1)S(1)} %reshape.377, bf16[8,512,512]{2,1,0:T(8,128)(2,1)} %bitcast.83), kind=kOutput, calls=%fused_computation.34 | convolution fusion | flops 100663296 | bytes 4612096 | tf_op jit(solution)/shard_map/dot_general | solution.py:197
  89.1 23.3 %all_to_all.20 = f32[8,24,512]{2,1,0:T(8,128)S(1)} all-to-all(f32[8,24,512]{2,1,0:T(8,128)S(1)} %convolution_bitcast_fusion.1), channel_id=1, replica_groups=mesh['req'=32,'tp'=8] {'tp'}, dimensions={0} | all-to-all | bytes 786432 | tf_op jit(solution)/shard_map/all_to_all | solution.py:200
  112.4 0.8 broadcast_in_dim.199
  113.1 3.5 %all-to-all-start.3 = ((f32[8,24,512]{2,1,0:T(8,128)}), f32[8,24,512]{2,1,0:T(8,128)S(1)}, u32[]{:S(2)}, u32[]{:S(2)}) async-start(f32[8,24,512]{2,1,0:T(8,128)} %broadcast_in_dim.199), calls=%async_computation.3 | async-start | bytes 786432 | tf_op jit(solution)/shard_map/all_to_all | solution.py:205
  116.6 13.9 %all-to-all-done.3 = f32[8,24,512]{2,1,0:T(8,128)S(1)} async-done(((f32[8,24,512]{2,1,0:T(8,128)}), f32[8,24,512]{2,1,0:T(8,128)S(1)}, u32[]{:S(2)}, u32[]{:S(2)}) %all-to-all-start.3) | async-done | bytes 393248 | tf_op jit(solution)/shard_map/all_to_all | solution.py:205
  130.7 0.8 multiply_convert_fusion
  (177 shorter events, 18.6 us)
Async XLA Ops:
  0.6 17.5 %copy-start = (bf16[24,128,128]{2,1,0:T(8,128)(2,1)S(1)}, bf16[24,128,128]{2,1,0:T(8,128)(2,1)}, u32[]{:S(2)}) copy-start(bf16[24,128,128]{2,1,0:T(8,128)(2,1)} %param.20) | copy-start | bytes 2359300
  4.0 14.8 %all-to-all-start = ((bf16[32,2,512]{2,1,0:T(2,128)(2,1)}), bf16[32,2,512]{2,1,0:T(2,128)(2,1)S(1)}, u32[]{:S(2)}, u32[]{:S(2)}) async-start(bf16[32,2,512]{2,1,0:T(2,128)(2,1)} %reshape.355), calls=%async_computation | async-start | bytes 131072 | tf_op jit(solution)/shard_map/all_to_all | solution.py:140
  18.9 58.6 %copy-start.3 = (bf16[24,128]{1,0:T(8,128)(2,1)S(1)}, bf16[24,128]{1,0:T(8,128)(2,1)}, u32[]{:S(2)}) copy-start(bf16[24,128]{1,0:T(8,128)(2,1)} %param.17) | copy-start | bytes 18436
  70.1 14.3 %all-to-all-start.1 = ((f32[32,2,516]{2,1,0:T(2,128)}), f32[32,2,516]{2,1,0:T(2,128)S(1)}, u32[]{:S(2)}, u32[]{:S(2)}) async-start(f32[32,2,516]{2,1,0:T(2,128)} %pad_maximum_fusion), calls=%async_computation.1 | async-start | bytes 327680 | tf_op jit(solution)/shard_map/all_to_all | solution.py:147
  77.5 7.7 %copy-start.4 = (bf16[24,128,128]{2,1,0:T(8,128)(2,1)S(1)}, bf16[24,128,128]{2,1,0:T(8,128)(2,1)}, u32[]{:S(2)}) copy-start(bf16[24,128,128]{2,1,0:T(8,128)(2,1)} %param.21) | copy-start | bytes 2359300
  85.6 31.0 %copy-start.2 = (bf16[4096]{0:T(1024)(128)(2,1)S(1)}, bf16[4096]{0:T(1024)(128)(2,1)}, u32[]{:S(2)}) copy-start(bf16[4096]{0:T(1024)(128)(2,1)} %param.27) | copy-start | bytes 24580
  85.6 44.9 %copy-start.1 = (bf16[24,4096]{1,0:T(8,128)(2,1)S(1)}, bf16[24,4096]{1,0:T(8,128)(2,1)}, u32[]{:S(2)}) copy-start(bf16[24,4096]{1,0:T(8,128)(2,1)} %param.26) | copy-start | bytes 589828
  113.1 17.4 %all-to-all-start.3 = ((f32[8,24,512]{2,1,0:T(8,128)}), f32[8,24,512]{2,1,0:T(8,128)S(1)}, u32[]{:S(2)}, u32[]{:S(2)}) async-start(f32[8,24,512]{2,1,0:T(8,128)} %broadcast_in_dim.199), calls=%async_computation.3 | async-start | bytes 786432 | tf_op jit(solution)/shard_map/all_to_all | solution.py:205

commit v3 on v2

--- a/solution.py
+++ b/solution.py
@@ -4,6 +4,8 @@
 import jax.numpy as jnp
 from jax import lax
 from jax.sharding import PartitionSpec as P
+from jax.experimental import pallas as pl
+from jax.experimental.pallas import tpu as pltpu
 
 HD = 128
 WIN = 4096
@@ -75,6 +77,112 @@
         row_count, heads_dev
     )
     return (normalized, log_total)
+
+
+def prefix_kernel(
+    prompt_ref, low_ref, has_ref, query_ref, key_ref, value_ref, group_ref, bound_ref,
+    out_ref, log_ref, running, weight_sum, weighted,
+):
+    g = pl.program_id(0)
+    j = pl.program_id(1)
+    block_len = key_ref.shape[0]
+
+    @pl.when((g == 0) & (j == 0))
+    def _init():
+        running[...] = jnp.full(running.shape, FAR_BELOW, jnp.float32)
+        weight_sum[...] = jnp.zeros(weight_sum.shape, jnp.float32)
+        weighted[...] = jnp.zeros(weighted.shape, jnp.float32)
+
+    key_start = j * block_len
+    prompt_count = prompt_ref[g]
+    needed = (
+        (has_ref[g] > 0)
+        & (key_start < prompt_count)
+        & ((j == 0) | (key_start + block_len > low_ref[g]))
+    )
+
+    @pl.when(needed)
+    def _step():
+        scores = lax.dot_general(
+            query_ref[...], key_ref[...], (((1,), (1,)), ((), ())),
+            preferred_element_type=jnp.float32,
+        ) * (1.0 / math.sqrt(HD))
+        positions = key_start + lax.broadcasted_iota(jnp.int32, scores.shape, 1)
+        usable = (
+            (group_ref[...] == g)
+            & (positions < prompt_count)
+            & ((positions < SINKS) | (positions >= bound_ref[...]))
+        )
+        masked = jnp.where(usable, scores, FAR_BELOW)
+        old = running[...]
+        updated = jnp.maximum(old, jnp.max(masked, axis=1, keepdims=True))
+        weights = jnp.where(usable, jnp.exp(masked - updated), 0.0)
+        rescale = jnp.exp(old - updated)
+        weight_sum[...] = weight_sum[...] * rescale + jnp.sum(weights, axis=1, keepdims=True)
+        weighted[...] = weighted[...] * rescale + jnp.dot(
+            weights.astype(jnp.bfloat16), value_ref[...], preferred_element_type=jnp.float32
+        )
+        running[...] = updated
+
+    @pl.when((g == pl.num_programs(0) - 1) & (j == pl.num_programs(1) - 1))
+    def _finish():
+        bounded = jnp.maximum(weight_sum[...], 1.0)
+        out_ref[...] = weighted[...] / bounded
+        log_ref[...] = running[...] + jnp.log(bounded)
+
+
+def prefix_attend_kernel(
+    rows_query, row_group, row_suffix, prefix_key, prefix_value, prompt_len, first_group
+):
+    row_count = rows_query.shape[0]
+    groups_dev, prompt_max, _ = prefix_key.shape
+    heads_dev = rows_query.shape[1] // HD
+    block_len = min(512, prompt_max)
+    local_group = row_group - first_group
+    owned = (local_group >= 0) & (local_group < groups_dev)
+    member = local_group[:, None] == jnp.arange(groups_dev, dtype=jnp.int32)[None, :]
+    row_prompt = jnp.sum(jnp.where(member, prompt_len[None, :], 0), axis=1)
+    row_low = row_prompt + row_suffix - WIN + 1
+    group_low = jnp.min(jnp.where(member, row_low[:, None], prompt_max), axis=0).astype(jnp.int32)
+    group_has = jnp.sum(member.astype(jnp.int32), axis=0).astype(jnp.int32)
+    rows = row_count * heads_dev
+    flat_query = rows_query.reshape(rows, HD)
+    flat_group = jnp.repeat(jnp.where(owned, local_group, -1), heads_dev).reshape(rows, 1)
+    flat_bound = jnp.repeat(row_low, heads_dev).reshape(rows, 1).astype(jnp.int32)
+    whole = lambda g, j, *_: (0, 0)
+    cache = lambda g, j, *_: (g, j, 0)
+    out, log = pl.pallas_call(
+        prefix_kernel,
+        grid_spec=pltpu.PrefetchScalarGridSpec(
+            num_scalar_prefetch=3,
+            grid=(groups_dev, prompt_max // block_len),
+            in_specs=[
+                pl.BlockSpec((rows, HD), whole),
+                pl.BlockSpec((None, block_len, HD), cache),
+                pl.BlockSpec((None, block_len, HD), cache),
+                pl.BlockSpec((rows, 1), whole),
+                pl.BlockSpec((rows, 1), whole),
+            ],
+            out_specs=[pl.BlockSpec((rows, HD), whole), pl.BlockSpec((rows, 1), whole)],
+            scratch_shapes=[
+                pltpu.VMEM((rows, 1), jnp.float32),
+                pltpu.VMEM((rows, 1), jnp.float32),
+                pltpu.VMEM((rows, HD), jnp.float32),
+            ],
+        ),
+        out_shape=[
+            jax.ShapeDtypeStruct((rows, HD), jnp.float32),
+            jax.ShapeDtypeStruct((rows, 1), jnp.float32),
+        ],
+        compiler_params=pltpu.CompilerParams(dimension_semantics=("arbitrary", "arbitrary")),
+        cost_estimate=pl.CostEstimate(
+            flops=4 * rows * groups_dev * prompt_max * HD,
+            transcendentals=rows * groups_dev * prompt_max,
+            bytes_accessed=2 * prefix_key.size * 2 + rows * HD * 6,
+        ),
+    )(prompt_len.astype(jnp.int32), group_low, group_has, flat_query, prefix_key, prefix_value,
+      flat_group, flat_bound)
+    return out.reshape(row_count, heads_dev * HD), log.reshape(row_count, heads_dev)
 
 
 def body(
@@ -140,8 +248,8 @@
     compact = lax.all_to_all(
         send_query.reshape(places, capacity, heads_dev * HD), "req", 0, 0, tiled=True
     ).reshape(slot_total, heads_dev * HD)
-    part_out, part_log = prefix_attend(
-        compact, slot_group, slot_suffix, prefix_key, prefix_value, prompt_len, first_group, blocks
+    part_out, part_log = prefix_attend_kernel(
+        compact, slot_group, slot_suffix, prefix_key, prefix_value, prompt_len, first_group
     )
     packed = jnp.concatenate([part_out, part_log], axis=1)
     returned = lax.all_to_all(

time: 133 us -> 109 us (0.82)
  matrix products: 39.1 us -> 6.11 us
  Pallas kernels: 0 us -> 19.1 us
  other arithmetic: 21.8 us -> 7.34 us
  local copies, waits for them, and re-layouts: 13 us -> 16 us
  starting transfers between devices: 18.5 us -> 21 us
    dot_general x24 -> x0, matrix products: 33 us -> none  [the longest x12 16.8 us: key_step(): jnp.einsum('rkhgp,gpkd->rkhd', rounded, value_block, preferred_element_ty...]
    pallas_call x0 -> x1, Pallas kernels: none -> 19.1 us  [prefix_attend_kernel(): pl.pallas_call(prefix_kernel, grid_spec=pltpu.PrefetchScalarGridSpec(num_...]
    lt x24 -> x0, other arithmetic: 8.85 us -> none  [the longest x12 8.77 us: key_step(): inside = positions[None, :] < prompt_len[:, None]]
    reduce_sum x13 -> x2, other arithmetic: 5.08 us -> 1.45 us  [the longest x1 0.74 us: prefix_attend_kernel(): row_prompt = jnp.sum(jnp.where(member, prompt_len[None, :], 0), axis=1)]
    all_to_all x1, starting transfers between devices: 7.38 us -> 9.97 us  [body(): lax.all_to_all(packed.reshape(places, capacity, packed.shape[1]), 'req',...]
    another operation x2 -> x4, local copies, waits for them, and re-layouts: 0.8 us -> 2.92 us  [the longest x1 0.76 us: prefix_attend_kernel(): jnp.repeat(row_low, heads_dev).reshape(rows, 1).astype(jnp.int32)]
  transfers between devices with their start and end apart: 3 -> 3, of which waited for: 2 -> 2; matrix products, arithmetic and copies ran while one was open for 10% -> 15% of each run, Pallas kernels for 0% -> 0%
where the time goes in v3:
time: 109 us; the launch traced here: 108 us
  blocking collectives  23.3 us (21%)
  starting transfers between devices  21 us (19%)
  Pallas kernels  19.1 us (18%)
  local copies, waits for them, and re-layouts  16 us (15%)
  waiting for transfers between devices  14 us (13%)
  other arithmetic  7.34 us (7%)
  matrix products  6.11 us (6%)
    all_to_all x1, blocking collectives, body(): lax.all_to_all(partial_value.reshape(req_dev, lanes, width).transpose(1,...  23.3 us
    pallas_call x1, Pallas kernels, prefix_attend_kernel(): pl.pallas_call(prefix_kernel, grid_spec=pltpu.PrefetchScalarGridSpec(num_...  19.1 us
    all_to_all x1, waiting for transfers between devices, body(): gathered = lax.all_to_all(spread, 'tp', 0, 0, tiled=True)  13.9 us
    all_to_all x1, starting transfers between devices, body(): lax.all_to_all(packed.reshape(places, capacity, packed.shape[1]), 'req',...  9.97 us
    all_to_all x1, starting transfers between devices, body(): lax.all_to_all(send_query.reshape(places, capacity, heads_dev * HD), 'req...  7.62 us
    dot_general x1, local copies, waits for them, and re-layouts, body(): jnp.dot(attended, o_weight, preferred_element_type=jnp.float32)  6.54 us
    all_to_all x1, starting transfers between devices, body(): gathered = lax.all_to_all(spread, 'tp', 0, 0, tiled=True)  3.45 us
    dot_general x1, matrix products, body(): jnp.dot(attended, o_weight, preferred_element_type=jnp.float32)  3.42 us
  transfers between devices with their start and end apart: 3, of which 2 were waited for; matrix products, arithmetic and copies ran while one was open for 15% of the time, Pallas kernels for 0%

profile of v3, /device:TPU:2, one launch (start us, length us, event | category | flops | bytes accessed | tf_op | source)
XLA Modules:
  0.0 107.8 jit_solution(10570087462673980703)
XLA Ops:
  0.7 0.8 and_select_fusion.1
  1.5 0.2 convert_reduce_fusion
  1.7 0.8 compare_select_fusion
  2.4 0.9 convolution_convert_fusion
  3.3 0.7 reshape.204
  4.0 7.6 %all-to-all-start = ((bf16[32,2,512]{2,1,0:T(2,128)(2,1)}), bf16[32,2,512]{2,1,0:T(2,128)(2,1)S(1)}, u32[]{:S(2)}, u32[]{:S(2)}) async-start(bf16[32,2,512]{2,1,0:T(2,128)(2,1)} %reshape.204), calls=%async_computation | async-start | bytes 131072 | tf_op jit(solution)/shard_map/all_to_all | solution.py:248
  11.6 0.7 fusion.22
  12.3 0.1 eq.71
  12.4 0.1 copy.26
  12.5 0.8 broadcast_in_dim.110
  13.3 0.8 broadcast_in_dim.116
  14.1 0.8 dynamic_slice.7
  14.8 0.7 reshape.207
  15.6 0.2 reduce_window_sum.11
  15.8 0.1 copy.27
  16.1 0.1 copy.29
  16.1 0.1 sub.58
  16.3 0.7 select_reduce_fusion.3
  17.0 0.1 copy.31
  17.1 0.1 reshape.203
  17.2 0.1 broadcast_in_dim.122
  17.3 0.8 reshape_reshape.13.bound_ref
  18.0 0.1 broadcast_in_dim.121
  18.1 0.8 reshape_reshape.12.group_ref
  18.9 0.1 iota_compare_fusion.3
  18.9 0.8 fusion.19
  19.8 0.6 fusion.27
  20.4 0.7 convert_reduce_fusion.1
  21.1 0.7 reshape_reshape.9.query_ref
  21.8 19.1 %shard_map.140 = (f32[256,128]{1,0:T(8,128)}, f32[256,1]{1,0:T(8,128)}) custom-call(s32[2]{0:T(128)} %prompt_ref.1, s32[2]{0:T(128)} %get-tuple-element.9.low_ref, s32[2]{0:T(128)} %get-tuple-element.8.has_ref, bf16[256,128]{1,0:T(8,128)(2,1)} %reshape_reshape.9.query_ref, bf16[2,6144,128]{2,1,0:T(8,128)(2,1)} %key_ref.1, bf16[2,6144,128]{2,1,0:T(8,128)(2,1)} %value_ref.1, ...), custom_call_target="tpu_custom_call" | custom-call | flops 1610612736 | bytes 6488064 | tf_op jit(solution)/shard_map/pallas_call | solution.py:154
  40.9 1.0 concatenate.8
  41.9 1.0 reduce.4
  42.9 0.1 concatenate.9
  43.1 0.7 pad_maximum_fusion
  43.8 10.0 %all-to-all-start.1 = ((f32[32,2,516]{2,1,0:T(2,128)}), f32[32,2,516]{2,1,0:T(2,128)S(1)}, u32[]{:S(2)}, u32[]{:S(2)}) async-start(f32[32,2,516]{2,1,0:T(2,128)} %pad_maximum_fusion), calls=%async_computation.1 | async-start | bytes 327680 | tf_op jit(solution)/shard_map/all_to_all | solution.py:255
  53.8 6.5 %copy.38 = bf16[4096,512]{1,0:T(8,128)(2,1)} copy(bf16[4096,512]{0,1:T(8,128)(2,1)} %bitcast.18) | data formatting | bytes 8388608 | tf_op jit(solution)/shard_map/dot_general | solution.py:305
  60.4 0.2 fusion.7
  60.5 0.1 all-to-all-done.1
  60.6 0.1 reshape.205
  60.8 0.6 gather_fusion
  61.5 0.4 fusion.4
  61.9 3.4 %convolution_bitcast_fusion = f32[8,24,512]{2,1,0:T(8,128)S(1)} fusion(bf16[24,512,1]{1,0,2:T(8,128)(2,1)S(1)} %reshape.220, bf16[8,512,512]{2,1,0:T(8,128)(2,1)} %bitcast.17), kind=kOutput, calls=%fused_computation.1 | convolution fusion | flops 100663296 | bytes 4612096 | tf_op jit(solution)/shard_map/dot_general | solution.py:305
  65.3 23.3 %all_to_all.20 = f32[8,24,512]{2,1,0:T(8,128)S(1)} all-to-all(f32[8,24,512]{2,1,0:T(8,128)S(1)} %convolution_bitcast_fusion), channel_id=1, replica_groups=mesh['req'=32,'tp'=8] {'tp'}, dimensions={0} | all-to-all | bytes 786432 | tf_op jit(solution)/shard_map/all_to_all | solution.py:308
  88.6 0.8 broadcast_in_dim.127
  89.4 3.5 %all-to-all-start.3 = ((f32[8,24,512]{2,1,0:T(8,128)}), f32[8,24,512]{2,1,0:T(8,128)S(1)}, u32[]{:S(2)}, u32[]{:S(2)}) async-start(f32[8,24,512]{2,1,0:T(8,128)} %broadcast_in_dim.127), calls=%async_computation.3 | async-start | bytes 786432 | tf_op jit(solution)/shard_map/all_to_all | solution.py:313
  92.9 13.9 %all-to-all-done.3 = f32[8,24,512]{2,1,0:T(8,128)S(1)} async-done(((f32[8,24,512]{2,1,0:T(8,128)}), f32[8,24,512]{2,1,0:T(8,128)S(1)}, u32[]{:S(2)}, u32[]{:S(2)}) %all-to-all-start.3) | async-done | bytes 393248 | tf_op jit(solution)/shard_map/all_to_all | solution.py:313
  106.8 0.2 multiply_reduce_fusion
  107.0 0.8 multiply_convert_fusion
  (32 shorter events, 0.5 us)
Async XLA Ops:
  0.6 19.2 %copy-start = (bf16[24,128,128]{2,1,0:T(8,128)(2,1)S(1)}, bf16[24,128,128]{2,1,0:T(8,128)(2,1)}, u32[]{:S(2)}) copy-start(bf16[24,128,128]{2,1,0:T(8,128)(2,1)} %param.18) | copy-start | bytes 2359300
  4.0 17.1 %all-to-all-start = ((bf16[32,2,512]{2,1,0:T(2,128)(2,1)}), bf16[32,2,512]{2,1,0:T(2,128)(2,1)S(1)}, u32[]{:S(2)}, u32[]{:S(2)}) async-start(bf16[32,2,512]{2,1,0:T(2,128)(2,1)} %reshape.204), calls=%async_computation | async-start | bytes 131072 | tf_op jit(solution)/shard_map/all_to_all | solution.py:248
  19.8 34.0 %copy-start.3 = (bf16[24,128]{1,0:T(8,128)(2,1)S(1)}, bf16[24,128]{1,0:T(8,128)(2,1)}, u32[]{:S(2)}) copy-start(bf16[24,128]{1,0:T(8,128)(2,1)} %param.15) | copy-start | bytes 18436
  43.8 16.8 %all-to-all-start.1 = ((f32[32,2,516]{2,1,0:T(2,128)}), f32[32,2,516]{2,1,0:T(2,128)S(1)}, u32[]{:S(2)}, u32[]{:S(2)}) async-start(f32[32,2,516]{2,1,0:T(2,128)} %pad_maximum_fusion), calls=%async_computation.1 | async-start | bytes 327680 | tf_op jit(solution)/shard_map/all_to_all | solution.py:255
  53.8 7.7 %copy-start.4 = (bf16[24,128,128]{2,1,0:T(8,128)(2,1)S(1)}, bf16[24,128,128]{2,1,0:T(8,128)(2,1)}, u32[]{:S(2)}) copy-start(bf16[24,128,128]{2,1,0:T(8,128)(2,1)} %param.19) | copy-start | bytes 2359300
  61.5 31.4 %copy-start.2 = (bf16[4096]{0:T(1024)(128)(2,1)S(1)}, bf16[4096]{0:T(1024)(128)(2,1)}, u32[]{:S(2)}) copy-start(bf16[4096]{0:T(1024)(128)(2,1)} %param.25) | copy-start | bytes 24580
  61.9 44.9 %copy-start.1 = (bf16[24,4096]{1,0:T(8,128)(2,1)S(1)}, bf16[24,4096]{1,0:T(8,128)(2,1)}, u32[]{:S(2)}) copy-start(bf16[24,4096]{1,0:T(8,128)(2,1)} %param.24) | copy-start | bytes 589828
  89.4 17.4 %all-to-all-start.3 = ((f32[8,24,512]{2,1,0:T(8,128)}), f32[8,24,512]{2,1,0:T(8,128)S(1)}, u32[]{:S(2)}, u32[]{:S(2)}) async-start(f32[8,24,512]{2,1,0:T(8,128)} %broadcast_in_dim.127), calls=%async_computation.3 | async-start | bytes 786432 | tf_op jit(solution)/shard_map/all_to_all | solution.py:313

commit v4 on v3

--- a/solution.py
+++ b/solution.py
@@ -306,12 +306,12 @@
     lanes = lax.axis_size("tp")
     width = partial_value.shape[1] // lanes
     pieces = lax.all_to_all(
-        partial_value.reshape(req_dev, lanes, width).transpose(1, 0, 2), "tp", 0, 0, tiled=True
-    )
-    owned_sum = jnp.sum(pieces, axis=0)
-    spread = jnp.broadcast_to(owned_sum[None], (lanes, req_dev, width))
-    gathered = lax.all_to_all(spread, "tp", 0, 0, tiled=True)
-    proj = gathered.transpose(1, 0, 2).reshape(req_dev, lanes * width)
+        lax.optimization_barrier(partial_value).reshape(req_dev, lanes, width), "tp", 1, 1, tiled=True
+    )
+    owned_sum = jnp.sum(pieces, axis=1, keepdims=True)
+    spread = jnp.broadcast_to(owned_sum, (req_dev, lanes, width))
+    gathered = lax.all_to_all(spread, "tp", 1, 1, tiled=True)
+    proj = gathered.reshape(req_dev, lanes * width)
     summed = residual.astype(jnp.float32) + proj
     hidden = summed.astype(jnp.bfloat16)
     inverse = lax.rsqrt(jnp.mean(summed * summed, axis=-1, keepdims=True) + NORM_EPS)

time: 109 us -> 109 us (level)
  local copies, waits for them, and re-layouts: 16 us -> 9.5 us
  waiting for transfers between devices: 14 us -> 20.5 us
  Pallas kernels: 19.1 us -> 22.4 us
  starting transfers between devices: 21 us -> 18.9 us
    all_to_all x1, waiting for transfers between devices: 0.09 us -> 6.65 us  [body(): lax.all_to_all(packed.reshape(places, capacity, packed.shape[1]), 'req',...]
    dot_general x1 -> x0, local copies, waits for them, and re-layouts: 6.54 us -> none  [body(): jnp.dot(attended, o_weight, preferred_element_type=jnp.float32)]
    pallas_call x1, Pallas kernels: 19.1 us -> 22.4 us  [prefix_attend_kernel(): pl.pallas_call(prefix_kernel, grid_spec=pltpu.PrefetchScalarGridSpec(num_...]
    all_to_all x1, starting transfers between devices: 9.97 us -> 7.83 us  [body(): lax.all_to_all(packed.reshape(places, capacity, packed.shape[1]), 'req',...]
  transfers between devices with their start and end apart: 3 -> 3, of which waited for: 2 -> 2; matrix products, arithmetic and copies ran while one was open for 15% -> 9% of each run, Pallas kernels for 0% -> 0%
where the time goes in v4:
time: 109 us; the launch traced here: 108 us
  blocking collectives  23.3 us (21%)
  Pallas kernels  22.4 us (21%)
  waiting for transfers between devices  20.5 us (19%)
  starting transfers between devices  18.9 us (17%)
  local copies, waits for them, and re-layouts  9.5 us (9%)
  other arithmetic  7.34 us (7%)
  matrix products  5.58 us (5%)
    all_to_all x1, blocking collectives, body(): lax.all_to_all(lax.optimization_barrier(partial_value).reshape(req_dev, l...  23.3 us
    pallas_call x1, Pallas kernels, prefix_attend_kernel(): pl.pallas_call(prefix_kernel, grid_spec=pltpu.PrefetchScalarGridSpec(num_...  22.4 us
    all_to_all x1, waiting for transfers between devices, body(): gathered = lax.all_to_all(spread, 'tp', 1, 1, tiled=True)  13.9 us
    all_to_all x1, starting transfers between devices, body(): lax.all_to_all(packed.reshape(places, capacity, packed.shape[1]), 'req',...  7.83 us
    all_to_all x1, starting transfers between devices, body(): lax.all_to_all(send_query.reshape(places, capacity, heads_dev * HD), 'req...  7.62 us
    all_to_all x1, waiting for transfers between devices, body(): lax.all_to_all(packed.reshape(places, capacity, packed.shape[1]), 'req',...  6.65 us
    all_to_all x1, starting transfers between devices, body(): gathered = lax.all_to_all(spread, 'tp', 1, 1, tiled=True)  3.45 us
    dot_general x1, matrix products, body(): jnp.dot(attended, o_weight, preferred_element_type=jnp.float32)  2.89 us
  transfers between devices with their start and end apart: 3, of which 2 were waited for; matrix products, arithmetic and copies ran while one was open for 9% of the time, Pallas kernels for 0%

profile of v4, /device:TPU:2, one launch (start us, length us, event | category | flops | bytes accessed | tf_op | source)
XLA Modules:
  0.0 108.5 jit_solution(18383284253666116817)
XLA Ops:
  0.7 0.8 and_select_fusion.1
  1.5 0.2 convert_reduce_fusion
  1.7 0.8 compare_select_fusion
  2.4 0.9 convolution_convert_fusion
  3.3 0.7 reshape.204
  4.0 7.6 %all-to-all-start = ((bf16[32,2,512]{2,1,0:T(2,128)(2,1)}), bf16[32,2,512]{2,1,0:T(2,128)(2,1)S(1)}, u32[]{:S(2)}, u32[]{:S(2)}) async-start(bf16[32,2,512]{2,1,0:T(2,128)(2,1)} %reshape.204), calls=%async_computation | async-start | bytes 131072 | tf_op jit(solution)/shard_map/all_to_all | solution.py:248
  11.6 0.7 fusion.25
  12.3 0.1 eq.71
  12.4 0.1 copy.24
  12.5 0.8 broadcast_in_dim.110
  13.3 0.8 broadcast_in_dim.116
  14.1 0.8 dynamic_slice.7
  14.8 0.7 reshape.207
  15.6 0.2 reduce_window_sum.11
  15.8 0.1 copy.25
  15.8 0.1 copy.26
  16.1 0.1 copy.27
  16.1 0.1 sub.58
  16.3 0.7 select_reduce_fusion.3
  17.0 0.1 copy.29
  17.1 0.1 reshape.203
  17.2 0.1 broadcast_in_dim.122
  17.3 0.8 reshape_reshape.13.bound_ref
  18.0 0.1 broadcast_in_dim.121
  18.1 0.8 reshape_reshape.12.group_ref
  18.9 0.1 iota_compare_fusion.3
  18.9 0.8 fusion.22
  19.8 0.6 fusion.30
  20.4 0.7 convert_reduce_fusion.1
  21.1 0.7 reshape_reshape.9.query_ref
  21.8 22.4 %shard_map.140 = (f32[256,128]{1,0:T(8,128)}, f32[256,1]{1,0:T(8,128)}) custom-call(s32[2]{0:T(128)} %prompt_ref.1, s32[2]{0:T(128)} %get-tuple-element.9.low_ref, s32[2]{0:T(128)} %get-tuple-element.8.has_ref, bf16[256,128]{1,0:T(8,128)(2,1)} %reshape_reshape.9.query_ref, bf16[2,6144,128]{2,1,0:T(8,128)(2,1)} %key_ref.1, bf16[2,6144,128]{2,1,0:T(8,128)(2,1)} %value_ref.1, ...), custom_call_target="tpu_custom_call" | custom-call | flops 1610612736 | bytes 6488064 | tf_op jit(solution)/shard_map/pallas_call | solution.py:154
  44.2 1.0 concatenate.8
  45.2 1.0 reduce.4
  46.2 0.1 concatenate.9
  46.4 0.7 pad_maximum_fusion
  47.1 7.8 %all-to-all-start.1 = ((f32[32,2,516]{2,1,0:T(2,128)}), f32[32,2,516]{2,1,0:T(2,128)S(1)}, u32[]{:S(2)}, u32[]{:S(2)}) async-start(f32[32,2,516]{2,1,0:T(2,128)} %pad_maximum_fusion), calls=%async_computation.1 | async-start | bytes 327680 | tf_op jit(solution)/shard_map/all_to_all | solution.py:255
  55.0 0.2 fusion.7
  55.2 6.6 %all-to-all-done.1 = f32[32,2,516]{2,1,0:T(2,128)S(1)} async-done(((f32[32,2,516]{2,1,0:T(2,128)}), f32[32,2,516]{2,1,0:T(2,128)S(1)}, u32[]{:S(2)}, u32[]{:S(2)}) %all-to-all-start.1) | async-done | bytes 132128 | tf_op jit(solution)/shard_map/all_to_all | solution.py:255
  61.8 0.1 reshape.205
  61.9 0.6 gather_fusion
  62.7 0.4 fusion.4
  63.1 2.9 %fusion.9 = f32[24,4096]{1,0:T(8,128)S(1)} fusion(bf16[512,4096]{1,0:T(8,128)(2,1)} %param.23, bf16[3,8,4,128]{3,2,1,0:T(4,128)(2,1)S(1)} %bitcast.26), kind=kOutput, calls=%fused_computation.19 | convolution fusion | flops 100663296 | bytes 4612096 | tf_op jit(solution)/shard_map/dot_general | solution.py:305
  66.0 23.3 %all_to_all.20 = f32[24,8,512]{2,0,1:T(8,128)S(1)} all-to-all(f32[24,8,512]{2,0,1:T(8,128)S(1)} %bitcast.23), channel_id=1, replica_groups=mesh['req'=32,'tp'=8] {'tp'}, dimensions={1} | all-to-all | bytes 786432 | tf_op jit(solution)/shard_map/all_to_all | solution.py:308
  89.3 0.8 broadcast_in_dim.127
  90.1 3.5 %all-to-all-start.3 = ((f32[24,8,512]{2,0,1:T(8,128)}), f32[24,8,512]{2,0,1:T(8,128)S(1)}, u32[]{:S(2)}, u32[]{:S(2)}) async-start(f32[24,8,512]{2,0,1:T(8,128)} %broadcast_in_dim.127), calls=%async_computation.3 | async-start | bytes 786432 | tf_op jit(solution)/shard_map/all_to_all | solution.py:313
  93.6 13.9 %all-to-all-done.3 = f32[24,8,512]{2,0,1:T(8,128)S(1)} async-done(((f32[24,8,512]{2,0,1:T(8,128)}), f32[24,8,512]{2,0,1:T(8,128)S(1)}, u32[]{:S(2)}, u32[]{:S(2)}) %all-to-all-start.3) | async-done | bytes 393248 | tf_op jit(solution)/shard_map/all_to_all | solution.py:313
  107.5 0.2 multiply_reduce_fusion
  107.7 0.8 multiply_convert_fusion
  (31 shorter events, 0.4 us)
Async XLA Ops:
  0.6 19.2 %copy-start = (bf16[24,128,128]{2,1,0:T(8,128)(2,1)S(1)}, bf16[24,128,128]{2,1,0:T(8,128)(2,1)}, u32[]{:S(2)}) copy-start(bf16[24,128,128]{2,1,0:T(8,128)(2,1)} %param.18) | copy-start | bytes 2359300
  4.0 17.1 %all-to-all-start = ((bf16[32,2,512]{2,1,0:T(2,128)(2,1)}), bf16[32,2,512]{2,1,0:T(2,128)(2,1)S(1)}, u32[]{:S(2)}, u32[]{:S(2)}) async-start(bf16[32,2,512]{2,1,0:T(2,128)(2,1)} %reshape.204), calls=%async_computation | async-start | bytes 131072 | tf_op jit(solution)/shard_map/all_to_all | solution.py:248
  19.8 35.2 %copy-start.3 = (bf16[24,128]{1,0:T(8,128)(2,1)S(1)}, bf16[24,128]{1,0:T(8,128)(2,1)}, u32[]{:S(2)}) copy-start(bf16[24,128]{1,0:T(8,128)(2,1)} %param.15) | copy-start | bytes 18436
  21.8 40.9 %copy-start.4 = (bf16[24,128,128]{2,1,0:T(8,128)(2,1)S(1)}, bf16[24,128,128]{2,1,0:T(8,128)(2,1)}, u32[]{:S(2)}) copy-start(bf16[24,128,128]{2,1,0:T(8,128)(2,1)} %param.19) | copy-start | bytes 2359300
  47.1 14.7 %all-to-all-start.1 = ((f32[32,2,516]{2,1,0:T(2,128)}), f32[32,2,516]{2,1,0:T(2,128)S(1)}, u32[]{:S(2)}, u32[]{:S(2)}) async-start(f32[32,2,516]{2,1,0:T(2,128)} %pad_maximum_fusion), calls=%async_computation.1 | async-start | bytes 327680 | tf_op jit(solution)/shard_map/all_to_all | solution.py:255
  63.0 30.5 %copy-start.2 = (bf16[4096]{0:T(1024)(128)(2,1)S(1)}, bf16[4096]{0:T(1024)(128)(2,1)}, u32[]{:S(2)}) copy-start(bf16[4096]{0:T(1024)(128)(2,1)} %param.25) | copy-start | bytes 24580
  63.1 44.4 %copy-start.1 = (bf16[24,4096]{1,0:T(8,128)(2,1)S(1)}, bf16[24,4096]{1,0:T(8,128)(2,1)}, u32[]{:S(2)}) copy-start(bf16[24,4096]{1,0:T(8,128)(2,1)} %param.24) | copy-start | bytes 589828
  90.1 17.4 %all-to-all-start.3 = ((f32[24,8,512]{2,0,1:T(8,128)}), f32[24,8,512]{2,0,1:T(8,128)S(1)}, u32[]{:S(2)}, u32[]{:S(2)}) async-start(f32[24,8,512]{2,0,1:T(8,128)} %broadcast_in_dim.127), calls=%async_computation.3 | async-start | bytes 786432 | tf_op jit(solution)/shard_map/all_to_all | solution.py:313

commit v5 on v4

--- a/solution.py
+++ b/solution.py
@@ -306,9 +306,10 @@
     lanes = lax.axis_size("tp")
     width = partial_value.shape[1] // lanes
     pieces = lax.all_to_all(
-        lax.optimization_barrier(partial_value).reshape(req_dev, lanes, width), "tp", 1, 1, tiled=True
-    )
-    owned_sum = jnp.sum(pieces, axis=1, keepdims=True)
+        lax.optimization_barrier(partial_value).astype(jnp.bfloat16).reshape(req_dev, lanes, width),
+        "tp", 1, 1, tiled=True,
+    )
+    owned_sum = jnp.sum(pieces.astype(jnp.float32), axis=1, keepdims=True)
     spread = jnp.broadcast_to(owned_sum, (req_dev, lanes, width))
     gathered = lax.all_to_all(spread, "tp", 1, 1, tiled=True)
     proj = gathered.reshape(req_dev, lanes * width)

time: 109 us -> 103 us (0.945); the launches traced: 108 us -> 101 us
  Pallas kernels: 22.4 us -> 13.9 us
  starting transfers between devices: 18.9 us -> 24.6 us
  blocking collectives: 23.3 us -> 19.1 us
    pallas_call x1, Pallas kernels: 22.4 us -> 13.9 us  [prefix_attend_kernel(): pl.pallas_call(prefix_kernel, grid_spec=pltpu.PrefetchScalarGridSpec(num_...]
    all_to_all x1, starting transfers between devices: 7.83 us -> 13.5 us  [body(): lax.all_to_all(packed.reshape(places, capacity, packed.shape[1]), 'req',...]
    all_to_all x1, blocking collectives: 23.3 us -> 19.1 us  [body(): lax.all_to_all(lax.optimization_barrier(partial_value).astype(jnp.bfloat1...]
  transfers between devices with their start and end apart: 3 -> 3, of which waited for: 2 -> 2; matrix products, arithmetic and copies ran while one was open for 9% -> 10% of each run, Pallas kernels for 0% -> 0%
where the time goes in v5:
time: 103 us; the launch traced here: 101 us
  starting transfers between devices  24.6 us (24%)
  waiting for transfers between devices  20.2 us (20%)
  blocking collectives  19.1 us (19%)
  Pallas kernels  13.9 us (13%)
  local copies, waits for them, and re-layouts  9.49 us (9%)
  other arithmetic  7.35 us (7%)
  matrix products  5.54 us (5%)
    all_to_all x1, blocking collectives, body(): lax.all_to_all(lax.optimization_barrier(partial_value).astype(jnp.bfloat1...  19.1 us
    pallas_call x1, Pallas kernels, prefix_attend_kernel(): pl.pallas_call(prefix_kernel, grid_spec=pltpu.PrefetchScalarGridSpec(num_...  13.9 us
    all_to_all x1, waiting for transfers between devices, body(): gathered = lax.all_to_all(spread, 'tp', 1, 1, tiled=True)  13.6 us
    all_to_all x1, starting transfers between devices, body(): lax.all_to_all(packed.reshape(places, capacity, packed.shape[1]), 'req',...  13.5 us
    all_to_all x1, starting transfers between devices, body(): lax.all_to_all(send_query.reshape(places, capacity, heads_dev * HD), 'req...  7.62 us
    all_to_all x1, waiting for transfers between devices, body(): lax.all_to_all(packed.reshape(places, capacity, packed.shape[1]), 'req',...  6.65 us
    all_to_all x1, starting transfers between devices, body(): gathered = lax.all_to_all(spread, 'tp', 1, 1, tiled=True)  3.45 us
    dot_general x1, matrix products, body(): jnp.dot(attended, o_weight, preferred_element_type=jnp.float32)  2.85 us
  transfers between devices with their start and end apart: 3, of which 2 were waited for; matrix products, arithmetic and copies ran while one was open for 10% of the time, Pallas kernels for 0%

profile of v5, /device:TPU:2, one launch (start us, length us, event | category | flops | bytes accessed | tf_op | source)
XLA Modules:
  0.0 101.0 jit_solution(16155718586460882146)
XLA Ops:
  0.7 0.8 and_select_fusion.1
  1.5 0.2 convert_reduce_fusion.1
  1.7 0.8 compare_select_fusion
  2.4 0.9 convolution_convert_fusion
  3.3 0.7 reshape.204
  4.0 7.6 %all-to-all-start = ((bf16[32,2,512]{2,1,0:T(2,128)(2,1)}), bf16[32,2,512]{2,1,0:T(2,128)(2,1)S(1)}, u32[]{:S(2)}, u32[]{:S(2)}) async-start(bf16[32,2,512]{2,1,0:T(2,128)(2,1)} %reshape.204), calls=%async_computation | async-start | bytes 131072 | tf_op jit(solution)/shard_map/all_to_all | solution.py:248
  11.6 0.7 fusion.25
  12.3 0.1 eq.71
  12.4 0.1 copy.24
  12.5 0.8 broadcast_in_dim.110
  13.3 0.8 broadcast_in_dim.116
  14.1 0.8 dynamic_slice.7
  14.8 0.7 reshape.207
  15.6 0.2 reduce_window_sum.11
  15.8 0.1 copy.25
  15.8 0.1 copy.26
  16.1 0.1 copy.27
  16.1 0.1 sub.58
  16.3 0.7 select_reduce_fusion.3
  17.0 0.1 copy.29
  17.1 0.1 reshape.203
  17.2 0.1 broadcast_in_dim.122
  17.3 0.8 reshape_reshape.13.bound_ref
  18.0 0.1 broadcast_in_dim.121
  18.1 0.8 reshape_reshape.12.group_ref
  18.9 0.1 iota_compare_fusion.3
  18.9 0.8 fusion.22
  19.8 0.6 fusion.30
  20.4 0.7 convert_reduce_fusion.2
  21.1 0.7 reshape_reshape.9.query_ref
  21.8 13.9 %shard_map.140 = (f32[256,128]{1,0:T(8,128)}, f32[256,1]{1,0:T(8,128)}) custom-call(s32[2]{0:T(128)} %prompt_ref.1, s32[2]{0:T(128)} %get-tuple-element.9.low_ref, s32[2]{0:T(128)} %get-tuple-element.8.has_ref, bf16[256,128]{1,0:T(8,128)(2,1)} %reshape_reshape.9.query_ref, bf16[2,6144,128]{2,1,0:T(8,128)(2,1)} %key_ref.1, bf16[2,6144,128]{2,1,0:T(8,128)(2,1)} %value_ref.1, ...), custom_call_target="tpu_custom_call" | custom-call | flops 1610612736 | bytes 6488064 | tf_op jit(solution)/shard_map/pallas_call | solution.py:154
  35.7 1.0 concatenate.8
  36.6 1.0 reduce.4
  37.6 0.1 concatenate.9
  37.8 0.7 pad_maximum_fusion
  38.5 13.5 %all-to-all-start.1 = ((f32[32,2,516]{2,1,0:T(2,128)}), f32[32,2,516]{2,1,0:T(2,128)S(1)}, u32[]{:S(2)}, u32[]{:S(2)}) async-start(f32[32,2,516]{2,1,0:T(2,128)} %pad_maximum_fusion), calls=%async_computation.1 | async-start | bytes 327680 | tf_op jit(solution)/shard_map/all_to_all | solution.py:255
  52.1 0.2 fusion.7
  52.2 6.6 %all-to-all-done.1 = f32[32,2,516]{2,1,0:T(2,128)S(1)} async-done(((f32[32,2,516]{2,1,0:T(2,128)}), f32[32,2,516]{2,1,0:T(2,128)S(1)}, u32[]{:S(2)}, u32[]{:S(2)}) %all-to-all-start.1) | async-done | bytes 132128 | tf_op jit(solution)/shard_map/all_to_all | solution.py:255
  58.9 0.1 reshape.205
  59.0 0.6 gather_fusion
  59.8 0.4 fusion.4
  60.2 2.9 %fusion.9 = bf16[24,4096]{1,0:T(8,128)(2,1)S(1)} fusion(bf16[512,4096]{1,0:T(8,128)(2,1)} %param.23, bf16[3,8,4,128]{3,2,1,0:T(4,128)(2,1)S(1)} %bitcast.26), kind=kOutput, calls=%fused_computation.20 | convolution fusion | flops 100663296 | bytes 4415488 | tf_op jit(solution)/shard_map/dot_general | solution.py:305
  63.0 19.1 %all_to_all.20 = bf16[24,8,512]{2,0,1:T(8,128)(2,1)S(1)} all-to-all(bf16[24,8,512]{2,0,1:T(8,128)(2,1)S(1)} %bitcast.23), channel_id=1, replica_groups=mesh['req'=32,'tp'=8] {'tp'}, dimensions={1} | all-to-all | bytes 393216 | tf_op jit(solution)/shard_map/all_to_all | solution.py:308
  82.1 0.8 broadcast_in_dim.127
  82.9 3.5 %all-to-all-start.3 = ((f32[24,8,512]{2,0,1:T(8,128)}), f32[24,8,512]{2,0,1:T(8,128)S(1)}, u32[]{:S(2)}, u32[]{:S(2)}) async-start(f32[24,8,512]{2,0,1:T(8,128)} %broadcast_in_dim.127), calls=%async_computation.3 | async-start | bytes 786432 | tf_op jit(solution)/shard_map/all_to_all | solution.py:314
  86.4 13.6 %all-to-all-done.3 = f32[24,8,512]{2,0,1:T(8,128)S(1)} async-done(((f32[24,8,512]{2,0,1:T(8,128)}), f32[24,8,512]{2,0,1:T(8,128)S(1)}, u32[]{:S(2)}, u32[]{:S(2)}) %all-to-all-start.3) | async-done | bytes 393248 | tf_op jit(solution)/shard_map/all_to_all | solution.py:314
  100.0 0.2 multiply_reduce_fusion
  100.2 0.8 multiply_convert_fusion
  (31 shorter events, 0.4 us)
Async XLA Ops:
  0.6 19.2 %copy-start = (bf16[24,128,128]{2,1,0:T(8,128)(2,1)S(1)}, bf16[24,128,128]{2,1,0:T(8,128)(2,1)}, u32[]{:S(2)}) copy-start(bf16[24,128,128]{2,1,0:T(8,128)(2,1)} %param.18) | copy-start | bytes 2359300
  4.0 17.1 %all-to-all-start = ((bf16[32,2,512]{2,1,0:T(2,128)(2,1)}), bf16[32,2,512]{2,1,0:T(2,128)(2,1)S(1)}, u32[]{:S(2)}, u32[]{:S(2)}) async-start(bf16[32,2,512]{2,1,0:T(2,128)(2,1)} %reshape.204), calls=%async_computation | async-start | bytes 131072 | tf_op jit(solution)/shard_map/all_to_all | solution.py:248
  19.8 32.3 %copy-start.3 = (bf16[24,128]{1,0:T(8,128)(2,1)S(1)}, bf16[24,128]{1,0:T(8,128)(2,1)}, u32[]{:S(2)}) copy-start(bf16[24,128]{1,0:T(8,128)(2,1)} %param.15) | copy-start | bytes 18436
  21.8 38.0 %copy-start.4 = (bf16[24,128,128]{2,1,0:T(8,128)(2,1)S(1)}, bf16[24,128,128]{2,1,0:T(8,128)(2,1)}, u32[]{:S(2)}) copy-start(bf16[24,128,128]{2,1,0:T(8,128)(2,1)} %param.19) | copy-start | bytes 2359300
  38.5 20.4 %all-to-all-start.1 = ((f32[32,2,516]{2,1,0:T(2,128)}), f32[32,2,516]{2,1,0:T(2,128)S(1)}, u32[]{:S(2)}, u32[]{:S(2)}) async-start(f32[32,2,516]{2,1,0:T(2,128)} %pad_maximum_fusion), calls=%async_computation.1 | async-start | bytes 327680 | tf_op jit(solution)/shard_map/all_to_all | solution.py:255
  59.6 26.8 %copy-start.2 = (bf16[4096]{0:T(1024)(128)(2,1)S(1)}, bf16[4096]{0:T(1024)(128)(2,1)}, u32[]{:S(2)}) copy-start(bf16[4096]{0:T(1024)(128)(2,1)} %param.25) | copy-start | bytes 24580
  59.8 40.2 %copy-start.1 = (bf16[24,4096]{1,0:T(8,128)(2,1)S(1)}, bf16[24,4096]{1,0:T(8,128)(2,1)}, u32[]{:S(2)}) copy-start(bf16[24,4096]{1,0:T(8,128)(2,1)} %param.24) | copy-start | bytes 589828
  82.9 17.0 %all-to-all-start.3 = ((f32[24,8,512]{2,0,1:T(8,128)}), f32[24,8,512]{2,0,1:T(8,128)S(1)}, u32[]{:S(2)}, u32[]{:S(2)}) async-start(f32[24,8,512]{2,0,1:T(8,128)} %broadcast_in_dim.127), calls=%async_computation.3 | async-start | bytes 786432 | tf_op jit(solution)/shard_map/all_to_all | solution.py:314

commit v6 on v5

--- a/solution.py
+++ b/solution.py
@@ -185,6 +185,153 @@
     return out.reshape(row_count, heads_dev * HD), log.reshape(row_count, heads_dev)
 
 
+TILE_SLOTS = 8
+KEY_BLOCK = 512
+
+
+def sorted_prefix_kernel(
+    meta_ref, query_ref, key_ref, value_ref, group_ref, bound_ref,
+    out_ref, log_ref, running, weight_sum, weighted,
+):
+    groups_dev = key_ref.shape[0]
+    rows = query_ref.shape[0]
+    tiles = (meta_ref.shape[0] - 4 * groups_dev) // groups_dev
+    tile_rows = rows // tiles
+    running[...] = jnp.full(running.shape, FAR_BELOW, jnp.float32)
+    weight_sum[...] = jnp.zeros(weight_sum.shape, jnp.float32)
+    weighted[...] = jnp.zeros(weighted.shape, jnp.float32)
+    for g in range(groups_dev):
+        prompt_count = meta_ref[g]
+
+        def tile_body(t, carry, g=g, prompt_count=prompt_count):
+            r0 = pl.multiple_of(t * tile_rows, tile_rows)
+            q = query_ref[pl.ds(r0, tile_rows), :]
+            grp = group_ref[pl.ds(r0, tile_rows), :]
+            bnd = bound_ref[pl.ds(r0, tile_rows), :]
+
+            def block(j, state):
+                old, total, acc = state
+                k0 = pl.multiple_of(j * KEY_BLOCK, KEY_BLOCK)
+                kb = key_ref[g, pl.ds(k0, KEY_BLOCK), :]
+                vb = value_ref[g, pl.ds(k0, KEY_BLOCK), :]
+                scores = lax.dot_general(
+                    q, kb, (((1,), (1,)), ((), ())), preferred_element_type=jnp.float32
+                ) * (1.0 / math.sqrt(HD))
+                positions = k0 + lax.broadcasted_iota(jnp.int32, scores.shape, 1)
+                usable = (
+                    (grp == g)
+                    & (positions < prompt_count)
+                    & ((positions < SINKS) | (positions >= bnd))
+                )
+                masked = jnp.where(usable, scores, FAR_BELOW)
+                updated = jnp.maximum(old, jnp.max(masked, axis=1, keepdims=True))
+                weights = jnp.where(usable, jnp.exp(masked - updated), 0.0)
+                rescale = jnp.exp(old - updated)
+                total = total * rescale + jnp.sum(weights, axis=1, keepdims=True)
+                acc = acc * rescale + jnp.dot(
+                    weights.astype(jnp.bfloat16), vb, preferred_element_type=jnp.float32
+                )
+                return (updated, total, acc)
+
+            state = (
+                running[pl.ds(r0, tile_rows), :],
+                weight_sum[pl.ds(r0, tile_rows), :],
+                weighted[pl.ds(r0, tile_rows), :],
+            )
+            state = block(0, state)
+            first = meta_ref[4 * groups_dev + g * tiles + t]
+            state = lax.fori_loop(first, meta_ref[3 * groups_dev + g], block, state)
+            running[pl.ds(r0, tile_rows), :] = state[0]
+            weight_sum[pl.ds(r0, tile_rows), :] = state[1]
+            weighted[pl.ds(r0, tile_rows), :] = state[2]
+            return carry
+
+        lax.fori_loop(meta_ref[groups_dev + g], meta_ref[2 * groups_dev + g], tile_body, 0)
+    bounded = jnp.maximum(weight_sum[...], 1.0)
+    out_ref[...] = weighted[...] / bounded
+    log_ref[...] = running[...] + jnp.log(bounded)
+
+
+def prefix_attend_sorted(
+    rows_query, row_group, row_suffix, prefix_key, prefix_value, prompt_len, first_group
+):
+    slots = rows_query.shape[0]
+    groups_dev, prompt_max, _ = prefix_key.shape
+    heads_dev = rows_query.shape[1] // HD
+    tiles = slots // TILE_SLOTS
+    blocks = prompt_max // KEY_BLOCK
+    local_group = row_group - first_group
+    owned = (local_group >= 0) & (local_group < groups_dev)
+    sort_key = jnp.where(owned, local_group, groups_dev)
+    member = sort_key[:, None] == jnp.arange(groups_dev, dtype=jnp.int32)[None, :]
+    row_prompt = jnp.sum(jnp.where(member, prompt_len[None, :], 0), axis=1)
+    row_low = row_prompt + row_suffix - WIN + 1
+    index = jnp.arange(slots, dtype=jnp.int32)
+    before = (sort_key[None, :] < sort_key[:, None]) | (
+        (sort_key[None, :] == sort_key[:, None]) & (index[None, :] < index[:, None])
+    )
+    rank = jnp.sum(before.astype(jnp.int32), axis=1)
+    order = jnp.sum(jnp.where(rank[None, :] == index[:, None], index[None, :], 0), axis=1)
+    sorted_key = sort_key[order]
+    sorted_low = row_low[order]
+    counts = jnp.sum(member.astype(jnp.int32), axis=0)
+    starts = jnp.cumsum(counts) - counts
+    tile_lo = starts // TILE_SLOTS
+    tile_hi = jnp.where(counts > 0, (starts + counts + TILE_SLOTS - 1) // TILE_SLOTS, tile_lo)
+    block_hi = (prompt_len + KEY_BLOCK - 1) // KEY_BLOCK
+    in_group = sorted_key.reshape(1, tiles, TILE_SLOTS) == jnp.arange(groups_dev, dtype=jnp.int32)[
+        :, None, None
+    ]
+    tile_low = jnp.min(
+        jnp.where(in_group, sorted_low.reshape(1, tiles, TILE_SLOTS), prompt_max), axis=2
+    )
+    tile_first = jnp.clip(jnp.floor_divide(tile_low, KEY_BLOCK), 1, blocks)
+    meta = jnp.concatenate(
+        [prompt_len, tile_lo, tile_hi, block_hi, tile_first.reshape(-1)]
+    ).astype(jnp.int32)
+    rows = slots * heads_dev
+    flat_query = rows_query[order].reshape(rows, HD)
+    flat_group = jnp.repeat(jnp.where(sorted_key < groups_dev, sorted_key, -1), heads_dev).reshape(
+        rows, 1
+    ).astype(jnp.int32)
+    flat_bound = jnp.repeat(sorted_low, heads_dev).reshape(rows, 1).astype(jnp.int32)
+    whole2 = lambda i, *_: (0, 0)
+    whole3 = lambda i, *_: (0, 0, 0)
+    out, log = pl.pallas_call(
+        sorted_prefix_kernel,
+        grid_spec=pltpu.PrefetchScalarGridSpec(
+            num_scalar_prefetch=1,
+            grid=(1,),
+            in_specs=[
+                pl.BlockSpec((rows, HD), whole2),
+                pl.BlockSpec(prefix_key.shape, whole3),
+                pl.BlockSpec(prefix_value.shape, whole3),
+                pl.BlockSpec((rows, 1), whole2),
+                pl.BlockSpec((rows, 1), whole2),
+            ],
+            out_specs=[pl.BlockSpec((rows, HD), whole2), pl.BlockSpec((rows, 1), whole2)],
+            scratch_shapes=[
+                pltpu.VMEM((rows, 1), jnp.float32),
+                pltpu.VMEM((rows, 1), jnp.float32),
+                pltpu.VMEM((rows, HD), jnp.float32),
+            ],
+        ),
+        out_shape=[
+            jax.ShapeDtypeStruct((rows, HD), jnp.float32),
+            jax.ShapeDtypeStruct((rows, 1), jnp.float32),
+        ],
+        compiler_params=pltpu.CompilerParams(vmem_limit_bytes=48 * 1024 * 1024),
+        cost_estimate=pl.CostEstimate(
+            flops=2 * rows * prompt_max * HD,
+            transcendentals=rows * prompt_max // 2,
+            bytes_accessed=2 * prefix_key.size * 2 + rows * HD * 6,
+        ),
+    )(meta, flat_query, prefix_key, prefix_value, flat_group, flat_bound)
+    out = out.reshape(slots, heads_dev * HD)[rank]
+    log = log.reshape(slots, heads_dev)[rank]
+    return out, log
+
+
 def body(
     query,
     new_key,
@@ -248,7 +395,7 @@
     compact = lax.all_to_all(
         send_query.reshape(places, capacity, heads_dev * HD), "req", 0, 0, tiled=True
     ).reshape(slot_total, heads_dev * HD)
-    part_out, part_log = prefix_attend_kernel(
+    part_out, part_log = prefix_attend_sorted(
         compact, slot_group, slot_suffix, prefix_key, prefix_value, prompt_len, first_group
     )
     packed = jnp.concatenate([part_out, part_log], axis=1)

time: 103 us -> 128 us (1.24); the launches traced: 101 us -> 128 us
  starting transfers between devices: 24.6 us -> 59.3 us
  Pallas kernels: 13.9 us -> 2.56 us
  local copies, waits for them, and re-layouts: 9.49 us -> 13.8 us
    all_to_all x1, starting transfers between devices: 13.5 us -> 48.2 us  [body(): lax.all_to_all(packed.reshape(places, capacity, packed.shape[1]), 'req',...]
    pallas_call x1, Pallas kernels: 13.9 us -> 2.56 us  [prefix_attend_sorted(): pl.pallas_call(sorted_prefix_kernel, grid_spec=pltpu.PrefetchScalarGridSp...]
    gather x0 -> x5, local copies, waits for them, and re-layouts: none -> 3.51 us  [the longest x1 0.78 us: prefix_attend_sorted(): sorted_key = sort_key[order]]
    another operation x4 -> x3, local copies, waits for them, and re-layouts: 2.92 us -> 0.93 us  [the longest x1 0.76 us: prefix_attend_kernel(): jnp.repeat(row_low, heads_dev).reshape(rows, 1).astype(jnp.int32)]
    unnamed x10 -> x12, local copies, waits for them, and re-layouts: 0.03 us -> 1.92 us
  transfers between devices with their start and end apart: 3 -> 3, of which waited for: 2 -> 2; matrix products, arithmetic and copies ran while one was open for 10% -> 9% of each run, Pallas kernels for 0% -> 0%
where the time goes in v6:
time: 128 us
  starting transfers between devices  59.3 us (46%)
  waiting for transfers between devices  20.2 us (16%)
  blocking collectives  19.1 us (15%)
  local copies, waits for them, and re-layouts  13.8 us (11%)
  other arithmetic  6.4 us (5%)
  matrix products  5.54 us (4%)
  Pallas kernels  2.56 us (2%)
    all_to_all x1, starting transfers between devices, body(): lax.all_to_all(packed.reshape(places, capacity, packed.shape[1]), 'req',...  48.2 us
    all_to_all x1, blocking collectives, body(): lax.all_to_all(lax.optimization_barrier(partial_value).astype(jnp.bfloat1...  19.1 us
    all_to_all x1, waiting for transfers between devices, body(): gathered = lax.all_to_all(spread, 'tp', 1, 1, tiled=True)  13.6 us
    all_to_all x1, starting transfers between devices, body(): lax.all_to_all(send_query.reshape(places, capacity, heads_dev * HD), 'req...  7.62 us
    all_to_all x1, waiting for transfers between devices, body(): lax.all_to_all(packed.reshape(places, capacity, packed.shape[1]), 'req',...  6.65 us
    all_to_all x1, starting transfers between devices, body(): gathered = lax.all_to_all(spread, 'tp', 1, 1, tiled=True)  3.45 us
    dot_general x1, matrix products, body(): jnp.dot(attended, o_weight, preferred_element_type=jnp.float32)  2.86 us
    pallas_call x1, Pallas kernels, prefix_attend_sorted(): pl.pallas_call(sorted_prefix_kernel, grid_spec=pltpu.PrefetchScalarGridSp...  2.56 us
  transfers between devices with their start and end apart: 3, of which 2 were waited for; matrix products, arithmetic and copies ran while one was open for 9% of the time, Pallas kernels for 0%

profile of v6, /device:TPU:2, one launch (start us, length us, event | category | flops | bytes accessed | tf_op | source)
XLA Modules:
  0.0 127.8 jit_solution(17468367300307561125)
XLA Ops:
  0.7 0.8 and_select_fusion
  1.5 0.2 convert_reduce_fusion.2
  1.7 0.8 compare_select_fusion
  2.4 0.9 convolution_convert_fusion
  3.3 0.7 reshape.283
  4.0 7.6 %all-to-all-start = ((bf16[32,2,512]{2,1,0:T(2,128)(2,1)}), bf16[32,2,512]{2,1,0:T(2,128)(2,1)S(1)}, u32[]{:S(2)}, u32[]{:S(2)}) async-start(bf16[32,2,512]{2,1,0:T(2,128)(2,1)} %reshape.283), calls=%async_computation | async-start | bytes 131072 | tf_op jit(solution)/shard_map/all_to_all | solution.py:395
  11.6 0.7 fusion.27
  12.3 0.1 eq.106
  12.5 0.8 broadcast_in_dim.137
  13.3 0.2 reduce_window_sum.18
  13.6 0.8 broadcast_in_dim.144
  14.6 0.1 sub.87
  14.8 0.2 convert_reduce_fusion.1
  14.9 0.9 select_reduce_fusion.4
  15.8 0.7 and_select_fusion.2
  16.5 0.1 select_reduce_fusion
  16.6 0.8 gather_fusion
  17.5 0.8 dynamic_slice.7
  18.2 0.7 reshape.291
  19.1 0.1 reshape.282
  19.2 0.8 gather_fusion.1
  20.0 0.1 select_reduce_fusion.3
  20.3 0.2 reduce-window.9
  20.7 0.1 reshape_reshape.8.group_ref
  20.9 0.8 fusion.24
  21.7 0.6 fusion.35
  22.3 0.7 concatenate.6.meta_ref
  23.1 0.7 gather_fusion.2
  23.9 1.9 %copy-done.1 = bf16[2,6144,128]{2,1,0:T(8,128)(2,1)S(1)} copy-done((bf16[2,6144,128]{2,1,0:T(8,128)(2,1)S(1)}, bf16[2,6144,128]{2,1,0:T(8,128)(2,1)}, u32[]{:S(2)}) %copy-start.1) | copy-done | bytes 3145752
  25.8 2.6 %shard_map.140 = (f32[256,128]{1,0:T(8,128)S(1)}, f32[256,1]{1,0:T(8,128)S(1)}) custom-call(s32[24]{0:T(128)S(1)} %concatenate.6.meta_ref, bf16[256,128]{1,0:T(8,128)(2,1)S(1)} %reshape.285.query_ref, bf16[2,6144,128]{2,1,0:T(8,128)(2,1)S(1)} %copy-done.1, bf16[2,6144,128]{2,1,0:T(8,128)(2,1)} %value_ref.1, s32[256,1]{1,0:T(8,128)S(1)} %reshape_reshape.8.group_ref, ...), custom_call_target="tpu_custom_call" | custom-call | flops 402653184 | bytes 6488064 | tf_op jit(solution)/shard_map/pallas_call | solution.py:300
  28.4 0.1 reduce.4
  28.5 0.1 reshape.287
  28.6 0.7 gather_fusion.3
  29.3 0.6 gather_fusion.4
  29.9 0.8 reshape.288
  30.6 48.2 %all-to-all-start.1 = ((f32[32,2,516]{2,1,0:T(2,128)}), f32[32,2,516]{2,1,0:T(2,128)S(1)}, u32[]{:S(2)}, u32[]{:S(2)}) async-start(f32[32,2,516]{2,1,0:T(2,128)} %reshape.288), calls=%async_computation.1 | async-start | bytes 327680 | tf_op jit(solution)/shard_map/all_to_all | solution.py:402
  78.9 0.2 fusion.9
  79.1 6.6 %all-to-all-done.1 = f32[32,2,516]{2,1,0:T(2,128)S(1)} async-done(((f32[32,2,516]{2,1,0:T(2,128)}), f32[32,2,516]{2,1,0:T(2,128)S(1)}, u32[]{:S(2)}, u32[]{:S(2)}) %all-to-all-start.1) | async-done | bytes 132128 | tf_op jit(solution)/shard_map/all_to_all | solution.py:402
  85.7 0.1 reshape.289
  85.8 0.6 gather_fusion.5
  86.6 0.4 fusion.4
  87.0 2.9 %fusion.11 = bf16[24,4096]{1,0:T(8,128)(2,1)S(1)} fusion(bf16[512,4096]{1,0:T(8,128)(2,1)} %param.23, bf16[3,8,4,128]{3,2,1,0:T(4,128)(2,1)S(1)} %bitcast.43), kind=kOutput, calls=%fused_computation.31 | convolution fusion | flops 100663296 | bytes 4415488 | tf_op jit(solution)/shard_map/dot_general | solution.py:452
  89.8 19.1 %all_to_all.20 = bf16[24,8,512]{2,0,1:T(8,128)(2,1)S(1)} all-to-all(bf16[24,8,512]{2,0,1:T(8,128)(2,1)S(1)} %bitcast.40), channel_id=1, replica_groups=mesh['req'=32,'tp'=8] {'tp'}, dimensions={1} | all-to-all | bytes 393216 | tf_op jit(solution)/shard_map/all_to_all | solution.py:455
  108.9 0.8 broadcast_in_dim.156
  109.7 3.5 %all-to-all-start.3 = ((f32[24,8,512]{2,0,1:T(8,128)}), f32[24,8,512]{2,0,1:T(8,128)S(1)}, u32[]{:S(2)}, u32[]{:S(2)}) async-start(f32[24,8,512]{2,0,1:T(8,128)} %broadcast_in_dim.156), calls=%async_computation.3 | async-start | bytes 786432 | tf_op jit(solution)/shard_map/all_to_all | solution.py:461
  113.2 13.6 %all-to-all-done.3 = f32[24,8,512]{2,0,1:T(8,128)S(1)} async-done(((f32[24,8,512]{2,0,1:T(8,128)}), f32[24,8,512]{2,0,1:T(8,128)S(1)}, u32[]{:S(2)}, u32[]{:S(2)}) %all-to-all-start.3) | async-done | bytes 393248 | tf_op jit(solution)/shard_map/all_to_all | solution.py:461
  126.8 0.2 multiply_reduce_fusion
  127.0 0.8 multiply_convert_fusion
  (55 shorter events, 1.5 us)
Async XLA Ops:
  0.6 21.1 %copy-start = (bf16[24,128,128]{2,1,0:T(8,128)(2,1)S(1)}, bf16[24,128,128]{2,1,0:T(8,128)(2,1)}, u32[]{:S(2)}) copy-start(bf16[24,128,128]{2,1,0:T(8,128)(2,1)} %param.18) | copy-start | bytes 2359300
  4.0 19.1 %all-to-all-start = ((bf16[32,2,512]{2,1,0:T(2,128)(2,1)}), bf16[32,2,512]{2,1,0:T(2,128)(2,1)S(1)}, u32[]{:S(2)}, u32[]{:S(2)}) async-start(bf16[32,2,512]{2,1,0:T(2,128)(2,1)} %reshape.283), calls=%async_computation | async-start | bytes 131072 | tf_op jit(solution)/shard_map/all_to_all | solution.py:395
  23.9 1.9 %copy-start.1 = (bf16[2,6144,128]{2,1,0:T(8,128)(2,1)S(1)}, bf16[2,6144,128]{2,1,0:T(8,128)(2,1)}, u32[]{:S(2)}) copy-start(bf16[2,6144,128]{2,1,0:T(8,128)(2,1)} %key_ref.1) | copy-start | bytes 9437188
  25.8 53.1 %copy-start.4 = (bf16[24,128]{1,0:T(8,128)(2,1)S(1)}, bf16[24,128]{1,0:T(8,128)(2,1)}, u32[]{:S(2)}) copy-start(bf16[24,128]{1,0:T(8,128)(2,1)} %param.15) | copy-start | bytes 18436
  25.8 60.8 %copy-start.5 = (bf16[24,128,128]{2,1,0:T(8,128)(2,1)S(1)}, bf16[24,128,128]{2,1,0:T(8,128)(2,1)}, u32[]{:S(2)}) copy-start(bf16[24,128,128]{2,1,0:T(8,128)(2,1)} %param.19) | copy-start | bytes 2359300
  30.6 55.1 %all-to-all-start.1 = ((f32[32,2,516]{2,1,0:T(2,128)}), f32[32,2,516]{2,1,0:T(2,128)S(1)}, u32[]{:S(2)}, u32[]{:S(2)}) async-start(f32[32,2,516]{2,1,0:T(2,128)} %reshape.288), calls=%async_computation.1 | async-start | bytes 327680 | tf_op jit(solution)/shard_map/all_to_all | solution.py:402
  86.4 26.7 %copy-start.3 = (bf16[4096]{0:T(1024)(128)(2,1)S(1)}, bf16[4096]{0:T(1024)(128)(2,1)}, u32[]{:S(2)}) copy-start(bf16[4096]{0:T(1024)(128)(2,1)} %param.25) | copy-start | bytes 24580
  86.6 40.2 %copy-start.2 = (bf16[24,4096]{1,0:T(8,128)(2,1)S(1)}, bf16[24,4096]{1,0:T(8,128)(2,1)}, u32[]{:S(2)}) copy-start(bf16[24,4096]{1,0:T(8,128)(2,1)} %param.24) | copy-start | bytes 589828
  109.7 17.0 %all-to-all-start.3 = ((f32[24,8,512]{2,0,1:T(8,128)}), f32[24,8,512]{2,0,1:T(8,128)S(1)}, u32[]{:S(2)}, u32[]{:S(2)}) async-start(f32[24,8,512]{2,0,1:T(8,128)} %broadcast_in_dim.156), calls=%async_computation.3 | async-start | bytes 786432 | tf_op jit(solution)/shard_map/all_to_all | solution.py:461

commit v7 on v6

--- a/solution.py
+++ b/solution.py
@@ -185,8 +185,8 @@
     return out.reshape(row_count, heads_dev * HD), log.reshape(row_count, heads_dev)
 
 
-TILE_SLOTS = 8
-KEY_BLOCK = 512
+TILE_SLOTS = 16
+KEY_BLOCK = 1024
 
 
 def sorted_prefix_kernel(

time: 128 us -> 100 us (0.78)
  starting transfers between devices: 59.3 us -> 16.8 us
  Pallas kernels: 2.56 us -> 15.8 us
    all_to_all x1, starting transfers between devices: 48.2 us -> 5.75 us  [body(): lax.all_to_all(packed.reshape(places, capacity, packed.shape[1]), 'req',...]
    pallas_call x1, Pallas kernels: 2.56 us -> 15.8 us  [prefix_attend_sorted(): pl.pallas_call(sorted_prefix_kernel, grid_spec=pltpu.PrefetchScalarGridSp...]
  transfers between devices with their start and end apart: 3 -> 3, of which waited for: 2 -> 2; matrix products, arithmetic and copies ran while one was open for 9% -> 12% of each run, Pallas kernels for 0% -> 0%
where the time goes in v7:
time: 100 us; the launch traced here: 98.7 us
  waiting for transfers between devices  20.3 us (20%)
  blocking collectives  19.1 us (19%)
  starting transfers between devices  16.8 us (17%)
  Pallas kernels  15.8 us (16%)
  local copies, waits for them, and re-layouts  13.8 us (14%)
  other arithmetic  6.4 us (6%)
  matrix products  5.54 us (6%)
  between operations  1 us (1%)
    all_to_all x1, blocking collectives, body(): lax.all_to_all(lax.optimization_barrier(partial_value).astype(jnp.bfloat1...  19.1 us
    pallas_call x1, Pallas kernels, prefix_attend_sorted(): pl.pallas_call(sorted_prefix_kernel, grid_spec=pltpu.PrefetchScalarGridSp...  15.8 us
    all_to_all x1, waiting for transfers between devices, body(): gathered = lax.all_to_all(spread, 'tp', 1, 1, tiled=True)  13.6 us
    all_to_all x1, starting transfers between devices, body(): lax.all_to_all(send_query.reshape(places, capacity, heads_dev * HD), 'req...  7.62 us
    all_to_all x1, waiting for transfers between devices, body(): lax.all_to_all(packed.reshape(places, capacity, packed.shape[1]), 'req',...  6.72 us
    all_to_all x1, starting transfers between devices, body(): lax.all_to_all(packed.reshape(places, capacity, packed.shape[1]), 'req',...  5.75 us
    all_to_all x1, starting transfers between devices, body(): gathered = lax.all_to_all(spread, 'tp', 1, 1, tiled=True)  3.45 us
    dot_general x1, matrix products, body(): jnp.dot(attended, o_weight, preferred_element_type=jnp.float32)  2.86 us
  transfers between devices with their start and end apart: 3, of which 2 were waited for; matrix products, arithmetic and copies ran while one was open for 12% of the time, Pallas kernels for 0%

profile of v7, /device:TPU:2, one launch (start us, length us, event | category | flops | bytes accessed | tf_op | source)
XLA Modules:
  0.0 98.7 jit_solution(2308521380454080361)
XLA Ops:
  0.7 0.8 and_select_fusion
  1.5 0.2 convert_reduce_fusion.2
  1.7 0.8 compare_select_fusion
  2.4 0.9 convolution_convert_fusion
  3.3 0.7 reshape.283
  4.0 7.6 %all-to-all-start = ((bf16[32,2,512]{2,1,0:T(2,128)(2,1)}), bf16[32,2,512]{2,1,0:T(2,128)(2,1)S(1)}, u32[]{:S(2)}, u32[]{:S(2)}) async-start(bf16[32,2,512]{2,1,0:T(2,128)(2,1)} %reshape.283), calls=%async_computation | async-start | bytes 131072 | tf_op jit(solution)/shard_map/all_to_all | solution.py:395
  11.6 0.7 fusion.27
  12.3 0.1 eq.106
  12.5 0.8 broadcast_in_dim.137
  13.3 0.2 reduce_window_sum.18
  13.6 0.8 broadcast_in_dim.144
  14.6 0.1 sub.87
  14.8 0.2 convert_reduce_fusion.1
  14.9 0.9 select_reduce_fusion.4
  15.8 0.7 and_select_fusion.2
  16.5 0.1 select_reduce_fusion
  16.6 0.8 gather_fusion
  17.5 0.8 dynamic_slice.7
  18.2 0.7 reshape.291
  19.1 0.1 reshape.282
  19.2 0.8 gather_fusion.1
  20.0 0.1 select_reduce_fusion.3
  20.3 0.2 reduce-window.9
  20.7 0.1 reshape_reshape.8.group_ref
  20.9 0.8 fusion.24
  21.7 0.6 fusion.35
  22.3 0.7 concatenate.6.meta_ref
  23.1 0.7 gather_fusion.2
  23.9 1.9 %copy-done.1 = bf16[2,6144,128]{2,1,0:T(8,128)(2,1)S(1)} copy-done((bf16[2,6144,128]{2,1,0:T(8,128)(2,1)S(1)}, bf16[2,6144,128]{2,1,0:T(8,128)(2,1)}, u32[]{:S(2)}) %copy-start.1) | copy-done | bytes 3145752
  25.8 15.8 %shard_map.140 = (f32[256,128]{1,0:T(8,128)S(1)}, f32[256,1]{1,0:T(8,128)S(1)}) custom-call(s32[16]{0:T(128)S(1)} %concatenate.6.meta_ref, bf16[256,128]{1,0:T(8,128)(2,1)S(1)} %reshape.285.query_ref, bf16[2,6144,128]{2,1,0:T(8,128)(2,1)S(1)} %copy-done.1, bf16[2,6144,128]{2,1,0:T(8,128)(2,1)} %value_ref.1, s32[256,1]{1,0:T(8,128)S(1)} %reshape_reshape.8.group_ref, ...), custom_call_target="tpu_custom_call" | custom-call | flops 402653184 | bytes 6488064 | tf_op jit(solution)/shard_map/pallas_call | solution.py:300
  41.6 0.1 reduce.4
  41.8 0.1 reshape.287
  41.9 0.7 gather_fusion.3
  42.5 0.6 gather_fusion.4
  43.1 0.8 reshape.288
  43.9 5.7 %all-to-all-start.1 = ((f32[32,2,516]{2,1,0:T(2,128)}), f32[32,2,516]{2,1,0:T(2,128)S(1)}, u32[]{:S(2)}, u32[]{:S(2)}) async-start(f32[32,2,516]{2,1,0:T(2,128)} %reshape.288), calls=%async_computation.1 | async-start | bytes 327680 | tf_op jit(solution)/shard_map/all_to_all | solution.py:402
  49.7 0.2 fusion.9
  49.9 6.7 %all-to-all-done.1 = f32[32,2,516]{2,1,0:T(2,128)S(1)} async-done(((f32[32,2,516]{2,1,0:T(2,128)}), f32[32,2,516]{2,1,0:T(2,128)S(1)}, u32[]{:S(2)}, u32[]{:S(2)}) %all-to-all-start.1) | async-done | bytes 132128 | tf_op jit(solution)/shard_map/all_to_all | solution.py:402
  56.6 0.1 reshape.289
  56.7 0.6 gather_fusion.5
  57.5 0.4 fusion.4
  57.9 2.9 %fusion.11 = bf16[24,4096]{1,0:T(8,128)(2,1)S(1)} fusion(bf16[512,4096]{1,0:T(8,128)(2,1)} %param.23, bf16[3,8,4,128]{3,2,1,0:T(4,128)(2,1)S(1)} %bitcast.43), kind=kOutput, calls=%fused_computation.31 | convolution fusion | flops 100663296 | bytes 4415488 | tf_op jit(solution)/shard_map/dot_general | solution.py:452
  60.7 19.1 %all_to_all.20 = bf16[24,8,512]{2,0,1:T(8,128)(2,1)S(1)} all-to-all(bf16[24,8,512]{2,0,1:T(8,128)(2,1)S(1)} %bitcast.40), channel_id=1, replica_groups=mesh['req'=32,'tp'=8] {'tp'}, dimensions={1} | all-to-all | bytes 393216 | tf_op jit(solution)/shard_map/all_to_all | solution.py:455
  79.8 0.8 broadcast_in_dim.156
  80.6 3.5 %all-to-all-start.3 = ((f32[24,8,512]{2,0,1:T(8,128)}), f32[24,8,512]{2,0,1:T(8,128)S(1)}, u32[]{:S(2)}, u32[]{:S(2)}) async-start(f32[24,8,512]{2,0,1:T(8,128)} %broadcast_in_dim.156), calls=%async_computation.3 | async-start | bytes 786432 | tf_op jit(solution)/shard_map/all_to_all | solution.py:461
  84.1 13.6 %all-to-all-done.3 = f32[24,8,512]{2,0,1:T(8,128)S(1)} async-done(((f32[24,8,512]{2,0,1:T(8,128)}), f32[24,8,512]{2,0,1:T(8,128)S(1)}, u32[]{:S(2)}, u32[]{:S(2)}) %all-to-all-start.3) | async-done | bytes 393248 | tf_op jit(solution)/shard_map/all_to_all | solution.py:461
  97.7 0.2 multiply_reduce_fusion
  97.9 0.8 multiply_convert_fusion
  (55 shorter events, 1.5 us)
Async XLA Ops:
  0.6 21.1 %copy-start = (bf16[24,128,128]{2,1,0:T(8,128)(2,1)S(1)}, bf16[24,128,128]{2,1,0:T(8,128)(2,1)}, u32[]{:S(2)}) copy-start(bf16[24,128,128]{2,1,0:T(8,128)(2,1)} %param.18) | copy-start | bytes 2359300
  4.0 19.1 %all-to-all-start = ((bf16[32,2,512]{2,1,0:T(2,128)(2,1)}), bf16[32,2,512]{2,1,0:T(2,128)(2,1)S(1)}, u32[]{:S(2)}, u32[]{:S(2)}) async-start(bf16[32,2,512]{2,1,0:T(2,128)(2,1)} %reshape.283), calls=%async_computation | async-start | bytes 131072 | tf_op jit(solution)/shard_map/all_to_all | solution.py:395
  23.9 1.9 %copy-start.1 = (bf16[2,6144,128]{2,1,0:T(8,128)(2,1)S(1)}, bf16[2,6144,128]{2,1,0:T(8,128)(2,1)}, u32[]{:S(2)}) copy-start(bf16[2,6144,128]{2,1,0:T(8,128)(2,1)} %key_ref.1) | copy-start | bytes 9437188
  25.8 23.9 %copy-start.4 = (bf16[24,128]{1,0:T(8,128)(2,1)S(1)}, bf16[24,128]{1,0:T(8,128)(2,1)}, u32[]{:S(2)}) copy-start(bf16[24,128]{1,0:T(8,128)(2,1)} %param.15) | copy-start | bytes 18436
  25.8 31.7 %copy-start.5 = (bf16[24,128,128]{2,1,0:T(8,128)(2,1)S(1)}, bf16[24,128,128]{2,1,0:T(8,128)(2,1)}, u32[]{:S(2)}) copy-start(bf16[24,128,128]{2,1,0:T(8,128)(2,1)} %param.19) | copy-start | bytes 2359300
  43.9 12.7 %all-to-all-start.1 = ((f32[32,2,516]{2,1,0:T(2,128)}), f32[32,2,516]{2,1,0:T(2,128)S(1)}, u32[]{:S(2)}, u32[]{:S(2)}) async-start(f32[32,2,516]{2,1,0:T(2,128)} %reshape.288), calls=%async_computation.1 | async-start | bytes 327680 | tf_op jit(solution)/shard_map/all_to_all | solution.py:402
  57.3 26.7 %copy-start.3 = (bf16[4096]{0:T(1024)(128)(2,1)S(1)}, bf16[4096]{0:T(1024)(128)(2,1)}, u32[]{:S(2)}) copy-start(bf16[4096]{0:T(1024)(128)(2,1)} %param.25) | copy-start | bytes 24580
  57.5 40.2 %copy-start.2 = (bf16[24,4096]{1,0:T(8,128)(2,1)S(1)}, bf16[24,4096]{1,0:T(8,128)(2,1)}, u32[]{:S(2)}) copy-start(bf16[24,4096]{1,0:T(8,128)(2,1)} %param.24) | copy-start | bytes 589828
  80.6 17.0 %all-to-all-start.3 = ((f32[24,8,512]{2,0,1:T(8,128)}), f32[24,8,512]{2,0,1:T(8,128)S(1)}, u32[]{:S(2)}, u32[]{:S(2)}) async-start(f32[24,8,512]{2,0,1:T(8,128)} %broadcast_in_dim.156), calls=%async_computation.3 | async-start | bytes 786432 | tf_op jit(solution)/shard_map/all_to_all | solution.py:461

commit v8 on v7

--- a/solution.py
+++ b/solution.py
@@ -187,6 +187,7 @@
 
 TILE_SLOTS = 16
 KEY_BLOCK = 1024
+SINK_BLOCK = 128
 
 
 def sorted_prefix_kernel(
@@ -209,20 +210,22 @@
             grp = group_ref[pl.ds(r0, tile_rows), :]
             bnd = bound_ref[pl.ds(r0, tile_rows), :]
 
-            def block(j, state):
+            late = jnp.maximum(bnd, SINK_BLOCK)
+
+            def attend(k0, kb, vb, state, sinks):
                 old, total, acc = state
-                k0 = pl.multiple_of(j * KEY_BLOCK, KEY_BLOCK)
-                kb = key_ref[g, pl.ds(k0, KEY_BLOCK), :]
-                vb = value_ref[g, pl.ds(k0, KEY_BLOCK), :]
                 scores = lax.dot_general(
                     q, kb, (((1,), (1,)), ((), ())), preferred_element_type=jnp.float32
                 ) * (1.0 / math.sqrt(HD))
                 positions = k0 + lax.broadcasted_iota(jnp.int32, scores.shape, 1)
-                usable = (
-                    (grp == g)
-                    & (positions < prompt_count)
-                    & ((positions < SINKS) | (positions >= bnd))
-                )
+                if sinks:
+                    usable = (
+                        (grp == g)
+                        & (positions < prompt_count)
+                        & ((positions < SINKS) | (positions >= bnd))
+                    )
+                else:
+                    usable = (grp == g) & (positions < prompt_count) & (positions >= late)
                 masked = jnp.where(usable, scores, FAR_BELOW)
                 updated = jnp.maximum(old, jnp.max(masked, axis=1, keepdims=True))
                 weights = jnp.where(usable, jnp.exp(masked - updated), 0.0)
@@ -238,7 +241,18 @@
                 weight_sum[pl.ds(r0, tile_rows), :],
                 weighted[pl.ds(r0, tile_rows), :],
             )
-            state = block(0, state)
+            state = attend(
+                0, key_ref[g, pl.ds(0, SINK_BLOCK), :], value_ref[g, pl.ds(0, SINK_BLOCK), :],
+                state, True,
+            )
+
+            def block(j, state):
+                k0 = pl.multiple_of(j * KEY_BLOCK, KEY_BLOCK)
+                return attend(
+                    k0, key_ref[g, pl.ds(k0, KEY_BLOCK), :], value_ref[g, pl.ds(k0, KEY_BLOCK), :],
+                    state, False,
+                )
+
             first = meta_ref[4 * groups_dev + g * tiles + t]
             state = lax.fori_loop(first, meta_ref[3 * groups_dev + g], block, state)
             running[pl.ds(r0, tile_rows), :] = state[0]
@@ -285,7 +299,9 @@
     tile_low = jnp.min(
         jnp.where(in_group, sorted_low.reshape(1, tiles, TILE_SLOTS), prompt_max), axis=2
     )
-    tile_first = jnp.clip(jnp.floor_divide(tile_low, KEY_BLOCK), 1, blocks)
+    tile_first = jnp.clip(
+        jnp.floor_divide(jnp.maximum(tile_low, SINK_BLOCK), KEY_BLOCK), 0, blocks
+    )
     meta = jnp.concatenate(
         [prompt_len, tile_lo, tile_hi, block_hi, tile_first.reshape(-1)]
     ).astype(jnp.int32)

time: 100 us -> 104 us (1.040)
  starting transfers between devices: 16.8 us -> 33.6 us
  Pallas kernels: 15.8 us -> 2.56 us
    all_to_all x1, starting transfers between devices: 5.75 us -> 22.6 us  [body(): lax.all_to_all(packed.reshape(places, capacity, packed.shape[1]), 'req',...]
    pallas_call x1, Pallas kernels: 15.8 us -> 2.56 us  [prefix_attend_sorted(): pl.pallas_call(sorted_prefix_kernel, grid_spec=pltpu.PrefetchScalarGridSp...]
  transfers between devices with their start and end apart: 3 -> 3, of which waited for: 2 -> 2; matrix products, arithmetic and copies ran while one was open for 12% -> 11% of each run, Pallas kernels for 0% -> 0%
where the time goes in v8:
time: 104 us; the launch traced here: 102 us
  starting transfers between devices  33.6 us (32%)
  waiting for transfers between devices  20.2 us (19%)
  blocking collectives  19.1 us (18%)
  local copies, waits for them, and re-layouts  13.9 us (13%)
  other arithmetic  6.4 us (6%)
  matrix products  5.54 us (5%)
  Pallas kernels  2.56 us (2%)
    all_to_all x1, starting transfers between devices, body(): lax.all_to_all(packed.reshape(places, capacity, packed.shape[1]), 'req',...  22.6 us
    all_to_all x1, blocking collectives, body(): lax.all_to_all(lax.optimization_barrier(partial_value).astype(jnp.bfloat1...  19.1 us
    all_to_all x1, waiting for transfers between devices, body(): gathered = lax.all_to_all(spread, 'tp', 1, 1, tiled=True)  13.6 us
    all_to_all x1, starting transfers between devices, body(): lax.all_to_all(send_query.reshape(places, capacity, heads_dev * HD), 'req...  7.62 us
    all_to_all x1, waiting for transfers between devices, body(): lax.all_to_all(packed.reshape(places, capacity, packed.shape[1]), 'req',...  6.65 us
    all_to_all x1, starting transfers between devices, body(): gathered = lax.all_to_all(spread, 'tp', 1, 1, tiled=True)  3.45 us
    dot_general x1, matrix products, body(): jnp.dot(attended, o_weight, preferred_element_type=jnp.float32)  2.86 us
    pallas_call x1, Pallas kernels, prefix_attend_sorted(): pl.pallas_call(sorted_prefix_kernel, grid_spec=pltpu.PrefetchScalarGridSp...  2.56 us
  transfers between devices with their start and end apart: 3, of which 2 were waited for; matrix products, arithmetic and copies ran while one was open for 11% of the time, Pallas kernels for 0%

profile of v8, /device:TPU:2, one launch (start us, length us, event | category | flops | bytes accessed | tf_op | source)
XLA Modules:
  0.0 102.3 jit_solution(1823776379425712429)
XLA Ops:
  0.7 0.8 and_select_fusion
  1.5 0.2 convert_reduce_fusion.2
  1.7 0.8 compare_select_fusion
  2.4 0.9 convolution_convert_fusion
  3.3 0.7 reshape.295
  4.0 7.6 %all-to-all-start = ((bf16[32,2,512]{2,1,0:T(2,128)(2,1)}), bf16[32,2,512]{2,1,0:T(2,128)(2,1)S(1)}, u32[]{:S(2)}, u32[]{:S(2)}) async-start(bf16[32,2,512]{2,1,0:T(2,128)(2,1)} %reshape.295), calls=%async_computation | async-start | bytes 131072 | tf_op jit(solution)/shard_map/all_to_all | solution.py:411
  11.6 0.7 fusion.27
  12.3 0.1 eq.106
  12.5 0.8 broadcast_in_dim.137
  13.3 0.2 reduce_window_sum.18
  13.6 0.8 broadcast_in_dim.144
  14.6 0.1 sub.87
  14.8 0.2 convert_reduce_fusion.1
  14.9 0.9 select_reduce_fusion.4
  15.9 0.1 reshape.294
  16.0 0.1 select_reduce_fusion
  16.1 0.8 gather_fusion
  16.9 0.8 gather_fusion.1
  17.9 0.1 select_reduce_fusion.3
  18.0 0.7 and_select_fusion.1
  18.7 0.8 dynamic_slice.7
  19.5 0.7 reshape.303
  20.4 0.2 reduce-window.9
  20.8 0.1 reshape_reshape.8.group_ref
  21.0 0.8 fusion.24
  21.8 0.6 fusion.35
  22.4 0.7 concatenate.6.meta_ref
  23.2 0.7 gather_fusion.2
  24.0 1.9 %copy-done.1 = bf16[2,6144,128]{2,1,0:T(8,128)(2,1)S(1)} copy-done((bf16[2,6144,128]{2,1,0:T(8,128)(2,1)S(1)}, bf16[2,6144,128]{2,1,0:T(8,128)(2,1)}, u32[]{:S(2)}) %copy-start.1) | copy-done | bytes 3145752
  25.9 2.6 %shard_map.140 = (f32[256,128]{1,0:T(8,128)S(1)}, f32[256,1]{1,0:T(8,128)S(1)}) custom-call(s32[16]{0:T(128)S(1)} %concatenate.6.meta_ref, bf16[256,128]{1,0:T(8,128)(2,1)S(1)} %reshape.297.query_ref, bf16[2,6144,128]{2,1,0:T(8,128)(2,1)S(1)} %copy-done.1, bf16[2,6144,128]{2,1,0:T(8,128)(2,1)} %value_ref.1, s32[256,1]{1,0:T(8,128)S(1)} %reshape_reshape.8.group_ref, ...), custom_call_target="tpu_custom_call" | custom-call | flops 402653184 | bytes 6488064 | tf_op jit(solution)/shard_map/pallas_call | solution.py:316
  28.5 0.1 reduce.4
  28.6 0.1 reshape.299
  28.7 0.7 gather_fusion.3
  29.4 0.6 gather_fusion.4
  30.0 0.8 reshape.300
  30.8 22.6 %all-to-all-start.1 = ((f32[32,2,516]{2,1,0:T(2,128)}), f32[32,2,516]{2,1,0:T(2,128)S(1)}, u32[]{:S(2)}, u32[]{:S(2)}) async-start(f32[32,2,516]{2,1,0:T(2,128)} %reshape.300), calls=%async_computation.1 | async-start | bytes 327680 | tf_op jit(solution)/shard_map/all_to_all | solution.py:418
  53.4 0.2 fusion.9
  53.5 6.6 %all-to-all-done.1 = f32[32,2,516]{2,1,0:T(2,128)S(1)} async-done(((f32[32,2,516]{2,1,0:T(2,128)}), f32[32,2,516]{2,1,0:T(2,128)S(1)}, u32[]{:S(2)}, u32[]{:S(2)}) %all-to-all-start.1) | async-done | bytes 132128 | tf_op jit(solution)/shard_map/all_to_all | solution.py:418
  60.2 0.1 reshape.301
  60.3 0.6 gather_fusion.5
  61.1 0.4 fusion.4
  61.4 2.9 %fusion.11 = bf16[24,4096]{1,0:T(8,128)(2,1)S(1)} fusion(bf16[512,4096]{1,0:T(8,128)(2,1)} %param.23, bf16[3,8,4,128]{3,2,1,0:T(4,128)(2,1)S(1)} %bitcast.43), kind=kOutput, calls=%fused_computation.31 | convolution fusion | flops 100663296 | bytes 4415488 | tf_op jit(solution)/shard_map/dot_general | solution.py:468
  64.3 19.1 %all_to_all.20 = bf16[24,8,512]{2,0,1:T(8,128)(2,1)S(1)} all-to-all(bf16[24,8,512]{2,0,1:T(8,128)(2,1)S(1)} %bitcast.40), channel_id=1, replica_groups=mesh['req'=32,'tp'=8] {'tp'}, dimensions={1} | all-to-all | bytes 393216 | tf_op jit(solution)/shard_map/all_to_all | solution.py:471
  83.4 0.8 broadcast_in_dim.156
  84.2 3.5 %all-to-all-start.3 = ((f32[24,8,512]{2,0,1:T(8,128)}), f32[24,8,512]{2,0,1:T(8,128)S(1)}, u32[]{:S(2)}, u32[]{:S(2)}) async-start(f32[24,8,512]{2,0,1:T(8,128)} %broadcast_in_dim.156), calls=%async_computation.3 | async-start | bytes 786432 | tf_op jit(solution)/shard_map/all_to_all | solution.py:477
  87.7 13.6 %all-to-all-done.3 = f32[24,8,512]{2,0,1:T(8,128)S(1)} async-done(((f32[24,8,512]{2,0,1:T(8,128)}), f32[24,8,512]{2,0,1:T(8,128)S(1)}, u32[]{:S(2)}, u32[]{:S(2)}) %all-to-all-start.3) | async-done | bytes 393248 | tf_op jit(solution)/shard_map/all_to_all | solution.py:477
  101.3 0.2 multiply_reduce_fusion
  101.5 0.8 multiply_convert_fusion
  (58 shorter events, 1.6 us)
Async XLA Ops:
  0.6 21.2 %copy-start = (bf16[24,128,128]{2,1,0:T(8,128)(2,1)S(1)}, bf16[24,128,128]{2,1,0:T(8,128)(2,1)}, u32[]{:S(2)}) copy-start(bf16[24,128,128]{2,1,0:T(8,128)(2,1)} %param.18) | copy-start | bytes 2359300
  4.0 19.2 %all-to-all-start = ((bf16[32,2,512]{2,1,0:T(2,128)(2,1)}), bf16[32,2,512]{2,1,0:T(2,128)(2,1)S(1)}, u32[]{:S(2)}, u32[]{:S(2)}) async-start(bf16[32,2,512]{2,1,0:T(2,128)(2,1)} %reshape.295), calls=%async_computation | async-start | bytes 131072 | tf_op jit(solution)/shard_map/all_to_all | solution.py:411
  24.0 1.9 %copy-start.1 = (bf16[2,6144,128]{2,1,0:T(8,128)(2,1)S(1)}, bf16[2,6144,128]{2,1,0:T(8,128)(2,1)}, u32[]{:S(2)}) copy-start(bf16[2,6144,128]{2,1,0:T(8,128)(2,1)} %key_ref.1) | copy-start | bytes 9437188
  25.9 27.4 %copy-start.4 = (bf16[24,128]{1,0:T(8,128)(2,1)S(1)}, bf16[24,128]{1,0:T(8,128)(2,1)}, u32[]{:S(2)}) copy-start(bf16[24,128]{1,0:T(8,128)(2,1)} %param.15) | copy-start | bytes 18436
  25.9 35.2 %copy-start.5 = (bf16[24,128,128]{2,1,0:T(8,128)(2,1)S(1)}, bf16[24,128,128]{2,1,0:T(8,128)(2,1)}, u32[]{:S(2)}) copy-start(bf16[24,128,128]{2,1,0:T(8,128)(2,1)} %param.19) | copy-start | bytes 2359300
  30.8 29.4 %all-to-all-start.1 = ((f32[32,2,516]{2,1,0:T(2,128)}), f32[32,2,516]{2,1,0:T(2,128)S(1)}, u32[]{:S(2)}, u32[]{:S(2)}) async-start(f32[32,2,516]{2,1,0:T(2,128)} %reshape.300), calls=%async_computation.1 | async-start | bytes 327680 | tf_op jit(solution)/shard_map/all_to_all | solution.py:418
  60.9 26.7 %copy-start.3 = (bf16[4096]{0:T(1024)(128)(2,1)S(1)}, bf16[4096]{0:T(1024)(128)(2,1)}, u32[]{:S(2)}) copy-start(bf16[4096]{0:T(1024)(128)(2,1)} %param.25) | copy-start | bytes 24580
  61.0 40.2 %copy-start.2 = (bf16[24,4096]{1,0:T(8,128)(2,1)S(1)}, bf16[24,4096]{1,0:T(8,128)(2,1)}, u32[]{:S(2)}) copy-start(bf16[24,4096]{1,0:T(8,128)(2,1)} %param.24) | copy-start | bytes 589828
  84.2 17.0 %all-to-all-start.3 = ((f32[24,8,512]{2,0,1:T(8,128)}), f32[24,8,512]{2,0,1:T(8,128)S(1)}, u32[]{:S(2)}, u32[]{:S(2)}) async-start(f32[24,8,512]{2,0,1:T(8,128)} %broadcast_in_dim.156), calls=%async_computation.3 | async-start | bytes 786432 | tf_op jit(solution)/shard_map/all_to_all | solution.py:477

commit v9 on v7

--- a/solution.py
+++ b/solution.py
@@ -451,15 +451,14 @@
     attended = attended.reshape(req_dev, heads_dev * HD).astype(jnp.bfloat16)
     partial_value = jnp.dot(attended, o_weight, preferred_element_type=jnp.float32)
     lanes = lax.axis_size("tp")
-    width = partial_value.shape[1] // lanes
-    pieces = lax.all_to_all(
-        lax.optimization_barrier(partial_value).astype(jnp.bfloat16).reshape(req_dev, lanes, width),
-        "tp", 1, 1, tiled=True,
-    )
-    owned_sum = jnp.sum(pieces.astype(jnp.float32), axis=1, keepdims=True)
-    spread = jnp.broadcast_to(owned_sum, (req_dev, lanes, width))
-    gathered = lax.all_to_all(spread, "tp", 1, 1, tiled=True)
-    proj = gathered.reshape(req_dev, lanes * width)
+    sent = lax.optimization_barrier(partial_value).astype(jnp.bfloat16)
+    proj = sent.astype(jnp.float32)
+    distance = 1
+    while distance < lanes:
+        pairs = [(i, i ^ distance) for i in range(lanes)]
+        proj = proj + lax.ppermute(sent, "tp", pairs).astype(jnp.float32)
+        sent = proj
+        distance *= 2
     summed = residual.astype(jnp.float32) + proj
     hidden = summed.astype(jnp.bfloat16)
     inverse = lax.rsqrt(jnp.mean(summed * summed, axis=-1, keepdims=True) + NORM_EPS)

time: 100 us -> 118 us (1.18); the launches traced: 98.7 us -> 119 us
  starting transfers between devices: 16.8 us -> 43.8 us
  waiting for transfers between devices: 20.3 us -> 46.4 us
  blocking collectives: 19.1 us -> 0 us
  Pallas kernels: 15.8 us -> 2.56 us
    ppermute x0 -> x3, waiting for transfers between devices: none -> 39.7 us  [body(): proj = proj + lax.ppermute(sent, 'tp', pairs).astype(jnp.float32)]
    all_to_all x1 -> x0, blocking collectives: 19.1 us -> none  [body(): lax.all_to_all(lax.optimization_barrier(partial_value).astype(jnp.bfloat1...]
    all_to_all x1, starting transfers between devices: 5.75 us -> 24.6 us  [body(): lax.all_to_all(packed.reshape(places, capacity, packed.shape[1]), 'req',...]
    all_to_all x1 -> x0, waiting for transfers between devices: 13.6 us -> none  [body(): gathered = lax.all_to_all(spread, 'tp', 1, 1, tiled=True)]
    pallas_call x1, Pallas kernels: 15.8 us -> 2.56 us  [prefix_attend_sorted(): pl.pallas_call(sorted_prefix_kernel, grid_spec=pltpu.PrefetchScalarGridSp...]
    ppermute x0 -> x3, starting transfers between devices: none -> 11.6 us  [body(): proj = proj + lax.ppermute(sent, 'tp', pairs).astype(jnp.float32)]
    all_to_all x1 -> x0, starting transfers between devices: 3.45 us -> none  [body(): gathered = lax.all_to_all(spread, 'tp', 1, 1, tiled=True)]
  transfers between devices with their start and end apart: 3 -> 5, of which waited for: 2 -> 4; matrix products, arithmetic and copies ran while one was open for 12% -> 10% of each run, Pallas kernels for 0% -> 0%
where the time goes in v9:
time: 118 us; the launch traced here: 119 us
  waiting for transfers between devices  46.4 us (39%)
  starting transfers between devices  43.8 us (37%)
  local copies, waits for them, and re-layouts  12.9 us (11%)
  other arithmetic  6.46 us (5%)
  matrix products  5.55 us (5%)
  Pallas kernels  2.56 us (2%)
    ppermute x3, waiting for transfers between devices, body(): proj = proj + lax.ppermute(sent, 'tp', pairs).astype(jnp.float32)  39.7 us
    all_to_all x1, starting transfers between devices, body(): lax.all_to_all(packed.reshape(places, capacity, packed.shape[1]), 'req',...  24.6 us
    ppermute x3, starting transfers between devices, body(): proj = proj + lax.ppermute(sent, 'tp', pairs).astype(jnp.float32)  11.6 us
    all_to_all x1, starting transfers between devices, body(): lax.all_to_all(send_query.reshape(places, capacity, heads_dev * HD), 'req...  7.62 us
    all_to_all x1, waiting for transfers between devices, body(): lax.all_to_all(packed.reshape(places, capacity, packed.shape[1]), 'req',...  6.65 us
    dot_general x1, matrix products, body(): jnp.dot(attended, o_weight, preferred_element_type=jnp.float32)  2.85 us
    pallas_call x1, Pallas kernels, prefix_attend_sorted(): pl.pallas_call(sorted_prefix_kernel, grid_spec=pltpu.PrefetchScalarGridSp...  2.56 us
  transfers between devices with their start and end apart: 5, of which 4 were waited for; matrix products, arithmetic and copies ran while one was open for 10% of the time, Pallas kernels for 0%

profile of v9, /device:TPU:2, one launch (start us, length us, event | category | flops | bytes accessed | tf_op | source)
XLA Modules:
  0.0 118.7 jit_solution(15640622603291853910)
XLA Ops:
  0.7 0.8 and_select_fusion
  1.5 0.2 convert_reduce_fusion.1
  1.7 0.8 compare_select_fusion
  2.4 0.9 convolution_convert_fusion
  3.3 0.7 reshape.276
  4.0 7.6 %all-to-all-start = ((bf16[32,2,512]{2,1,0:T(2,128)(2,1)}), bf16[32,2,512]{2,1,0:T(2,128)(2,1)S(1)}, u32[]{:S(2)}, u32[]{:S(2)}) async-start(bf16[32,2,512]{2,1,0:T(2,128)(2,1)} %reshape.276), calls=%async_computation | async-start | bytes 131072 | tf_op jit(solution)/shard_map/all_to_all | solution.py:395
  11.6 0.7 fusion.26
  12.5 0.8 broadcast_in_dim.131
  13.3 0.2 reduce_window_sum.18
  13.6 0.8 broadcast_in_dim.138
  14.6 0.1 sub.87
  14.8 0.2 convert_reduce_fusion
  14.9 0.9 select_reduce_fusion.4
  15.8 0.7 and_select_fusion.2
  16.5 0.1 select_reduce_fusion
  16.6 0.8 gather_fusion
  17.5 0.8 dynamic_slice.7
  18.2 0.7 reshape.284
  19.1 0.1 reshape.275
  19.2 0.8 gather_fusion.1
  20.0 0.1 select_reduce_fusion.3
  20.3 0.2 reduce-window.9
  20.9 0.8 fusion.23
  21.7 0.6 fusion.35
  22.3 0.7 concatenate.6.meta_ref
  23.1 0.7 gather_fusion.2
  23.9 1.9 %copy-done.1 = bf16[2,6144,128]{2,1,0:T(8,128)(2,1)S(1)} copy-done((bf16[2,6144,128]{2,1,0:T(8,128)(2,1)S(1)}, bf16[2,6144,128]{2,1,0:T(8,128)(2,1)}, u32[]{:S(2)}) %copy-start.1) | copy-done | bytes 3145752
  25.8 2.6 %shard_map.140 = (f32[256,128]{1,0:T(8,128)S(1)}, f32[256,1]{1,0:T(8,128)S(1)}) custom-call(s32[16]{0:T(128)S(1)} %concatenate.6.meta_ref, bf16[256,128]{1,0:T(8,128)(2,1)S(1)} %reshape.278.query_ref, bf16[2,6144,128]{2,1,0:T(8,128)(2,1)S(1)} %copy-done.1, bf16[2,6144,128]{2,1,0:T(8,128)(2,1)} %value_ref.1, s32[256,1]{1,0:T(8,128)S(1)} %reshape_reshape.8.group_ref, ...), custom_call_target="tpu_custom_call" | custom-call | flops 402653184 | bytes 6488064 | tf_op jit(solution)/shard_map/pallas_call | solution.py:300
  28.4 0.1 reduce.4
  28.5 0.1 reshape.280
  28.6 0.7 gather_fusion.3
  29.3 0.6 gather_fusion.4
  29.9 0.8 reshape.281
  30.6 24.6 %all-to-all-start.1 = ((f32[32,2,516]{2,1,0:T(2,128)}), f32[32,2,516]{2,1,0:T(2,128)S(1)}, u32[]{:S(2)}, u32[]{:S(2)}) async-start(f32[32,2,516]{2,1,0:T(2,128)} %reshape.281), calls=%async_computation.1 | async-start | bytes 327680 | tf_op jit(solution)/shard_map/all_to_all | solution.py:402
  55.3 0.2 fusion.8
  55.5 6.6 %all-to-all-done.1 = f32[32,2,516]{2,1,0:T(2,128)S(1)} async-done(((f32[32,2,516]{2,1,0:T(2,128)}), f32[32,2,516]{2,1,0:T(2,128)S(1)}, u32[]{:S(2)}, u32[]{:S(2)}) %all-to-all-start.1) | async-done | bytes 132128 | tf_op jit(solution)/shard_map/all_to_all | solution.py:402
  62.1 0.1 reshape.282
  62.3 0.6 gather_fusion.5
  63.0 0.4 fusion.4
  63.4 2.9 %fusion.10 = bf16[24,4096]{1,0:T(8,128)(2,1)S(1)} fusion(bf16[512,4096]{1,0:T(8,128)(2,1)} %param.23, bf16[3,8,4,128]{3,2,1,0:T(4,128)(2,1)S(1)} %bitcast.32), kind=kOutput, calls=%fused_computation.29 | convolution fusion | flops 100663296 | bytes 4415488 | tf_op jit(solution)/shard_map/dot_general | solution.py:452
  66.3 2.0 %collective-permute-start = (bf16[24,4096]{1,0:T(8,128)(2,1)S(1)}, bf16[24,4096]{1,0:T(8,128)(2,1)S(1)}, u32[]{:S(2)}, u32[]{:S(2)}) collective-permute-start(bf16[24,4096]{1,0:T(8,128)(2,1)S(1)} %fusion.10), channel_id=1, source_target_pairs={{0,1},{1,0},{2,3},{3,2},{4,5},{5,4},{6,7},{7,6},{8,9},{9,8},{10,11... | collective-permute-start | bytes 589832 | tf_op jit(solution)/shard_map/ppermute | solution.py:459
  68.2 5.2 %collective-permute-done = bf16[24,4096]{1,0:T(8,128)(2,1)S(1)} collective-permute-done((bf16[24,4096]{1,0:T(8,128)(2,1)S(1)}, bf16[24,4096]{1,0:T(8,128)(2,1)S(1)}, u32[]{:S(2)}, u32[]{:S(2)}) %collective-permute-start) | collective-permute-done | bytes 196640 | tf_op jit(solution)/shard_map/ppermute | solution.py:459
  73.5 3.4 %collective-permute-start.1 = (f32[24,4096]{1,0:T(8,128)S(1)}, f32[24,4096]{1,0:T(8,128)S(1)}, u32[]{:S(2)}, u32[]{:S(2)}) collective-permute-start(f32[24,4096]{1,0:T(8,128)S(1)} %convert_add_fusion), channel_id=1, source_target_pairs={{0,2},{1,3},{2,0},{3,1},{4,6},{5,7},{6,4},{7,5},{8,10},{9,11},{10,... | collective-permute-start | bytes 1179656 | tf_op jit(solution)/shard_map/ppermute | solution.py:459
  76.8 17.2 %collective-permute-done.1 = f32[24,4096]{1,0:T(8,128)S(1)} collective-permute-done((f32[24,4096]{1,0:T(8,128)S(1)}, f32[24,4096]{1,0:T(8,128)S(1)}, u32[]{:S(2)}, u32[]{:S(2)}) %collective-permute-start.1) | collective-permute-done | bytes 393248 | tf_op jit(solution)/shard_map/ppermute | solution.py:459
  94.1 6.3 %collective-permute-start.2 = (f32[24,4096]{1,0:T(8,128)S(1)}, f32[24,4096]{1,0:T(8,128)S(1)}, u32[]{:S(2)}, u32[]{:S(2)}) collective-permute-start(f32[24,4096]{1,0:T(8,128)S(1)} %fusion.33), channel_id=1, source_target_pairs={{0,4},{1,5},{2,6},{3,7},{4,0},{5,1},{6,2},{7,3},{8,12},{9,13},{10,... | collective-permute-start | bytes 1179656 | tf_op jit(solution)/shard_map/ppermute | solution.py:459
  100.4 17.3 %collective-permute-done.2 = f32[24,4096]{1,0:T(8,128)S(1)} collective-permute-done((f32[24,4096]{1,0:T(8,128)S(1)}, f32[24,4096]{1,0:T(8,128)S(1)}, u32[]{:S(2)}, u32[]{:S(2)}) %collective-permute-start.2) | collective-permute-done | bytes 393248 | tf_op jit(solution)/shard_map/ppermute | solution.py:459
  117.7 0.2 multiply_reduce_fusion
  117.9 0.8 multiply_convert_fusion
  (56 shorter events, 1.7 us)
Async XLA Ops:
  0.6 21.1 %copy-start = (bf16[24,128,128]{2,1,0:T(8,128)(2,1)S(1)}, bf16[24,128,128]{2,1,0:T(8,128)(2,1)}, u32[]{:S(2)}) copy-start(bf16[24,128,128]{2,1,0:T(8,128)(2,1)} %param.18) | copy-start | bytes 2359300
  4.0 19.1 %all-to-all-start = ((bf16[32,2,512]{2,1,0:T(2,128)(2,1)}), bf16[32,2,512]{2,1,0:T(2,128)(2,1)S(1)}, u32[]{:S(2)}, u32[]{:S(2)}) async-start(bf16[32,2,512]{2,1,0:T(2,128)(2,1)} %reshape.276), calls=%async_computation | async-start | bytes 131072 | tf_op jit(solution)/shard_map/all_to_all | solution.py:395
  23.9 1.9 %copy-start.1 = (bf16[2,6144,128]{2,1,0:T(8,128)(2,1)S(1)}, bf16[2,6144,128]{2,1,0:T(8,128)(2,1)}, u32[]{:S(2)}) copy-start(bf16[2,6144,128]{2,1,0:T(8,128)(2,1)} %key_ref.1) | copy-start | bytes 9437188
  25.8 29.5 %copy-start.4 = (bf16[24,128]{1,0:T(8,128)(2,1)S(1)}, bf16[24,128]{1,0:T(8,128)(2,1)}, u32[]{:S(2)}) copy-start(bf16[24,128]{1,0:T(8,128)(2,1)} %param.15) | copy-start | bytes 18436
  25.8 37.2 %copy-start.5 = (bf16[24,128,128]{2,1,0:T(8,128)(2,1)S(1)}, bf16[24,128,128]{2,1,0:T(8,128)(2,1)}, u32[]{:S(2)}) copy-start(bf16[24,128,128]{2,1,0:T(8,128)(2,1)} %param.19) | copy-start | bytes 2359300
  30.6 31.5 %all-to-all-start.1 = ((f32[32,2,516]{2,1,0:T(2,128)}), f32[32,2,516]{2,1,0:T(2,128)S(1)}, u32[]{:S(2)}, u32[]{:S(2)}) async-start(f32[32,2,516]{2,1,0:T(2,128)} %reshape.281), calls=%async_computation.1 | async-start | bytes 327680 | tf_op jit(solution)/shard_map/all_to_all | solution.py:402
  62.3 38.1 %copy-start.3 = (bf16[4096]{0:T(1024)(128)(2,1)S(1)}, bf16[4096]{0:T(1024)(128)(2,1)}, u32[]{:S(2)}) copy-start(bf16[4096]{0:T(1024)(128)(2,1)} %param.25) | copy-start | bytes 24580
  62.3 55.5 %copy-start.2 = (bf16[24,4096]{1,0:T(8,128)(2,1)S(1)}, bf16[24,4096]{1,0:T(8,128)(2,1)}, u32[]{:S(2)}) copy-start(bf16[24,4096]{1,0:T(8,128)(2,1)} %param.24) | copy-start | bytes 589828
  66.3 7.2 %collective-permute-start = (bf16[24,4096]{1,0:T(8,128)(2,1)S(1)}, bf16[24,4096]{1,0:T(8,128)(2,1)S(1)}, u32[]{:S(2)}, u32[]{:S(2)}) collective-permute-start(bf16[24,4096]{1,0:T(8,128)(2,1)S(1)} %fusion.10), channel_id=1, source_target_pairs={{0,1},{1,0},{2,3},{3,2},{4,5},{5,4},{6,7},{7,6},{8,9},{9,8},{10,11... | collective-permute-start | bytes 589832 | tf_op jit(solution)/shard_map/ppermute | solution.py:459
  73.5 20.5 %collective-permute-start.1 = (f32[24,4096]{1,0:T(8,128)S(1)}, f32[24,4096]{1,0:T(8,128)S(1)}, u32[]{:S(2)}, u32[]{:S(2)}) collective-permute-start(f32[24,4096]{1,0:T(8,128)S(1)} %convert_add_fusion), channel_id=1, source_target_pairs={{0,2},{1,3},{2,0},{3,1},{4,6},{5,7},{6,4},{7,5},{8,10},{9,11},{10,... | collective-permute-start | bytes 1179656 | tf_op jit(solution)/shard_map/ppermute | solution.py:459
  94.1 23.6 %collective-permute-start.2 = (f32[24,4096]{1,0:T(8,128)S(1)}, f32[24,4096]{1,0:T(8,128)S(1)}, u32[]{:S(2)}, u32[]{:S(2)}) collective-permute-start(f32[24,4096]{1,0:T(8,128)S(1)} %fusion.33), channel_id=1, source_target_pairs={{0,4},{1,5},{2,6},{3,7},{4,0},{5,1},{6,2},{7,3},{8,12},{9,13},{10,... | collective-permute-start | bytes 1179656 | tf_op jit(solution)/shard_map/ppermute | solution.py:459

commit v10 on v7

--- a/solution.py
+++ b/solution.py
@@ -398,13 +398,15 @@
     part_out, part_log = prefix_attend_sorted(
         compact, slot_group, slot_suffix, prefix_key, prefix_value, prompt_len, first_group
     )
-    packed = jnp.concatenate([part_out, part_log], axis=1)
-    returned = lax.all_to_all(
-        packed.reshape(places, capacity, packed.shape[1]), "req", 0, 0, tiled=True
-    ).reshape(slot_total, packed.shape[1])
-    picked = returned[own_slot]
-    prefix_out = picked[:, : heads_dev * HD]
-    prefix_log = picked[:, heads_dev * HD :]
+    returned_out = lax.all_to_all(
+        part_out.astype(jnp.bfloat16).reshape(places, capacity, heads_dev * HD), "req", 0, 0,
+        tiled=True,
+    ).reshape(slot_total, heads_dev * HD)
+    returned_log = lax.all_to_all(
+        part_log.reshape(places, capacity, heads_dev), "req", 0, 0, tiled=True
+    ).reshape(slot_total, heads_dev)
+    prefix_out = returned_out[own_slot].astype(jnp.float32)
+    prefix_log = returned_log[own_slot]
     queries = query.reshape(req_dev, kv_dev, repeat, HD)
     key_rows = suffix_key.reshape(req_dev, suffix_max, kv_dev, HD)
     value_rows = suffix_value.reshape(req_dev, suffix_max, kv_dev, HD)

time: 100 us -> 114 us (1.14)
  starting transfers between devices: 16.8 us -> 32.2 us
  Pallas kernels: 15.8 us -> 10.1 us
  waiting for transfers between devices: 20.3 us -> 24.1 us
    all_to_all x1 -> x2, starting transfers between devices: 5.75 us -> 21.1 us  [the longest x1 16.1 us: body(): lax.all_to_all(part_log.reshape(places, capacity, heads_dev), 'req', 0, 0...]
    pallas_call x1, Pallas kernels: 15.8 us -> 10.1 us  [prefix_attend_sorted(): pl.pallas_call(sorted_prefix_kernel, grid_spec=pltpu.PrefetchScalarGridSp...]
    all_to_all x1 -> x2, waiting for transfers between devices: 6.72 us -> 10.5 us  [the longest x1 5.73 us: body(): lax.all_to_all(part_out.astype(jnp.bfloat16).reshape(places, capacity, he...]
  transfers between devices with their start and end apart: 3 -> 4, of which waited for: 2 -> 3; matrix products, arithmetic and copies ran while one was open for 12% -> 12% of each run, Pallas kernels for 0% -> 0%
where the time goes in v10:
time: 114 us; the launch traced here: 113 us
  starting transfers between devices  32.2 us (28%)
  waiting for transfers between devices  24.1 us (21%)
  blocking collectives  19 us (17%)
  local copies, waits for them, and re-layouts  14.8 us (13%)
  Pallas kernels  10.1 us (9%)
  other arithmetic  6.38 us (6%)
  matrix products  5.54 us (5%)
    all_to_all x1, blocking collectives, body(): lax.all_to_all(lax.optimization_barrier(partial_value).astype(jnp.bfloat1...  19 us
    all_to_all x1, starting transfers between devices, body(): lax.all_to_all(part_log.reshape(places, capacity, heads_dev), 'req', 0, 0...  16.1 us
    all_to_all x1, waiting for transfers between devices, body(): gathered = lax.all_to_all(spread, 'tp', 1, 1, tiled=True)  13.5 us
    pallas_call x1, Pallas kernels, prefix_attend_sorted(): pl.pallas_call(sorted_prefix_kernel, grid_spec=pltpu.PrefetchScalarGridSp...  10.1 us
    all_to_all x1, starting transfers between devices, body(): lax.all_to_all(send_query.reshape(places, capacity, heads_dev * HD), 'req...  7.62 us
    all_to_all x1, waiting for transfers between devices, body(): lax.all_to_all(part_out.astype(jnp.bfloat16).reshape(places, capacity, he...  5.73 us
    all_to_all x1, starting transfers between devices, body(): lax.all_to_all(part_out.astype(jnp.bfloat16).reshape(places, capacity, he...  4.97 us
    all_to_all x1, waiting for transfers between devices, body(): lax.all_to_all(part_log.reshape(places, capacity, heads_dev), 'req', 0, 0...  4.8 us
  transfers between devices with their start and end apart: 4, of which 3 were waited for; matrix products, arithmetic and copies ran while one was open for 12% of the time, Pallas kernels for 0%

profile of v10, /device:TPU:2, one launch (start us, length us, event | category | flops | bytes accessed | tf_op | source)
XLA Modules:
  0.0 113.1 jit_solution(8328751648122384989)
XLA Ops:
  0.7 0.8 and_select_fusion
  1.5 0.2 convert_reduce_fusion.2
  1.7 0.8 compare_select_fusion
  2.4 0.9 convolution_convert_fusion
  3.3 0.7 reshape.290
  4.0 7.6 %all-to-all-start = ((bf16[32,2,512]{2,1,0:T(2,128)(2,1)}), bf16[32,2,512]{2,1,0:T(2,128)(2,1)S(1)}, u32[]{:S(2)}, u32[]{:S(2)}) async-start(bf16[32,2,512]{2,1,0:T(2,128)(2,1)} %reshape.290), calls=%async_computation | async-start | bytes 131072 | tf_op jit(solution)/shard_map/all_to_all | solution.py:395
  11.6 0.7 fusion.27
  12.5 0.8 broadcast_in_dim.138
  13.3 0.2 reduce_window_sum.18
  13.6 0.8 broadcast_in_dim.145
  14.6 0.1 sub.87
  14.8 0.2 convert_reduce_fusion.1
  14.9 0.9 select_reduce_fusion.4
  15.8 0.7 and_select_fusion.2
  16.5 0.1 select_reduce_fusion
  16.6 0.8 gather_fusion
  17.5 0.8 dynamic_slice.7
  18.2 0.7 reshape.298
  19.1 0.1 reshape.289
  19.2 0.8 gather_fusion.1
  20.0 0.1 select_reduce_fusion.3
  20.3 0.2 reduce-window.9
  20.9 0.8 fusion.24
  21.7 0.6 fusion.35
  22.3 0.2 fusion.9
  22.5 0.7 concatenate.3.meta_ref
  23.3 0.7 gather_fusion.2
  24.1 1.9 %copy-done.1 = bf16[2,6144,128]{2,1,0:T(8,128)(2,1)S(1)} copy-done((bf16[2,6144,128]{2,1,0:T(8,128)(2,1)S(1)}, bf16[2,6144,128]{2,1,0:T(8,128)(2,1)}, u32[]{:S(2)}) %copy-start.1) | copy-done | bytes 3145752
  26.0 10.1 %shard_map.140 = (f32[256,128]{1,0:T(8,128)S(1)}, f32[256,1]{1,0:T(8,128)S(1)}) custom-call(s32[16]{0:T(128)S(1)} %concatenate.3.meta_ref, bf16[256,128]{1,0:T(8,128)(2,1)S(1)} %reshape.292.query_ref, bf16[2,6144,128]{2,1,0:T(8,128)(2,1)S(1)} %copy-done.1, bf16[2,6144,128]{2,1,0:T(8,128)(2,1)} %value_ref.1, s32[256,1]{1,0:T(8,128)S(1)} %reshape_reshape.8.group_ref, ...), custom_call_target="tpu_custom_call" | custom-call | flops 402653184 | bytes 6488064 | tf_op jit(solution)/shard_map/pallas_call | solution.py:300
  36.1 0.1 reduce.4
  36.2 0.1 reshape.295
  36.3 1.2 %gather_fusion.5 = f32[64,4]{1,0:T(8,128)} fusion(f32[64,4]{1,0:T(8,128)S(1)} %reshape.295, s32[1024]{0:T(1024)S(1)} %pad_clamp_fusion.1), kind=kCustom, calls=%fused_computation.5 | custom fusion | bytes 2304 | tf_op jit(solution)/shard_map/gather | solution.py:331
  37.5 16.1 %all-to-all-start.2 = ((f32[32,2,4]{2,1,0:T(2,128)}), f32[32,2,4]{2,1,0:T(2,128)S(1)}, u32[]{:S(2)}, u32[]{:S(2)}) async-start(f32[32,2,4]{2,1,0:T(2,128)} %bitcast.6), calls=%async_computation.2 | async-start | bytes 65536 | tf_op jit(solution)/shard_map/all_to_all | solution.py:405
  53.8 0.7 gather_fusion.3
  54.5 0.7 convert_element_type.81
  55.1 4.8 %all-to-all-done.2 = f32[32,2,4]{2,1,0:T(2,128)S(1)} async-done(((f32[32,2,4]{2,1,0:T(2,128)}), f32[32,2,4]{2,1,0:T(2,128)S(1)}, u32[]{:S(2)}, u32[]{:S(2)}) %all-to-all-start.2) | async-done | bytes 1056 | tf_op jit(solution)/shard_map/all_to_all | solution.py:405
  59.9 5.0 %all-to-all-start.1 = ((bf16[32,2,512]{2,1,0:T(2,128)(2,1)}), bf16[32,2,512]{2,1,0:T(2,128)(2,1)S(1)}, u32[]{:S(2)}, u32[]{:S(2)}) async-start(bf16[32,2,512]{2,1,0:T(2,128)(2,1)} %convert_element_type.81), calls=%async_computation.1 | async-start | bytes 131072 | tf_op jit(solution)/shard_map/all_to_all | solution.py:401
  64.9 0.6 gather_fusion.6
  65.6 5.7 %all-to-all-done.1 = bf16[32,2,512]{2,1,0:T(2,128)(2,1)S(1)} async-done(((bf16[32,2,512]{2,1,0:T(2,128)(2,1)}), bf16[32,2,512]{2,1,0:T(2,128)(2,1)S(1)}, u32[]{:S(2)}, u32[]{:S(2)}) %all-to-all-start.1) | async-done | bytes 65568 | tf_op jit(solution)/shard_map/all_to_all | solution.py:401
  71.3 0.6 gather_fusion.4
  72.0 0.4 fusion.4
  72.4 2.9 %fusion.11 = bf16[24,4096]{1,0:T(8,128)(2,1)S(1)} fusion(bf16[512,4096]{1,0:T(8,128)(2,1)} %param.23, bf16[3,8,4,128]{3,2,1,0:T(4,128)(2,1)S(1)} %bitcast.46), kind=kOutput, calls=%fused_computation.31 | convolution fusion | flops 100663296 | bytes 4415488 | tf_op jit(solution)/shard_map/dot_general | solution.py:454
  75.3 19.0 %all_to_all.25 = bf16[24,8,512]{2,0,1:T(8,128)(2,1)S(1)} all-to-all(bf16[24,8,512]{2,0,1:T(8,128)(2,1)S(1)} %bitcast.42), channel_id=1, replica_groups=mesh['req'=32,'tp'=8] {'tp'}, dimensions={1} | all-to-all | bytes 393216 | tf_op jit(solution)/shard_map/all_to_all | solution.py:457
  94.3 0.8 broadcast_in_dim.157
  95.1 3.5 %all-to-all-start.4 = ((f32[24,8,512]{2,0,1:T(8,128)}), f32[24,8,512]{2,0,1:T(8,128)S(1)}, u32[]{:S(2)}, u32[]{:S(2)}) async-start(f32[24,8,512]{2,0,1:T(8,128)} %broadcast_in_dim.157), calls=%async_computation.4 | async-start | bytes 786432 | tf_op jit(solution)/shard_map/all_to_all | solution.py:463
  98.6 13.5 %all-to-all-done.4 = f32[24,8,512]{2,0,1:T(8,128)S(1)} async-done(((f32[24,8,512]{2,0,1:T(8,128)}), f32[24,8,512]{2,0,1:T(8,128)S(1)}, u32[]{:S(2)}, u32[]{:S(2)}) %all-to-all-start.4) | async-done | bytes 393248 | tf_op jit(solution)/shard_map/all_to_all | solution.py:463
  112.1 0.2 multiply_reduce_fusion
  112.3 0.8 multiply_convert_fusion
  (56 shorter events, 1.7 us)
Async XLA Ops:
  0.6 21.1 %copy-start = (bf16[24,128,128]{2,1,0:T(8,128)(2,1)S(1)}, bf16[24,128,128]{2,1,0:T(8,128)(2,1)}, u32[]{:S(2)}) copy-start(bf16[24,128,128]{2,1,0:T(8,128)(2,1)} %param.18) | copy-start | bytes 2359300
  4.0 19.3 %all-to-all-start = ((bf16[32,2,512]{2,1,0:T(2,128)(2,1)}), bf16[32,2,512]{2,1,0:T(2,128)(2,1)S(1)}, u32[]{:S(2)}, u32[]{:S(2)}) async-start(bf16[32,2,512]{2,1,0:T(2,128)(2,1)} %reshape.290), calls=%async_computation | async-start | bytes 131072 | tf_op jit(solution)/shard_map/all_to_all | solution.py:395
  22.3 31.4 %copy-start.4 = (bf16[24,128]{1,0:T(8,128)(2,1)S(1)}, bf16[24,128]{1,0:T(8,128)(2,1)}, u32[]{:S(2)}) copy-start(bf16[24,128]{1,0:T(8,128)(2,1)} %param.15) | copy-start | bytes 18436
  24.1 1.9 %copy-start.1 = (bf16[2,6144,128]{2,1,0:T(8,128)(2,1)S(1)}, bf16[2,6144,128]{2,1,0:T(8,128)(2,1)}, u32[]{:S(2)}) copy-start(bf16[2,6144,128]{2,1,0:T(8,128)(2,1)} %key_ref.1) | copy-start | bytes 9437188
  26.0 46.0 %copy-start.5 = (bf16[24,128,128]{2,1,0:T(8,128)(2,1)S(1)}, bf16[24,128,128]{2,1,0:T(8,128)(2,1)}, u32[]{:S(2)}) copy-start(bf16[24,128,128]{2,1,0:T(8,128)(2,1)} %param.19) | copy-start | bytes 2359300
  37.5 22.4 %all-to-all-start.2 = ((f32[32,2,4]{2,1,0:T(2,128)}), f32[32,2,4]{2,1,0:T(2,128)S(1)}, u32[]{:S(2)}, u32[]{:S(2)}) async-start(f32[32,2,4]{2,1,0:T(2,128)} %bitcast.6), calls=%async_computation.2 | async-start | bytes 65536 | tf_op jit(solution)/shard_map/all_to_all | solution.py:405
  59.9 11.4 %all-to-all-start.1 = ((bf16[32,2,512]{2,1,0:T(2,128)(2,1)}), bf16[32,2,512]{2,1,0:T(2,128)(2,1)S(1)}, u32[]{:S(2)}, u32[]{:S(2)}) async-start(bf16[32,2,512]{2,1,0:T(2,128)(2,1)} %convert_element_type.81), calls=%async_computation.1 | async-start | bytes 131072 | tf_op jit(solution)/shard_map/all_to_all | solution.py:401
  65.6 33.0 %copy-start.3 = (bf16[4096]{0:T(1024)(128)(2,1)S(1)}, bf16[4096]{0:T(1024)(128)(2,1)}, u32[]{:S(2)}) copy-start(bf16[4096]{0:T(1024)(128)(2,1)} %param.25) | copy-start | bytes 24580
  72.0 40.1 %copy-start.2 = (bf16[24,4096]{1,0:T(8,128)(2,1)S(1)}, bf16[24,4096]{1,0:T(8,128)(2,1)}, u32[]{:S(2)}) copy-start(bf16[24,4096]{1,0:T(8,128)(2,1)} %param.24) | copy-start | bytes 589828
  95.1 17.0 %all-to-all-start.4 = ((f32[24,8,512]{2,0,1:T(8,128)}), f32[24,8,512]{2,0,1:T(8,128)S(1)}, u32[]{:S(2)}, u32[]{:S(2)}) async-start(f32[24,8,512]{2,0,1:T(8,128)} %broadcast_in_dim.157), calls=%async_computation.4 | async-start | bytes 786432 | tf_op jit(solution)/shard_map/all_to_all | solution.py:463

commit v11 on v9

--- a/solution.py
+++ b/solution.py
@@ -452,13 +452,12 @@
     partial_value = jnp.dot(attended, o_weight, preferred_element_type=jnp.float32)
     lanes = lax.axis_size("tp")
     sent = lax.optimization_barrier(partial_value).astype(jnp.bfloat16)
-    proj = sent.astype(jnp.float32)
-    distance = 1
-    while distance < lanes:
-        pairs = [(i, i ^ distance) for i in range(lanes)]
-        proj = proj + lax.ppermute(sent, "tp", pairs).astype(jnp.float32)
-        sent = proj
-        distance *= 2
+    every = lax.all_to_all(
+        jnp.broadcast_to(sent[None], (lanes,) + sent.shape), "tp", 0, 0, tiled=True
+    )
+    proj = every[0].astype(jnp.float32)
+    for lane in range(1, lanes):
+        proj = proj + every[lane].astype(jnp.float32)
     summed = residual.astype(jnp.float32) + proj
     hidden = summed.astype(jnp.bfloat16)
     inverse = lax.rsqrt(jnp.mean(summed * summed, axis=-1, keepdims=True) + NORM_EPS)

time: 118 us -> 117 us (level)
  starting transfers between devices: 43.8 us -> 32.9 us
  Pallas kernels: 2.56 us -> 10.1 us
    all_to_all x0 -> x1, waiting for transfers between devices: none -> 40.3 us  [body(): lax.all_to_all(jnp.broadcast_to(sent[None], (lanes,) + sent.shape), 'tp',...]
    ppermute x3 -> x0, waiting for transfers between devices: 39.7 us -> none  [body(): proj = proj + lax.ppermute(sent, 'tp', pairs).astype(jnp.float32)]
    ppermute x3 -> x0, starting transfers between devices: 11.6 us -> none  [body(): proj = proj + lax.ppermute(sent, 'tp', pairs).astype(jnp.float32)]
    all_to_all x0 -> x1, starting transfers between devices: none -> 8.47 us  [body(): lax.all_to_all(jnp.broadcast_to(sent[None], (lanes,) + sent.shape), 'tp',...]
    all_to_all x1, starting transfers between devices: 24.6 us -> 16.8 us  [body(): lax.all_to_all(packed.reshape(places, capacity, packed.shape[1]), 'req',...]
    pallas_call x1, Pallas kernels: 2.56 us -> 10.1 us  [prefix_attend_sorted(): pl.pallas_call(sorted_prefix_kernel, grid_spec=pltpu.PrefetchScalarGridSp...]
    broadcast_in_dim x0 -> x1, local copies, waits for them, and re-layouts: none -> 1.33 us  [body(): jnp.broadcast_to(sent[None], (lanes,) + sent.shape)]
  transfers between devices with their start and end apart: 5 -> 3, of which waited for: 4 -> 2; matrix products, arithmetic and copies ran while one was open for 10% -> 9% of each run, Pallas kernels for 0% -> 0%
where the time goes in v11:
time: 117 us
  waiting for transfers between devices  46.9 us (40%)
  starting transfers between devices  32.9 us (28%)
  local copies, waits for them, and re-layouts  13.6 us (12%)
  Pallas kernels  10.1 us (9%)
  other arithmetic  6.52 us (6%)
  matrix products  5.55 us (5%)
    all_to_all x1, waiting for transfers between devices, body(): lax.all_to_all(jnp.broadcast_to(sent[None], (lanes,) + sent.shape), 'tp',...  40.3 us
    all_to_all x1, starting transfers between devices, body(): lax.all_to_all(packed.reshape(places, capacity, packed.shape[1]), 'req',...  16.8 us
    pallas_call x1, Pallas kernels, prefix_attend_sorted(): pl.pallas_call(sorted_prefix_kernel, grid_spec=pltpu.PrefetchScalarGridSp...  10.1 us
    all_to_all x1, starting transfers between devices, body(): lax.all_to_all(jnp.broadcast_to(sent[None], (lanes,) + sent.shape), 'tp',...  8.47 us
    all_to_all x1, starting transfers between devices, body(): lax.all_to_all(send_query.reshape(places, capacity, heads_dev * HD), 'req...  7.62 us
    all_to_all x1, waiting for transfers between devices, body(): lax.all_to_all(packed.reshape(places, capacity, packed.shape[1]), 'req',...  6.65 us
    dot_general x1, matrix products, body(): jnp.dot(attended, o_weight, preferred_element_type=jnp.float32)  2.85 us
  transfers between devices with their start and end apart: 3, of which 2 were waited for; matrix products, arithmetic and copies ran while one was open for 9% of the time, Pallas kernels for 0%

profile of v11, /device:TPU:2, one launch (start us, length us, event | category | flops | bytes accessed | tf_op | source)
XLA Modules:
  0.0 116.6 jit_solution(980627122600953043)
XLA Ops:
  0.7 0.8 and_select_fusion
  1.5 0.2 convert_reduce_fusion.1
  1.7 0.8 compare_select_fusion
  2.5 0.9 convolution_convert_fusion
  3.3 0.7 reshape.292
  4.0 7.6 %all-to-all-start = ((bf16[32,2,512]{2,1,0:T(2,128)(2,1)}), bf16[32,2,512]{2,1,0:T(2,128)(2,1)S(1)}, u32[]{:S(2)}, u32[]{:S(2)}) async-start(bf16[32,2,512]{2,1,0:T(2,128)(2,1)} %reshape.292), calls=%async_computation | async-start | bytes 131072 | tf_op jit(solution)/shard_map/all_to_all | solution.py:395
  11.6 0.7 fusion.26
  12.3 0.1 eq.106
  12.5 0.8 broadcast_in_dim.137
  13.3 0.2 reduce_window_sum.18
  13.6 0.8 broadcast_in_dim.144
  14.6 0.1 copy.20
  14.7 0.1 sub.87
  14.8 0.2 convert_reduce_fusion
  14.9 0.9 select_reduce_fusion.4
  15.8 0.7 and_select_fusion.2
  16.5 0.1 select_reduce_fusion
  16.6 0.8 gather_fusion
  17.5 0.8 dynamic_slice.7
  18.2 0.7 reshape.300
  19.0 0.1 copy.22
  19.1 0.1 reshape.291
  19.2 0.8 gather_fusion.1
  20.1 0.1 select_reduce_fusion.3
  20.3 0.2 reduce-window.9
  20.7 0.1 reshape_reshape.8.group_ref
  20.9 0.8 fusion.23
  21.7 0.6 fusion.34
  22.5 0.7 gather_fusion.2
  23.3 1.9 %copy-done.1 = bf16[2,6144,128]{2,1,0:T(8,128)(2,1)S(1)} copy-done((bf16[2,6144,128]{2,1,0:T(8,128)(2,1)S(1)}, bf16[2,6144,128]{2,1,0:T(8,128)(2,1)}, u32[]{:S(2)}) %copy-start.1) | copy-done | bytes 3145752
  25.1 10.1 %shard_map.140 = (f32[256,128]{1,0:T(8,128)S(1)}, f32[256,1]{1,0:T(8,128)S(1)}) custom-call(s32[16]{0:T(128)S(1)} %concatenate.6.meta_ref, bf16[256,128]{1,0:T(8,128)(2,1)S(1)} %reshape.294.query_ref, bf16[2,6144,128]{2,1,0:T(8,128)(2,1)S(1)} %copy-done.1, bf16[2,6144,128]{2,1,0:T(8,128)(2,1)} %value_ref.1, s32[256,1]{1,0:T(8,128)S(1)} %reshape_reshape.8.group_ref, ...), custom_call_target="tpu_custom_call" | custom-call | flops 402653184 | bytes 6488064 | tf_op jit(solution)/shard_map/pallas_call | solution.py:300
  35.3 0.1 reduce.4
  35.4 0.1 reshape.296
  35.6 0.7 gather_fusion.3
  36.2 0.6 gather_fusion.4
  36.8 0.8 reshape.297
  37.6 16.8 %all-to-all-start.1 = ((f32[32,2,516]{2,1,0:T(2,128)}), f32[32,2,516]{2,1,0:T(2,128)S(1)}, u32[]{:S(2)}, u32[]{:S(2)}) async-start(f32[32,2,516]{2,1,0:T(2,128)} %reshape.297), calls=%async_computation.1 | async-start | bytes 327680 | tf_op jit(solution)/shard_map/all_to_all | solution.py:402
  54.4 0.2 fusion.8
  54.6 6.6 %all-to-all-done.1 = f32[32,2,516]{2,1,0:T(2,128)S(1)} async-done(((f32[32,2,516]{2,1,0:T(2,128)}), f32[32,2,516]{2,1,0:T(2,128)S(1)}, u32[]{:S(2)}, u32[]{:S(2)}) %all-to-all-start.1) | async-done | bytes 132128 | tf_op jit(solution)/shard_map/all_to_all | solution.py:402
  61.3 0.1 reshape.298
  61.4 0.6 gather_fusion.5
  62.1 0.4 fusion.4
  62.5 2.9 %fusion.10 = bf16[24,4096]{1,0:T(8,128)(2,1)S(1)} fusion(bf16[512,4096]{1,0:T(8,128)(2,1)} %param.23, bf16[3,8,4,128]{3,2,1,0:T(4,128)(2,1)S(1)} %bitcast.35), kind=kOutput, calls=%fused_computation.28 | convolution fusion | flops 100663296 | bytes 4415488 | tf_op jit(solution)/shard_map/dot_general | solution.py:452
  65.4 1.3 %broadcast_in_dim.156 = bf16[8,24,4096]{2,1,0:T(8,128)(2,1)} broadcast(bf16[24,4096]{1,0:T(8,128)(2,1)S(1)} %fusion.10), dimensions={1,2} | broadcast | bytes 1769472 | tf_op jit(solution)/shard_map/broadcast_in_dim | solution.py:456
  66.7 8.5 %all-to-all-start.2 = ((bf16[8,24,4096]{2,1,0:T(8,128)(2,1)}), bf16[8,24,4096]{2,1,0:T(8,128)(2,1)S(1)}, u32[]{:S(2)}, u32[]{:S(2)}) async-start(bf16[8,24,4096]{2,1,0:T(8,128)(2,1)} %broadcast_in_dim.156), calls=%async_computation.2 | async-start | bytes 3145728 | tf_op jit(solution)/shard_map/all_to_all | solution.py:455
  75.2 40.3 %all-to-all-done.2 = bf16[8,24,4096]{2,1,0:T(8,128)(2,1)S(1)} async-done(((bf16[8,24,4096]{2,1,0:T(8,128)(2,1)}), bf16[8,24,4096]{2,1,0:T(8,128)(2,1)S(1)}, u32[]{:S(2)}, u32[]{:S(2)}) %all-to-all-start.2) | async-done | bytes 1572896 | tf_op jit(solution)/shard_map/all_to_all | solution.py:455
  115.5 0.4 multiply_reduce_fusion
  115.8 0.8 multiply_convert_fusion
  (53 shorter events, 1.4 us)
Async XLA Ops:
  0.6 21.1 %copy-start = (bf16[24,128,128]{2,1,0:T(8,128)(2,1)S(1)}, bf16[24,128,128]{2,1,0:T(8,128)(2,1)}, u32[]{:S(2)}) copy-start(bf16[24,128,128]{2,1,0:T(8,128)(2,1)} %param.18) | copy-start | bytes 2359300
  0.6 21.7 %copy-start.5 = (s32[2]{0:T(128)S(1)}, s32[2]{0:T(128)}, u32[]{:S(2)}) copy-start(s32[2]{0:T(128)} %param.21) | copy-start | bytes 28
  4.0 18.4 %all-to-all-start = ((bf16[32,2,512]{2,1,0:T(2,128)(2,1)}), bf16[32,2,512]{2,1,0:T(2,128)(2,1)S(1)}, u32[]{:S(2)}, u32[]{:S(2)}) async-start(bf16[32,2,512]{2,1,0:T(2,128)(2,1)} %reshape.292), calls=%async_computation | async-start | bytes 131072 | tf_op jit(solution)/shard_map/all_to_all | solution.py:395
  23.2 1.9 %copy-start.1 = (bf16[2,6144,128]{2,1,0:T(8,128)(2,1)S(1)}, bf16[2,6144,128]{2,1,0:T(8,128)(2,1)}, u32[]{:S(2)}) copy-start(bf16[2,6144,128]{2,1,0:T(8,128)(2,1)} %key_ref.1) | copy-start | bytes 9437188
  25.1 29.3 %copy-start.4 = (bf16[24,128]{1,0:T(8,128)(2,1)S(1)}, bf16[24,128]{1,0:T(8,128)(2,1)}, u32[]{:S(2)}) copy-start(bf16[24,128]{1,0:T(8,128)(2,1)} %param.15) | copy-start | bytes 18436
  35.3 26.8 %copy-start.6 = (bf16[24,128,128]{2,1,0:T(8,128)(2,1)S(1)}, bf16[24,128,128]{2,1,0:T(8,128)(2,1)}, u32[]{:S(2)}) copy-start(bf16[24,128,128]{2,1,0:T(8,128)(2,1)} %param.19) | copy-start | bytes 2359300
  37.6 23.7 %all-to-all-start.1 = ((f32[32,2,516]{2,1,0:T(2,128)}), f32[32,2,516]{2,1,0:T(2,128)S(1)}, u32[]{:S(2)}, u32[]{:S(2)}) async-start(f32[32,2,516]{2,1,0:T(2,128)} %reshape.297), calls=%async_computation.1 | async-start | bytes 327680 | tf_op jit(solution)/shard_map/all_to_all | solution.py:402
  65.4 9.8 %copy-start.3 = (bf16[4096]{0:T(1024)(128)(2,1)S(1)}, bf16[4096]{0:T(1024)(128)(2,1)}, u32[]{:S(2)}) copy-start(bf16[4096]{0:T(1024)(128)(2,1)} %param.25) | copy-start | bytes 24580
  65.4 50.1 %copy-start.2 = (bf16[24,4096]{1,0:T(8,128)(2,1)S(1)}, bf16[24,4096]{1,0:T(8,128)(2,1)}, u32[]{:S(2)}) copy-start(bf16[24,4096]{1,0:T(8,128)(2,1)} %param.24) | copy-start | bytes 589828
  66.7 48.8 %all-to-all-start.2 = ((bf16[8,24,4096]{2,1,0:T(8,128)(2,1)}), bf16[8,24,4096]{2,1,0:T(8,128)(2,1)S(1)}, u32[]{:S(2)}, u32[]{:S(2)}) async-start(bf16[8,24,4096]{2,1,0:T(8,128)(2,1)} %broadcast_in_dim.156), calls=%async_computation.2 | async-start | bytes 3145728 | tf_op jit(solution)/shard_map/all_to_all | solution.py:455

commit v12 on v8

--- a/solution.py
+++ b/solution.py
@@ -186,7 +186,7 @@
 
 
 TILE_SLOTS = 16
-KEY_BLOCK = 1024
+KEY_BLOCK = 2048
 SINK_BLOCK = 128
 
 

time: 104 us -> 98.1 us (0.943); the launches traced: 102 us -> 98.4 us
  starting transfers between devices: 33.6 us -> 24.9 us
  Pallas kernels: 2.56 us -> 7.47 us
    all_to_all x1, starting transfers between devices: 22.6 us -> 13.8 us  [body(): lax.all_to_all(packed.reshape(places, capacity, packed.shape[1]), 'req',...]
    pallas_call x1, Pallas kernels: 2.56 us -> 7.47 us  [prefix_attend_sorted(): pl.pallas_call(sorted_prefix_kernel, grid_spec=pltpu.PrefetchScalarGridSp...]
  transfers between devices with their start and end apart: 3 -> 3, of which waited for: 2 -> 2; matrix products, arithmetic and copies ran while one was open for 11% -> 12% of each run, Pallas kernels for 0% -> 0%
where the time goes in v12:
time: 98.1 us; the launch traced here: 98.4 us
  starting transfers between devices  24.9 us (25%)
  waiting for transfers between devices  20.2 us (21%)
  blocking collectives  19.1 us (19%)
  local copies, waits for them, and re-layouts  13.9 us (14%)
  Pallas kernels  7.47 us (8%)
  other arithmetic  6.4 us (7%)
  matrix products  5.54 us (6%)
  between operations  1.02 us (1%)
    all_to_all x1, blocking collectives, body(): lax.all_to_all(lax.optimization_barrier(partial_value).astype(jnp.bfloat1...  19.1 us
    all_to_all x1, starting transfers between devices, body(): lax.all_to_all(packed.reshape(places, capacity, packed.shape[1]), 'req',...  13.8 us
    all_to_all x1, waiting for transfers between devices, body(): gathered = lax.all_to_all(spread, 'tp', 1, 1, tiled=True)  13.6 us
    all_to_all x1, starting transfers between devices, body(): lax.all_to_all(send_query.reshape(places, capacity, heads_dev * HD), 'req...  7.62 us
    pallas_call x1, Pallas kernels, prefix_attend_sorted(): pl.pallas_call(sorted_prefix_kernel, grid_spec=pltpu.PrefetchScalarGridSp...  7.47 us
    all_to_all x1, waiting for transfers between devices, body(): lax.all_to_all(packed.reshape(places, capacity, packed.shape[1]), 'req',...  6.65 us
    all_to_all x1, starting transfers between devices, body(): gathered = lax.all_to_all(spread, 'tp', 1, 1, tiled=True)  3.45 us
    dot_general x1, matrix products, body(): jnp.dot(attended, o_weight, preferred_element_type=jnp.float32)  2.86 us
  transfers between devices with their start and end apart: 3, of which 2 were waited for; matrix products, arithmetic and copies ran while one was open for 12% of the time, Pallas kernels for 0%

profile of v12, /device:TPU:2, one launch (start us, length us, event | category | flops | bytes accessed | tf_op | source)
XLA Modules:
  0.0 98.4 jit_solution(16660455578773203419)
XLA Ops:
  0.7 0.8 and_select_fusion
  1.5 0.2 convert_reduce_fusion.2
  1.7 0.8 compare_select_fusion
  2.4 0.9 convolution_convert_fusion
  3.3 0.7 reshape.295
  4.0 7.6 %all-to-all-start = ((bf16[32,2,512]{2,1,0:T(2,128)(2,1)}), bf16[32,2,512]{2,1,0:T(2,128)(2,1)S(1)}, u32[]{:S(2)}, u32[]{:S(2)}) async-start(bf16[32,2,512]{2,1,0:T(2,128)(2,1)} %reshape.295), calls=%async_computation | async-start | bytes 131072 | tf_op jit(solution)/shard_map/all_to_all | solution.py:411
  11.6 0.7 fusion.27
  12.3 0.1 eq.106
  12.5 0.8 broadcast_in_dim.137
  13.3 0.2 reduce_window_sum.18
  13.6 0.8 broadcast_in_dim.144
  14.6 0.1 sub.87
  14.8 0.2 convert_reduce_fusion.1
  14.9 0.9 select_reduce_fusion.4
  15.9 0.1 reshape.294
  16.0 0.1 select_reduce_fusion
  16.1 0.8 gather_fusion
  16.9 0.8 gather_fusion.1
  17.9 0.1 select_reduce_fusion.3
  18.0 0.7 and_select_fusion.1
  18.7 0.8 dynamic_slice.7
  19.5 0.7 reshape.303
  20.4 0.2 reduce-window.9
  20.8 0.1 reshape_reshape.8.group_ref
  21.0 0.8 fusion.24
  21.8 0.6 fusion.35
  22.4 0.7 concatenate.6.meta_ref
  23.2 0.7 gather_fusion.2
  24.0 1.9 %copy-done.1 = bf16[2,6144,128]{2,1,0:T(8,128)(2,1)S(1)} copy-done((bf16[2,6144,128]{2,1,0:T(8,128)(2,1)S(1)}, bf16[2,6144,128]{2,1,0:T(8,128)(2,1)}, u32[]{:S(2)}) %copy-start.1) | copy-done | bytes 3145752
  25.9 7.5 %shard_map.140 = (f32[256,128]{1,0:T(8,128)S(1)}, f32[256,1]{1,0:T(8,128)S(1)}) custom-call(s32[16]{0:T(128)S(1)} %concatenate.6.meta_ref, bf16[256,128]{1,0:T(8,128)(2,1)S(1)} %reshape.297.query_ref, bf16[2,6144,128]{2,1,0:T(8,128)(2,1)S(1)} %copy-done.1, bf16[2,6144,128]{2,1,0:T(8,128)(2,1)} %value_ref.1, s32[256,1]{1,0:T(8,128)S(1)} %reshape_reshape.8.group_ref, ...), custom_call_target="tpu_custom_call" | custom-call | flops 402653184 | bytes 6488064 | tf_op jit(solution)/shard_map/pallas_call | solution.py:316
  33.4 0.1 reduce.4
  33.5 0.1 reshape.299
  33.6 0.7 gather_fusion.3
  34.3 0.6 gather_fusion.4
  34.9 0.8 reshape.300
  35.7 13.8 %all-to-all-start.1 = ((f32[32,2,516]{2,1,0:T(2,128)}), f32[32,2,516]{2,1,0:T(2,128)S(1)}, u32[]{:S(2)}, u32[]{:S(2)}) async-start(f32[32,2,516]{2,1,0:T(2,128)} %reshape.300), calls=%async_computation.1 | async-start | bytes 327680 | tf_op jit(solution)/shard_map/all_to_all | solution.py:418
  49.5 0.2 fusion.9
  49.7 6.6 %all-to-all-done.1 = f32[32,2,516]{2,1,0:T(2,128)S(1)} async-done(((f32[32,2,516]{2,1,0:T(2,128)}), f32[32,2,516]{2,1,0:T(2,128)S(1)}, u32[]{:S(2)}, u32[]{:S(2)}) %all-to-all-start.1) | async-done | bytes 132128 | tf_op jit(solution)/shard_map/all_to_all | solution.py:418
  56.4 0.1 reshape.301
  56.5 0.6 gather_fusion.5
  57.2 0.4 fusion.4
  57.6 2.9 %fusion.11 = bf16[24,4096]{1,0:T(8,128)(2,1)S(1)} fusion(bf16[512,4096]{1,0:T(8,128)(2,1)} %param.23, bf16[3,8,4,128]{3,2,1,0:T(4,128)(2,1)S(1)} %bitcast.43), kind=kOutput, calls=%fused_computation.31 | convolution fusion | flops 100663296 | bytes 4415488 | tf_op jit(solution)/shard_map/dot_general | solution.py:468
  60.5 19.1 %all_to_all.20 = bf16[24,8,512]{2,0,1:T(8,128)(2,1)S(1)} all-to-all(bf16[24,8,512]{2,0,1:T(8,128)(2,1)S(1)} %bitcast.40), channel_id=1, replica_groups=mesh['req'=32,'tp'=8] {'tp'}, dimensions={1} | all-to-all | bytes 393216 | tf_op jit(solution)/shard_map/all_to_all | solution.py:471
  79.6 0.8 broadcast_in_dim.156
  80.4 3.5 %all-to-all-start.3 = ((f32[24,8,512]{2,0,1:T(8,128)}), f32[24,8,512]{2,0,1:T(8,128)S(1)}, u32[]{:S(2)}, u32[]{:S(2)}) async-start(f32[24,8,512]{2,0,1:T(8,128)} %broadcast_in_dim.156), calls=%async_computation.3 | async-start | bytes 786432 | tf_op jit(solution)/shard_map/all_to_all | solution.py:477
  83.8 13.6 %all-to-all-done.3 = f32[24,8,512]{2,0,1:T(8,128)S(1)} async-done(((f32[24,8,512]{2,0,1:T(8,128)}), f32[24,8,512]{2,0,1:T(8,128)S(1)}, u32[]{:S(2)}, u32[]{:S(2)}) %all-to-all-start.3) | async-done | bytes 393248 | tf_op jit(solution)/shard_map/all_to_all | solution.py:477
  97.4 0.2 multiply_reduce_fusion
  97.6 0.8 multiply_convert_fusion
  (58 shorter events, 1.6 us)
Async XLA Ops:
  0.6 21.2 %copy-start = (bf16[24,128,128]{2,1,0:T(8,128)(2,1)S(1)}, bf16[24,128,128]{2,1,0:T(8,128)(2,1)}, u32[]{:S(2)}) copy-start(bf16[24,128,128]{2,1,0:T(8,128)(2,1)} %param.18) | copy-start | bytes 2359300
  4.0 19.2 %all-to-all-start = ((bf16[32,2,512]{2,1,0:T(2,128)(2,1)}), bf16[32,2,512]{2,1,0:T(2,128)(2,1)S(1)}, u32[]{:S(2)}, u32[]{:S(2)}) async-start(bf16[32,2,512]{2,1,0:T(2,128)(2,1)} %reshape.295), calls=%async_computation | async-start | bytes 131072 | tf_op jit(solution)/shard_map/all_to_all | solution.py:411
  24.0 1.9 %copy-start.1 = (bf16[2,6144,128]{2,1,0:T(8,128)(2,1)S(1)}, bf16[2,6144,128]{2,1,0:T(8,128)(2,1)}, u32[]{:S(2)}) copy-start(bf16[2,6144,128]{2,1,0:T(8,128)(2,1)} %key_ref.1) | copy-start | bytes 9437188
  25.9 23.6 %copy-start.4 = (bf16[24,128]{1,0:T(8,128)(2,1)S(1)}, bf16[24,128]{1,0:T(8,128)(2,1)}, u32[]{:S(2)}) copy-start(bf16[24,128]{1,0:T(8,128)(2,1)} %param.15) | copy-start | bytes 18436
  25.9 31.3 %copy-start.5 = (bf16[24,128,128]{2,1,0:T(8,128)(2,1)S(1)}, bf16[24,128,128]{2,1,0:T(8,128)(2,1)}, u32[]{:S(2)}) copy-start(bf16[24,128,128]{2,1,0:T(8,128)(2,1)} %param.19) | copy-start | bytes 2359300
  35.7 20.7 %all-to-all-start.1 = ((f32[32,2,516]{2,1,0:T(2,128)}), f32[32,2,516]{2,1,0:T(2,128)S(1)}, u32[]{:S(2)}, u32[]{:S(2)}) async-start(f32[32,2,516]{2,1,0:T(2,128)} %reshape.300), calls=%async_computation.1 | async-start | bytes 327680 | tf_op jit(solution)/shard_map/all_to_all | solution.py:418
  57.1 26.7 %copy-start.3 = (bf16[4096]{0:T(1024)(128)(2,1)S(1)}, bf16[4096]{0:T(1024)(128)(2,1)}, u32[]{:S(2)}) copy-start(bf16[4096]{0:T(1024)(128)(2,1)} %param.25) | copy-start | bytes 24580
  57.2 40.2 %copy-start.2 = (bf16[24,4096]{1,0:T(8,128)(2,1)S(1)}, bf16[24,4096]{1,0:T(8,128)(2,1)}, u32[]{:S(2)}) copy-start(bf16[24,4096]{1,0:T(8,128)(2,1)} %param.24) | copy-start | bytes 589828
  80.4 17.0 %all-to-all-start.3 = ((f32[24,8,512]{2,0,1:T(8,128)}), f32[24,8,512]{2,0,1:T(8,128)S(1)}, u32[]{:S(2)}, u32[]{:S(2)}) async-start(f32[24,8,512]{2,0,1:T(8,128)} %broadcast_in_dim.156), calls=%async_computation.3 | async-start | bytes 786432 | tf_op jit(solution)/shard_map/all_to_all | solution.py:477

commit v13 on v12

--- a/solution.py
+++ b/solution.py
@@ -185,7 +185,7 @@
     return out.reshape(row_count, heads_dev * HD), log.reshape(row_count, heads_dev)
 
 
-TILE_SLOTS = 16
+TILE_SLOTS = 8
 KEY_BLOCK = 2048
 SINK_BLOCK = 128
 

time: 98.1 us -> 106 us (1.081); the launches traced: 98.4 us -> 104 us
  starting transfers between devices: 24.9 us -> 35.4 us
  Pallas kernels: 7.47 us -> 2.56 us
    all_to_all x1, starting transfers between devices: 13.8 us -> 24.3 us  [body(): lax.all_to_all(packed.reshape(places, capacity, packed.shape[1]), 'req',...]
    pallas_call x1, Pallas kernels: 7.47 us -> 2.56 us  [prefix_attend_sorted(): pl.pallas_call(sorted_prefix_kernel, grid_spec=pltpu.PrefetchScalarGridSp...]
  transfers between devices with their start and end apart: 3 -> 3, of which waited for: 2 -> 2; matrix products, arithmetic and copies ran while one was open for 12% -> 11% of each run, Pallas kernels for 0% -> 0%
where the time goes in v13:
time: 106 us; the launch traced here: 104 us
  starting transfers between devices  35.4 us (33%)
  waiting for transfers between devices  20.2 us (19%)
  blocking collectives  19 us (18%)
  local copies, waits for them, and re-layouts  13.8 us (13%)
  other arithmetic  6.41 us (6%)
  matrix products  5.54 us (5%)
  Pallas kernels  2.56 us (2%)
    all_to_all x1, starting transfers between devices, body(): lax.all_to_all(packed.reshape(places, capacity, packed.shape[1]), 'req',...  24.3 us
    all_to_all x1, blocking collectives, body(): lax.all_to_all(lax.optimization_barrier(partial_value).astype(jnp.bfloat1...  19 us
    all_to_all x1, waiting for transfers between devices, body(): gathered = lax.all_to_all(spread, 'tp', 1, 1, tiled=True)  13.6 us
    all_to_all x1, starting transfers between devices, body(): lax.all_to_all(send_query.reshape(places, capacity, heads_dev * HD), 'req...  7.62 us
    all_to_all x1, waiting for transfers between devices, body(): lax.all_to_all(packed.reshape(places, capacity, packed.shape[1]), 'req',...  6.65 us
    all_to_all x1, starting transfers between devices, body(): gathered = lax.all_to_all(spread, 'tp', 1, 1, tiled=True)  3.45 us
    dot_general x1, matrix products, body(): jnp.dot(attended, o_weight, preferred_element_type=jnp.float32)  2.86 us
    pallas_call x1, Pallas kernels, prefix_attend_sorted(): pl.pallas_call(sorted_prefix_kernel, grid_spec=pltpu.PrefetchScalarGridSp...  2.56 us
  transfers between devices with their start and end apart: 3, of which 2 were waited for; matrix products, arithmetic and copies ran while one was open for 11% of the time, Pallas kernels for 0%

profile of v13, /device:TPU:2, one launch (start us, length us, event | category | flops | bytes accessed | tf_op | source)
XLA Modules:
  0.0 104.0 jit_solution(8784418506627506759)
XLA Ops:
  0.7 0.8 and_select_fusion
  1.5 0.2 convert_reduce_fusion.2
  1.7 0.8 compare_select_fusion
  2.4 0.9 convolution_convert_fusion
  3.3 0.7 reshape.295
  4.0 7.6 %all-to-all-start = ((bf16[32,2,512]{2,1,0:T(2,128)(2,1)}), bf16[32,2,512]{2,1,0:T(2,128)(2,1)S(1)}, u32[]{:S(2)}, u32[]{:S(2)}) async-start(bf16[32,2,512]{2,1,0:T(2,128)(2,1)} %reshape.295), calls=%async_computation | async-start | bytes 131072 | tf_op jit(solution)/shard_map/all_to_all | solution.py:411
  11.6 0.7 fusion.27
  12.3 0.1 eq.106
  12.5 0.8 broadcast_in_dim.137
  13.3 0.2 reduce_window_sum.18
  13.6 0.8 broadcast_in_dim.144
  14.6 0.1 sub.87
  14.8 0.2 convert_reduce_fusion.1
  14.9 0.9 select_reduce_fusion.4
  15.9 0.1 reshape.294
  16.0 0.1 select_reduce_fusion
  16.1 0.8 gather_fusion
  16.9 0.8 gather_fusion.1
  17.8 0.1 select_reduce_fusion.3
  18.0 0.7 and_select_fusion.1
  18.7 0.8 dynamic_slice.7
  19.4 0.7 reshape.303
  20.4 0.2 reduce-window.9
  20.8 0.1 reshape_reshape.8.group_ref
  21.0 0.8 fusion.24
  21.8 0.6 fusion.35
  22.4 0.7 concatenate.6.meta_ref
  23.2 0.7 gather_fusion.2
  24.0 1.9 %copy-done.1 = bf16[2,6144,128]{2,1,0:T(8,128)(2,1)S(1)} copy-done((bf16[2,6144,128]{2,1,0:T(8,128)(2,1)S(1)}, bf16[2,6144,128]{2,1,0:T(8,128)(2,1)}, u32[]{:S(2)}) %copy-start.1) | copy-done | bytes 3145752
  25.9 2.6 %shard_map.140 = (f32[256,128]{1,0:T(8,128)S(1)}, f32[256,1]{1,0:T(8,128)S(1)}) custom-call(s32[24]{0:T(128)S(1)} %concatenate.6.meta_ref, bf16[256,128]{1,0:T(8,128)(2,1)S(1)} %reshape.297.query_ref, bf16[2,6144,128]{2,1,0:T(8,128)(2,1)S(1)} %copy-done.1, bf16[2,6144,128]{2,1,0:T(8,128)(2,1)} %value_ref.1, s32[256,1]{1,0:T(8,128)S(1)} %reshape_reshape.8.group_ref, ...), custom_call_target="tpu_custom_call" | custom-call | flops 402653184 | bytes 6488064 | tf_op jit(solution)/shard_map/pallas_call | solution.py:316
  28.5 0.1 reduce.4
  28.6 0.1 reshape.299
  28.7 0.7 gather_fusion.3
  29.4 0.6 gather_fusion.4
  30.0 0.8 reshape.300
  30.8 24.3 %all-to-all-start.1 = ((f32[32,2,516]{2,1,0:T(2,128)}), f32[32,2,516]{2,1,0:T(2,128)S(1)}, u32[]{:S(2)}, u32[]{:S(2)}) async-start(f32[32,2,516]{2,1,0:T(2,128)} %reshape.300), calls=%async_computation.1 | async-start | bytes 327680 | tf_op jit(solution)/shard_map/all_to_all | solution.py:418
  55.1 0.2 fusion.9
  55.3 6.6 %all-to-all-done.1 = f32[32,2,516]{2,1,0:T(2,128)S(1)} async-done(((f32[32,2,516]{2,1,0:T(2,128)}), f32[32,2,516]{2,1,0:T(2,128)S(1)}, u32[]{:S(2)}, u32[]{:S(2)}) %all-to-all-start.1) | async-done | bytes 132128 | tf_op jit(solution)/shard_map/all_to_all | solution.py:418
  61.9 0.1 reshape.301
  62.0 0.6 gather_fusion.5
  62.8 0.4 fusion.4
  63.2 2.9 %fusion.11 = bf16[24,4096]{1,0:T(8,128)(2,1)S(1)} fusion(bf16[512,4096]{1,0:T(8,128)(2,1)} %param.23, bf16[3,8,4,128]{3,2,1,0:T(4,128)(2,1)S(1)} %bitcast.43), kind=kOutput, calls=%fused_computation.31 | convolution fusion | flops 100663296 | bytes 4415488 | tf_op jit(solution)/shard_map/dot_general | solution.py:468
  66.1 19.0 %all_to_all.20 = bf16[24,8,512]{2,0,1:T(8,128)(2,1)S(1)} all-to-all(bf16[24,8,512]{2,0,1:T(8,128)(2,1)S(1)} %bitcast.40), channel_id=1, replica_groups=mesh['req'=32,'tp'=8] {'tp'}, dimensions={1} | all-to-all | bytes 393216 | tf_op jit(solution)/shard_map/all_to_all | solution.py:471
  85.1 0.8 broadcast_in_dim.156
  85.9 3.5 %all-to-all-start.3 = ((f32[24,8,512]{2,0,1:T(8,128)}), f32[24,8,512]{2,0,1:T(8,128)S(1)}, u32[]{:S(2)}, u32[]{:S(2)}) async-start(f32[24,8,512]{2,0,1:T(8,128)} %broadcast_in_dim.156), calls=%async_computation.3 | async-start | bytes 786432 | tf_op jit(solution)/shard_map/all_to_all | solution.py:477
  89.4 13.6 %all-to-all-done.3 = f32[24,8,512]{2,0,1:T(8,128)S(1)} async-done(((f32[24,8,512]{2,0,1:T(8,128)}), f32[24,8,512]{2,0,1:T(8,128)S(1)}, u32[]{:S(2)}, u32[]{:S(2)}) %all-to-all-start.3) | async-done | bytes 393248 | tf_op jit(solution)/shard_map/all_to_all | solution.py:477
  103.0 0.2 multiply_reduce_fusion
  103.2 0.8 multiply_convert_fusion
  (58 shorter events, 1.6 us)
Async XLA Ops:
  0.6 21.2 %copy-start = (bf16[24,128,128]{2,1,0:T(8,128)(2,1)S(1)}, bf16[24,128,128]{2,1,0:T(8,128)(2,1)}, u32[]{:S(2)}) copy-start(bf16[24,128,128]{2,1,0:T(8,128)(2,1)} %param.18) | copy-start | bytes 2359300
  4.0 19.2 %all-to-all-start = ((bf16[32,2,512]{2,1,0:T(2,128)(2,1)}), bf16[32,2,512]{2,1,0:T(2,128)(2,1)S(1)}, u32[]{:S(2)}, u32[]{:S(2)}) async-start(bf16[32,2,512]{2,1,0:T(2,128)(2,1)} %reshape.295), calls=%async_computation | async-start | bytes 131072 | tf_op jit(solution)/shard_map/all_to_all | solution.py:411
  24.0 1.9 %copy-start.1 = (bf16[2,6144,128]{2,1,0:T(8,128)(2,1)S(1)}, bf16[2,6144,128]{2,1,0:T(8,128)(2,1)}, u32[]{:S(2)}) copy-start(bf16[2,6144,128]{2,1,0:T(8,128)(2,1)} %key_ref.1) | copy-start | bytes 9437188
  25.9 29.2 %copy-start.4 = (bf16[24,128]{1,0:T(8,128)(2,1)S(1)}, bf16[24,128]{1,0:T(8,128)(2,1)}, u32[]{:S(2)}) copy-start(bf16[24,128]{1,0:T(8,128)(2,1)} %param.15) | copy-start | bytes 18436
  25.9 36.9 %copy-start.5 = (bf16[24,128,128]{2,1,0:T(8,128)(2,1)S(1)}, bf16[24,128,128]{2,1,0:T(8,128)(2,1)}, u32[]{:S(2)}) copy-start(bf16[24,128,128]{2,1,0:T(8,128)(2,1)} %param.19) | copy-start | bytes 2359300
  30.8 31.2 %all-to-all-start.1 = ((f32[32,2,516]{2,1,0:T(2,128)}), f32[32,2,516]{2,1,0:T(2,128)S(1)}, u32[]{:S(2)}, u32[]{:S(2)}) async-start(f32[32,2,516]{2,1,0:T(2,128)} %reshape.300), calls=%async_computation.1 | async-start | bytes 327680 | tf_op jit(solution)/shard_map/all_to_all | solution.py:418
  62.6 26.7 %copy-start.3 = (bf16[4096]{0:T(1024)(128)(2,1)S(1)}, bf16[4096]{0:T(1024)(128)(2,1)}, u32[]{:S(2)}) copy-start(bf16[4096]{0:T(1024)(128)(2,1)} %param.25) | copy-start | bytes 24580
  62.8 40.2 %copy-start.2 = (bf16[24,4096]{1,0:T(8,128)(2,1)S(1)}, bf16[24,4096]{1,0:T(8,128)(2,1)}, u32[]{:S(2)}) copy-start(bf16[24,4096]{1,0:T(8,128)(2,1)} %param.24) | copy-start | bytes 589828
  85.9 17.0 %all-to-all-start.3 = ((f32[24,8,512]{2,0,1:T(8,128)}), f32[24,8,512]{2,0,1:T(8,128)S(1)}, u32[]{:S(2)}, u32[]{:S(2)}) async-start(f32[24,8,512]{2,0,1:T(8,128)} %broadcast_in_dim.156), calls=%async_computation.3 | async-start | bytes 786432 | tf_op jit(solution)/shard_map/all_to_all | solution.py:477
